TPU v7x, 256 devices: a whole 4x4x8 slice. The times are simulated.
256 devices in a mesh: rep: 16 (over z, core), exp: 16 (over y, x).
Axes of the slice: x: 4, y: 4, z: 8, core: 2. Of those that a mesh axis runs over, the one named last changes fastest.
Arguments:
- tokens: bfloat16 [2048, 2048], P('exp'), may hold values from -6 to 6
- expert_ids: int32 [2048, 2], P('exp'), may hold values from 0 to 15, all different within a row; in each aligned block of 128 rows (0 to 127, 128 to 255, ...) at most 32 rows name the same one
- gate_values: float32 [2048, 2], P('exp'), may hold values from 0.2 to 1
- grad_out: bfloat16 [2048, 2048], P('exp'), may hold values from -6 to 6
- w_up: bfloat16 [16, 2048, 8192], P('exp', None, 'rep'), may hold values from -0.125 to 0.125
- w_down: bfloat16 [16, 8192, 2048], P('exp', 'rep'), may hold values from -0.0625 to 0.0625
Outputs:
- mixed: bfloat16 [2048, 2048], P('exp', 'rep')
- grad_tokens: bfloat16 [2048, 2048], P('exp', 'rep')
- grad_w_up: bfloat16 [16, 2048, 8192], P('exp', None, 'rep')
- grad_w_down: bfloat16 [16, 8192, 2048], P('exp', 'rep')
Inputs may be any that keep to these rules, and one draw needn't show every extreme that they name: `expert_ids`: each row names 2 different experts. Within the rows of one index of exp (aligned blocks of 128 rows) no expert is named by more than 32 rows, a bound that some block reaches.
All inputs are finite; a program needn't handle non-finite values.
Results may differ from a plain program's by a relative error of at most 0.022.
Values may be sent and summed in bfloat16 or wider, within the bound.
No kernel may reach another device: no remote copies, remote signals or barrier semaphores. Data moves between devices by JAX's collectives and lax.ppermute only.
A program may use at most 128 MiB of HBM per device.

v0:
```python
import jax
import jax.numpy as jnp
from jax import lax
from jax.sharding import Mesh, PartitionSpec as P


def plan_slots(routed, experts, capacity):
    flat_ids = routed.reshape(-1)
    onehot = (flat_ids[:, None] == jnp.arange(experts, dtype=jnp.int32)[None, :]).astype(jnp.int32)
    before = jnp.cumsum(onehot, axis=0) - onehot
    position = jnp.sum(before * onehot, axis=1)
    counts = jnp.sum(onehot, axis=0)
    slotting_labels = flat_ids * capacity + position
    placed = (
        slotting_labels[None, :] == jnp.arange(experts * capacity, dtype=jnp.int32)[:, None]
    ).astype(jnp.bfloat16)
    return (placed, counts)


def expert_math(rows_in, rows_grad, live_mask, up_weight, down_weight, up_perm, down_perm):
    preact = jnp.dot(rows_in, up_weight, preferred_element_type=jnp.float32)
    sigmoid_val = jax.nn.sigmoid(preact)
    keep = live_mask[:, None]
    hidden_units = jnp.where(keep, preact * sigmoid_val, 0.0).astype(jnp.bfloat16)
    out_part = jnp.dot(hidden_units, down_perm, preferred_element_type=jnp.float32)
    grad_hidden = lax.dot_general(
        rows_grad, down_weight, (((1,), (1,)), ((), ())), preferred_element_type=jnp.float32
    )
    slope = sigmoid_val * (1.0 + preact * (1.0 - sigmoid_val))
    gradient_before_activation = jnp.where(keep, grad_hidden * slope, 0.0).astype(jnp.bfloat16)
    dx_part = lax.dot_general(
        gradient_before_activation,
        up_perm,
        (((1,), (1,)), ((), ())),
        preferred_element_type=jnp.float32,
    )
    grad_down_e = lax.dot_general(
        hidden_units, rows_grad, (((0,), (0,)), ((), ())), preferred_element_type=jnp.float32
    )
    grad_up_e = lax.dot_general(
        rows_in,
        gradient_before_activation,
        (((0,), (0,)), ((), ())),
        preferred_element_type=jnp.float32,
    )
    return (out_part, dx_part, grad_up_e, grad_down_e)


def pick(stacked, index, axis):
    return lax.dynamic_index_in_dim(stacked, index, axis=axis, keepdims=False)


def reduce_over_rep(part, n_z, n_core, cols):
    slots = part.shape[0]
    halves = part.reshape(slots, n_core, n_z * cols)
    got = lax.ppermute(halves[:, 1], "core", [(j, (j + 1) % n_core) for j in range(n_core)])
    pair_sum = (halves[:, 0].astype(jnp.float32) + got.astype(jnp.float32)).astype(jnp.bfloat16)
    blocks = pair_sum.reshape(slots, n_z, cols)
    acc = blocks[:, 0].astype(jnp.float32)
    for k in range(1, n_z):
        moved = lax.ppermute(blocks[:, k], "z", [(j, (j + k) % n_z) for j in range(n_z)])
        acc = acc + moved.astype(jnp.float32)
    return acc


def dispatch_rows(placed_rows, source, n_exp, capacity, n_core):
    core = lax.axis_index("core")
    width = source.shape[1]
    share = width // n_core
    mine = lax.dynamic_slice_in_dim(source, core * share, share, 1)
    sent = jnp.dot(placed_rows, mine, preferred_element_type=jnp.float32).astype(jnp.bfloat16)
    got = lax.all_to_all(
        sent.reshape(n_exp, capacity, share), "exp", split_axis=0, concat_axis=0, tiled=True
    ).reshape(n_exp * capacity, share)
    other = lax.ppermute(got, "core", [(j, (j + 1) % n_core) for j in range(n_core)])
    pair = jnp.stack([got, other])
    return jnp.concatenate([pick(pair, core, 0), pick(pair, 1 - core, 0)], axis=1)


def local(tokens, expert_ids, gate_values, grad_out, w_up, w_down):
    n_z = lax.axis_size("z")
    n_core = lax.axis_size("core")
    n_rep = n_z * n_core
    n_exp = lax.axis_size("exp")
    tok_count, width = tokens.shape
    top_k = expert_ids.shape[1]
    pair_count = tok_count * top_k
    capacity = max(2, min(tok_count, 2 * tok_count * top_k // n_exp))
    cols = width // n_rep
    up_weight = w_up[0]
    down_weight = w_down[0]
    ff_local = up_weight.shape[1]
    zi = lax.axis_index("z")
    core = lax.axis_index("core")
    down_blocks = jnp.roll(down_weight.reshape(ff_local, n_z, n_core, cols), (-zi, -core), (1, 2))
    down_perm = down_blocks.transpose(0, 2, 1, 3).reshape(ff_local, width)
    up_blocks = jnp.roll(up_weight.reshape(n_z, n_core, cols, ff_local), (-zi, -core), (0, 1))
    up_perm = up_blocks.transpose(1, 0, 2, 3).reshape(width, ff_local)
    grad_rows = (gate_values[:, :, None] * grad_out[:, None, :].astype(jnp.float32)).astype(
        jnp.bfloat16
    )
    grad_rows = grad_rows.reshape(pair_count, width)
    placed, counts = plan_slots(expert_ids, n_exp, capacity)
    summed = placed.reshape(n_exp * capacity, tok_count, top_k).sum(axis=2)
    count_parts = jnp.stack([counts // 16, counts % 16], axis=1).astype(jnp.bfloat16)
    got_counts = lax.all_to_all(count_parts, "exp", split_axis=0, concat_axis=0, tiled=True)
    count_values = got_counts[:, 0].astype(jnp.float32) * 16.0 + got_counts[:, 1].astype(
        jnp.float32
    )
    slot_mask = jnp.arange(capacity, dtype=jnp.float32)[None, :] < count_values[:, None]
    live_mask = slot_mask.reshape(-1)
    rows_in = dispatch_rows(summed, tokens, n_exp, capacity, n_core)
    rows_grad = dispatch_rows(placed, grad_rows, n_exp, capacity, n_core)
    out_part, dx_part, grad_up_e, grad_down_e = expert_math(
        rows_in, rows_grad, live_mask, up_weight, down_weight, up_perm, down_perm
    )
    parts = jnp.stack([out_part, dx_part], axis=1).astype(jnp.bfloat16)
    both = reduce_over_rep(parts.reshape(n_exp * capacity * 2, width), n_z, n_core, cols)
    both = both.reshape(n_exp * capacity, 2 * cols).astype(jnp.bfloat16)
    back_both = lax.all_to_all(
        both.reshape(n_exp, capacity, 2 * cols), "exp", split_axis=0, concat_axis=0, tiled=True
    ).reshape(n_exp * capacity, 2 * cols)
    back_out = back_both[:, :cols]
    back_dx = back_both[:, cols:]
    pair_out = jnp.einsum(
        "st,sd->td",
        placed,
        back_out,
        preferred_element_type=jnp.float32,
    )
    pair_dx = jnp.einsum(
        "st,sd->td",
        placed,
        back_dx,
        preferred_element_type=jnp.float32,
    )
    mixed = jnp.sum(gate_values[:, :, None] * pair_out.reshape(tok_count, top_k, cols), axis=1)
    grad_tokens = jnp.sum(pair_dx.reshape(tok_count, top_k, cols), axis=1)
    return (
        mixed.astype(jnp.bfloat16),
        grad_tokens.astype(jnp.bfloat16),
        grad_up_e.astype(jnp.bfloat16)[None],
        grad_down_e.astype(jnp.bfloat16)[None],
    )


def solution(mesh):
    n_rep, n_exp = mesh.devices.shape
    n_core = 2
    mesh3 = Mesh(mesh.devices.reshape(n_rep // n_core, n_core, n_exp), ("z", "core", "exp"))
    rep = ("z", "core")
    return jax.shard_map(
        local,
        mesh=mesh3,
        in_specs=(
            P("exp", None),
            P("exp", None),
            P("exp", None),
            P("exp", None),
            P("exp", None, rep),
            P("exp", rep, None),
        ),
        out_specs=(P("exp", rep), P("exp", rep), P("exp", None, rep), P("exp", rep, None)),
        check_vma=False,
    )
```

profile of v0, /device:TPU:2, one launch (start us, length us, event | category | flops | bytes accessed | tf_op | source)
XLA Modules:
  0.0 183.8 jit_solution(5302293526202029834)
XLA Ops:
  0.7 0.8 copy.99
  1.5 0.1 reshape.211
  1.6 0.1 eq.57
  1.8 0.6 reduce-window.6
  2.4 0.2 slice_reduce_fusion
  2.6 0.1 convert_reduce_fusion
  2.8 0.1 reduce_sum.55
  3.0 0.7 multiply_add_fusion
  3.8 1.4 convolution_convert_fusion.4
  5.2 7.5 %all-to-all-start.1 = ((bf16[16,32,1024]{2,1,0:T(8,128)(2,1)}), bf16[16,32,1024]{2,1,0:T(8,128)(2,1)}, u32[]{:S(2)}, u32[]{:S(2)}) async-start(bf16[16,32,1024]{2,1,0:T(8,128)(2,1)} %bitcast.6), calls=%async_computation.1 | async-start | bytes 2097152 | tf_op jit(solution)/shard_map/all_to_all | solution.py:72
  12.7 0.1 copy.98
  12.8 0.1 mul.73
  12.9 1.0 mul.75
  14.0 2.4 %mul.76 = f32[256,2048]{1,0:T(8,128)} reshape(f32[128,2,2048]{2,1,0:T(2,128)S(1)} %mul.75) | data formatting | bytes 4194304 | tf_op jit(solution)/shard_map/mul | solution.py:99
  16.4 2.9 %convolution_convert_fusion.5 = bf16[512,1024]{1,0:T(8,128)(2,1)} fusion(f32[256,2048]{1,0:T(8,128)} %mul.76, s32[]{:T(128)S(6)} %select_n.94, f32[256]{0:T(256)S(1)} %mul.73, s32[256]{0:T(256)S(1)} %multiply_add_fusion.1), kind=kOutput, calls=%fused_computation.43 | convolution fusion | flops 269615104 | bytes 2099204 | tf_op jit(solution)/shard_map/dot_general | solution.py:71
  19.3 9.3 %all-to-all-done.1 = bf16[16,32,1024]{2,1,0:T(8,128)(2,1)} async-done(((bf16[16,32,1024]{2,1,0:T(8,128)(2,1)}), bf16[16,32,1024]{2,1,0:T(8,128)(2,1)}, u32[]{:S(2)}, u32[]{:S(2)}) %all-to-all-start.1) | async-done | bytes 1048608 | tf_op jit(solution)/shard_map/all_to_all | solution.py:72
  28.6 6.0 %all-to-all-start.2 = ((bf16[16,32,1024]{2,1,0:T(8,128)(2,1)}), bf16[16,32,1024]{2,1,0:T(8,128)(2,1)}, u32[]{:S(2)}, u32[]{:S(2)}) async-start(bf16[16,32,1024]{2,1,0:T(8,128)(2,1)} %bitcast.17), calls=%async_computation.2 | async-start | bytes 2097152 | tf_op jit(solution)/shard_map/all_to_all | solution.py:72
  34.6 0.7 copy.102
  35.3 14.0 %all-to-all-done.2 = bf16[16,32,1024]{2,1,0:T(8,128)(2,1)} async-done(((bf16[16,32,1024]{2,1,0:T(8,128)(2,1)}), bf16[16,32,1024]{2,1,0:T(8,128)(2,1)}, u32[]{:S(2)}, u32[]{:S(2)}) %all-to-all-start.2) | async-done | bytes 1048608 | tf_op jit(solution)/shard_map/all_to_all | solution.py:72
  49.4 4.7 %all-to-all-start = ((bf16[16,1,2]{2,1,0:T(2,128)(2,1)}), bf16[16,1,2]{2,1,0:T(2,128)(2,1)S(1)}, u32[]{:S(2)}, u32[]{:S(2)}) async-start(bf16[16,1,2]{2,1,0:T(2,128)(2,1)} %copy.102), calls=%async_computation | async-start | bytes 16384 | tf_op jit(solution)/shard_map/all_to_all | solution.py:106
  54.1 0.8 fusion.8
  54.9 0.8 fusion.7
  55.6 1.5 copy.108
  57.2 2.9 %copy.105 = bf16[1,512,2048]{1,2,0:T(8,128)(2,1)S(1)} copy(bf16[1,512,2048]{2,1,0:T(8,128)(2,1)} %param.11) | data formatting | bytes 4194304 | tf_op args[5]
  60.0 0.8 fusion.11
  60.8 0.8 fusion.10
  61.6 0.2 copy.106
  61.8 0.1 copy.103
  62.1 3.4 %fusion.28 = (bf16[512,1024]{1,0:T(8,128)(2,1)S(1)}, bf16[512,1024]{1,0:T(8,128)(2,1)S(1)}, bf16[512,1024]{1,0:T(8,128)(2,1)S(1)}, bf16[512,1024]{1,0:T(8,128)(2,1)S(1)}) fusion(s32[]{:T(128)S(6)} %select_n.95, bf16[1,512,1024]{2,1,0:T(8,128)(2,1)} %bitcast.18, bf16[1,512,1024]{2,1,0:T(8,128)(2,1)} %bitcast.20, s32[]{:T(128)S(6)} %select_n.96, ...), kind=kLoop, calls=%fused_computation.50 | loop fusion | flops 2097152 | bytes 8388616 | tf_op jit(solution)/shard_map/jit(dynamic_index_in_dim)/squeeze | solution.py:50
  65.5 1.2 fusion.14
  66.9 1.3 fusion.1
  68.2 0.6 copy-done.4
  68.8 1.5 fusion.22
  70.4 1.3 fusion.2
  71.7 0.4 pad_maximum_fusion
  72.1 6.3 %copy.109 = bf16[512,2,2048]{2,1,0:T(2,128)(2,1)} copy(bf16[512,2,2048]{2,0,1:T(8,128)(2,1)S(1)} %pad_maximum_fusion) | data formatting | bytes 8388608 | tf_op jit(solution)/shard_map/stack | solution.py:117
  78.4 12.1 %convert_element_type.123 = bf16[1024,2,1024]{2,1,0:T(2,128)(2,1)} reshape(bf16[512,2,2048]{2,1,0:T(2,128)(2,1)} %copy.109) | data formatting | bytes 8388608 | tf_op jit(solution)/shard_map/convert_element_type | solution.py:117
  90.5 9.0 %slice_convert_fusion = (f32[1024,1,1024]{2,1,0:T(1,128)S(1)}, bf16[1024,1,1024]{2,1,0:T(2,128)(2,1)S(1)}) fusion(bf16[1024,2,1024]{2,1,0:T(2,128)(2,1)} %convert_element_type.123), kind=kLoop, calls=%fused_computation | loop fusion | flops 1048576 | bytes 10485760 | tf_op jit(solution)/shard_map/convert_element_type | solution.py:57
  99.5 0.8 copy.145
  100.3 0.6 collective-permute-start.2
  100.9 3.8 %collective-permute-done.2 = bf16[1024,1024]{1,0:T(8,128)(2,1)S(1)} collective-permute-done((bf16[1024,1024]{1,0:T(8,128)(2,1)S(1)}, bf16[1024,1024]{1,0:T(8,128)(2,1)S(1)}, u32[]{:S(2)}, u32[]{:S(2)}) %collective-permute-start.2) | collective-permute-done | bytes 2097184 | tf_op jit(solution)/shard_map/ppermute | solution.py:56
  104.7 1.4 fusion.5
  106.1 0.6 copy.129
  106.7 3.5 %fusion.64 = (bf16[1024,1,128]{2,1,0:T(2,128)(2,1)S(1)}, bf16[1024,1,128]{2,1,0:T(2,128)(2,1)S(1)}, bf16[1024,1,128]{2,1,0:T(2,128)(2,1)S(1)}, bf16[1024,1,128]{...) fusion(bf16[1024,8,128]{2,1,0:T(8,128)(2,1)S(1)} %bitcast.125), kind=kLoop, calls=%fused_computation.119 | loop fusion | bytes 4194304 | tf_op jit(solution)/shard_map/slice | solution.py:59
  110.3 5.9 %collective-permute-start.9 = (bf16[1024,128]{1,0:T(8,128)(2,1)S(1)}, bf16[1024,128]{1,0:T(8,128)(2,1)S(1)}, u32[]{:S(2)}, u32[]{:S(2)}) collective-permute-start(bf16[1024,128]{1,0:T(8,128)(2,1)S(1)} %bitcast.137), channel_id=1, source_target_pairs={{0,224},{32,0},{64,32},{96,64},{128,96},{160,128},{192,160},{224,1... | collective-permute-start | bytes 786440 | tf_op jit(solution)/shard_map/ppermute | solution.py:61
  116.7 4.3 %collective-permute-start.5 = (bf16[1024,128]{1,0:T(8,128)(2,1)S(1)}, bf16[1024,128]{1,0:T(8,128)(2,1)S(1)}, u32[]{:S(2)}, u32[]{:S(2)}) collective-permute-start(bf16[1024,128]{1,0:T(8,128)(2,1)S(1)} %bitcast.134), channel_id=1, source_target_pairs={{0,96},{32,128},{64,160},{96,192},{128,224},{160,0},{192,32},{224,... | collective-permute-start | bytes 786440 | tf_op jit(solution)/shard_map/ppermute | solution.py:61
  121.0 2.2 %collective-permute-start.6 = (bf16[1024,128]{1,0:T(8,128)(2,1)S(1)}, bf16[1024,128]{1,0:T(8,128)(2,1)S(1)}, u32[]{:S(2)}, u32[]{:S(2)}) collective-permute-start(bf16[1024,128]{1,0:T(8,128)(2,1)S(1)} %bitcast.133), channel_id=1, source_target_pairs={{0,128},{32,160},{64,192},{96,224},{128,0},{160,32},{192,64},{224,... | collective-permute-start | bytes 786440 | tf_op jit(solution)/shard_map/ppermute | solution.py:61
  123.2 3.3 %collective-permute-start.7 = (bf16[1024,128]{1,0:T(8,128)(2,1)S(1)}, bf16[1024,128]{1,0:T(8,128)(2,1)S(1)}, u32[]{:S(2)}, u32[]{:S(2)}) collective-permute-start(bf16[1024,128]{1,0:T(8,128)(2,1)S(1)} %bitcast.132), channel_id=1, source_target_pairs={{0,160},{32,192},{64,224},{96,0},{128,32},{160,64},{192,96},{224,1... | collective-permute-start | bytes 786440 | tf_op jit(solution)/shard_map/ppermute | solution.py:61
  126.5 1.9 %collective-permute-done.3 = bf16[1024,128]{1,0:T(8,128)(2,1)S(1)} collective-permute-done((bf16[1024,128]{1,0:T(8,128)(2,1)S(1)}, bf16[1024,128]{1,0:T(8,128)(2,1)S(1)}, u32[]{:S(2)}, u32[]{:S(2)}) %collective-permute-start.3) | collective-permute-done | bytes 262176 | tf_op jit(solution)/shard_map/ppermute | solution.py:61
  128.4 0.7 collective-permute-start.8
  129.2 2.8 %fusion.4 = bf16[1,512,2048]{2,1,0:T(8,128)(2,1)} fusion(bf16[512,1024]{1,0:T(8,128)(2,1)S(1)} %copy-done.13, bf16[512,1024]{1,0:T(8,128)(2,1)S(1)} %copy-done.11, f32[512,512]{1,0:T(8,128)S(1)} %copy-done.17, pred[512]{0:T(512)(128)(4,1)S(1)} %lt.80), kind=kOutput, calls=%fused_computation.19 | convolution fusion | flops 1080557568 | bytes 5243392 | tf_op jit(solution)/shard_map/dot_general | solution.py:37
  132.0 7.3 %collective-permute-done.4 = bf16[1024,128]{1,0:T(8,128)(2,1)S(1)} collective-permute-done((bf16[1024,128]{1,0:T(8,128)(2,1)S(1)}, bf16[1024,128]{1,0:T(8,128)(2,1)S(1)}, u32[]{:S(2)}, u32[]{:S(2)}) %collective-permute-start.4) | collective-permute-done | bytes 262176 | tf_op jit(solution)/shard_map/ppermute | solution.py:61
  139.3 15.7 %collective-permute-done.5 = bf16[1024,128]{1,0:T(8,128)(2,1)S(1)} collective-permute-done((bf16[1024,128]{1,0:T(8,128)(2,1)S(1)}, bf16[1024,128]{1,0:T(8,128)(2,1)S(1)}, u32[]{:S(2)}, u32[]{:S(2)}) %collective-permute-start.5) | collective-permute-done | bytes 262176 | tf_op jit(solution)/shard_map/ppermute | solution.py:61
  155.0 4.2 %collective-permute-done.6 = bf16[1024,128]{1,0:T(8,128)(2,1)S(1)} collective-permute-done((bf16[1024,128]{1,0:T(8,128)(2,1)S(1)}, bf16[1024,128]{1,0:T(8,128)(2,1)S(1)}, u32[]{:S(2)}, u32[]{:S(2)}) %collective-permute-start.6) | collective-permute-done | bytes 262176 | tf_op jit(solution)/shard_map/ppermute | solution.py:61
  159.1 6.5 %collective-permute-done.8 = bf16[1024,128]{1,0:T(8,128)(2,1)S(1)} collective-permute-done((bf16[1024,128]{1,0:T(8,128)(2,1)S(1)}, bf16[1024,128]{1,0:T(8,128)(2,1)S(1)}, u32[]{:S(2)}, u32[]{:S(2)}) %collective-permute-start.8) | collective-permute-done | bytes 262176 | tf_op jit(solution)/shard_map/ppermute | solution.py:61
  165.7 0.3 fusion.42
  165.9 0.8 convert_element_type.138
  166.7 7.3 %all-to-all-start.3 = ((bf16[16,32,256]{2,1,0:T(8,128)(2,1)}), bf16[16,32,256]{2,1,0:T(8,128)(2,1)S(1)}, u32[]{:S(2)}, u32[]{:S(2)}) async-start(bf16[16,32,256]{2,1,0:T(8,128)(2,1)} %convert_element_type.138), calls=%async_computation.3 | async-start | bytes 524288 | tf_op jit(solution)/shard_map/all_to_all | solution.py:120
  174.1 2.6 %fusion.3 = bf16[1,2048,512]{2,1,0:T(8,128)(2,1)} fusion(bf16[512,512]{1,0:T(8,128)(2,1)S(1)} %fusion.22, bf16[512,1024]{1,0:T(8,128)(2,1)S(1)} %copy-done.7, bf16[512,1024]{1,0:T(8,128)(2,1)S(1)} %copy-done.9), kind=kOutput, calls=%fused_computation.18 | convolution fusion | flops 1078984704 | bytes 4718592 | tf_op jit(solution)/shard_map/dot_general | solution.py:40
  176.7 4.9 %all-to-all-done.3 = bf16[16,32,256]{2,1,0:T(8,128)(2,1)S(1)} async-done(((bf16[16,32,256]{2,1,0:T(8,128)(2,1)}), bf16[16,32,256]{2,1,0:T(8,128)(2,1)S(1)}, u32[]{:S(2)}, u32[]{:S(2)}) %all-to-all-start.3) | async-done | bytes 262176 | tf_op jit(solution)/shard_map/all_to_all | solution.py:120
  181.6 0.3 fusion.43
  181.9 0.3 fusion.44
  182.2 0.9 multiply_reduce_fusion
  183.1 0.8 reduce_sum.58
  (62 shorter events, 1.1 us)
Async XLA Ops:
  0.6 3.1 %copy-start = (bf16[128,2048]{1,0:T(8,128)(2,1)S(1)}, bf16[128,2048]{1,0:T(8,128)(2,1)}, u32[]{:S(2)}) copy-start(bf16[128,2048]{1,0:T(8,128)(2,1)} %param.6) | copy-start | bytes 1572868
  0.6 12.0 %copy-start.15 = (f32[128,2]{0,1:T(2,128)S(1)}, f32[128,2]{0,1:T(2,128)}, u32[]{:S(2)}) copy-start(f32[128,2]{0,1:T(2,128)} %param.8) | copy-start | bytes 3076
  1.5 11.4 %copy-start.14 = (bf16[128,2048]{1,0:T(8,128)(2,1)S(1)}, bf16[128,2048]{1,0:T(8,128)(2,1)}, u32[]{:S(2)}) copy-start(bf16[128,2048]{1,0:T(8,128)(2,1)} %param.9) | copy-start | bytes 1572868
  5.2 23.4 %all-to-all-start.1 = ((bf16[16,32,1024]{2,1,0:T(8,128)(2,1)}), bf16[16,32,1024]{2,1,0:T(8,128)(2,1)}, u32[]{:S(2)}, u32[]{:S(2)}) async-start(bf16[16,32,1024]{2,1,0:T(8,128)(2,1)} %bitcast.6), calls=%async_computation.1 | async-start | bytes 2097152 | tf_op jit(solution)/shard_map/all_to_all | solution.py:72
  16.4 37.6 %copy-start.2 = (bf16[1,2048,512]{2,1,0:T(8,128)(2,1)S(1)}, bf16[1,2048,512]{2,1,0:T(8,128)(2,1)}, u32[]{:S(2)}) copy-start(bf16[1,2048,512]{2,1,0:T(8,128)(2,1)} %param.10) | copy-start | bytes 6291460
  28.6 20.8 %all-to-all-start.2 = ((bf16[16,32,1024]{2,1,0:T(8,128)(2,1)}), bf16[16,32,1024]{2,1,0:T(8,128)(2,1)}, u32[]{:S(2)}, u32[]{:S(2)}) async-start(bf16[16,32,1024]{2,1,0:T(8,128)(2,1)} %bitcast.17), calls=%async_computation.2 | async-start | bytes 2097152 | tf_op jit(solution)/shard_map/all_to_all | solution.py:72
  35.3 26.7 %collective-permute-start = (bf16[512,1024]{1,0:T(8,128)(2,1)}, bf16[512,1024]{1,0:T(8,128)(2,1)}, u32[]{:S(2)}, u32[]{:S(2)}) collective-permute-start(bf16[512,1024]{1,0:T(8,128)(2,1)} %bitcast.8), channel_id=1, source_target_pairs={{0,16},{16,0},{1,17},{17,1},{2,18},{18,2},{3,19},{19,3},{4,20},{20... | collective-permute-start | bytes 3145736 | tf_op jit(solution)/shard_map/ppermute | solution.py:75
  49.4 12.4 %all-to-all-start = ((bf16[16,1,2]{2,1,0:T(2,128)(2,1)}), bf16[16,1,2]{2,1,0:T(2,128)(2,1)S(1)}, u32[]{:S(2)}, u32[]{:S(2)}) async-start(bf16[16,1,2]{2,1,0:T(2,128)(2,1)} %copy.102), calls=%async_computation | async-start | bytes 16384 | tf_op jit(solution)/shard_map/all_to_all | solution.py:106
  54.1 8.0 %collective-permute-start.1 = (bf16[512,1024]{1,0:T(8,128)(2,1)}, bf16[512,1024]{1,0:T(8,128)(2,1)}, u32[]{:S(2)}, u32[]{:S(2)}) collective-permute-start(bf16[512,1024]{1,0:T(8,128)(2,1)} %bitcast.19), channel_id=1, source_target_pairs={{0,16},{16,0},{1,17},{17,1},{2,18},{18,2},{3,19},{19,3},{4,20},{20... | collective-permute-start | bytes 3145736 | tf_op jit(solution)/shard_map/ppermute | solution.py:75
  62.0 3.5 %copy-start.3 = (bf16[1,2048,512]{2,1,0:T(8,128)(2,1)S(1)}, bf16[1,2048,512]{2,1,0:T(8,128)(2,1)}, u32[]{:S(2)}) copy-start(bf16[1,2048,512]{2,1,0:T(8,128)(2,1)} %param.10) | copy-start | bytes 6291460
  65.5 1.3 copy-start.6
  65.5 1.4 copy-start.8
  65.5 2.7 %copy-start.10 = (bf16[512,1024]{1,0:T(8,128)(2,1)}, bf16[512,1024]{1,0:T(8,128)(2,1)S(1)}, u32[]{:S(2)}) copy-start(bf16[512,1024]{1,0:T(8,128)(2,1)S(1)} %get-tuple-element.18) | copy-start | bytes 3145732
  65.5 2.7 %copy-start.12 = (bf16[512,1024]{1,0:T(8,128)(2,1)}, bf16[512,1024]{1,0:T(8,128)(2,1)S(1)}, u32[]{:S(2)}) copy-start(bf16[512,1024]{1,0:T(8,128)(2,1)S(1)} %get-tuple-element.19) | copy-start | bytes 3145732
  66.9 1.4 copy-start.16
  66.9 1.9 %copy-start.4 = (bf16[1,512,2048]{2,1,0:T(8,128)(2,1)S(1)}, bf16[1,512,2048]{2,1,0:T(8,128)(2,1)}, u32[]{:S(2)}) copy-start(bf16[1,512,2048]{2,1,0:T(8,128)(2,1)} %param.11) | copy-start | bytes 6291460
  68.8 1.6 copy-start.5
  100.3 4.4 %collective-permute-start.2 = (bf16[1024,1024]{1,0:T(8,128)(2,1)S(1)}, bf16[1024,1024]{1,0:T(8,128)(2,1)S(1)}, u32[]{:S(2)}, u32[]{:S(2)}) collective-permute-start(bf16[1024,1024]{1,0:T(8,128)(2,1)S(1)} %bitcast.127), channel_id=1, source_target_pairs={{0,16},{16,0},{1,17},{17,1},{2,18},{18,2},{3,19},{19,3},{4,20},{20... | collective-permute-start | bytes 6291464 | tf_op jit(solution)/shard_map/ppermute | solution.py:56
  110.3 13.0 %collective-permute-start.9 = (bf16[1024,128]{1,0:T(8,128)(2,1)S(1)}, bf16[1024,128]{1,0:T(8,128)(2,1)S(1)}, u32[]{:S(2)}, u32[]{:S(2)}) collective-permute-start(bf16[1024,128]{1,0:T(8,128)(2,1)S(1)} %bitcast.137), channel_id=1, source_target_pairs={{0,224},{32,0},{64,32},{96,64},{128,96},{160,128},{192,160},{224,1... | collective-permute-start | bytes 786440 | tf_op jit(solution)/shard_map/ppermute | solution.py:61
  116.2 12.9 %copy-start.11 = (bf16[512,1024]{1,0:T(8,128)(2,1)S(1)}, bf16[512,1024]{1,0:T(8,128)(2,1)}, u32[]{:S(2)}) copy-start(bf16[512,1024]{1,0:T(8,128)(2,1)} %copy-done.10) | copy-start | bytes 3145732
  116.2 12.9 %copy-start.13 = (bf16[512,1024]{1,0:T(8,128)(2,1)S(1)}, bf16[512,1024]{1,0:T(8,128)(2,1)}, u32[]{:S(2)}) copy-start(bf16[512,1024]{1,0:T(8,128)(2,1)} %copy-done.12) | copy-start | bytes 3145732
  116.2 12.9 %copy-start.17 = (f32[512,512]{1,0:T(8,128)S(1)}, f32[512,512]{1,0:T(8,128)}, u32[]{:S(2)}) copy-start(f32[512,512]{1,0:T(8,128)} %copy-done.16) | copy-start | bytes 3145732
  116.3 12.2 %collective-permute-start.3 = (bf16[1024,128]{1,0:T(8,128)(2,1)S(1)}, bf16[1024,128]{1,0:T(8,128)(2,1)S(1)}, u32[]{:S(2)}, u32[]{:S(2)}) collective-permute-start(bf16[1024,128]{1,0:T(8,128)(2,1)S(1)} %bitcast.135), channel_id=1, source_target_pairs={{0,32},{32,64},{64,96},{96,128},{128,160},{160,192},{192,224},{224... | collective-permute-start | bytes 786440 | tf_op jit(solution)/shard_map/ppermute | solution.py:61
  116.6 22.7 %collective-permute-start.4 = (bf16[1024,128]{1,0:T(8,128)(2,1)S(1)}, bf16[1024,128]{1,0:T(8,128)(2,1)S(1)}, u32[]{:S(2)}, u32[]{:S(2)}) collective-permute-start(bf16[1024,128]{1,0:T(8,128)(2,1)S(1)} %bitcast.136), channel_id=1, source_target_pairs={{0,64},{32,96},{64,128},{96,160},{128,192},{160,224},{192,0},{224,... | collective-permute-start | bytes 786440 | tf_op jit(solution)/shard_map/ppermute | solution.py:61
  116.7 38.3 %collective-permute-start.5 = (bf16[1024,128]{1,0:T(8,128)(2,1)S(1)}, bf16[1024,128]{1,0:T(8,128)(2,1)S(1)}, u32[]{:S(2)}, u32[]{:S(2)}) collective-permute-start(bf16[1024,128]{1,0:T(8,128)(2,1)S(1)} %bitcast.134), channel_id=1, source_target_pairs={{0,96},{32,128},{64,160},{96,192},{128,224},{160,0},{192,32},{224,... | collective-permute-start | bytes 786440 | tf_op jit(solution)/shard_map/ppermute | solution.py:61
  121.0 38.1 %collective-permute-start.6 = (bf16[1024,128]{1,0:T(8,128)(2,1)S(1)}, bf16[1024,128]{1,0:T(8,128)(2,1)S(1)}, u32[]{:S(2)}, u32[]{:S(2)}) collective-permute-start(bf16[1024,128]{1,0:T(8,128)(2,1)S(1)} %bitcast.133), channel_id=1, source_target_pairs={{0,128},{32,160},{64,192},{96,224},{128,0},{160,32},{192,64},{224,... | collective-permute-start | bytes 786440 | tf_op jit(solution)/shard_map/ppermute | solution.py:61
  123.2 35.9 %collective-permute-start.7 = (bf16[1024,128]{1,0:T(8,128)(2,1)S(1)}, bf16[1024,128]{1,0:T(8,128)(2,1)S(1)}, u32[]{:S(2)}, u32[]{:S(2)}) collective-permute-start(bf16[1024,128]{1,0:T(8,128)(2,1)S(1)} %bitcast.132), channel_id=1, source_target_pairs={{0,160},{32,192},{64,224},{96,0},{128,32},{160,64},{192,96},{224,1... | collective-permute-start | bytes 786440 | tf_op jit(solution)/shard_map/ppermute | solution.py:61
  128.4 37.2 %collective-permute-start.8 = (bf16[1024,128]{1,0:T(8,128)(2,1)S(1)}, bf16[1024,128]{1,0:T(8,128)(2,1)S(1)}, u32[]{:S(2)}, u32[]{:S(2)}) collective-permute-start(bf16[1024,128]{1,0:T(8,128)(2,1)S(1)} %bitcast.131), channel_id=1, source_target_pairs={{0,192},{32,224},{64,0},{96,32},{128,64},{160,96},{192,128},{224,1... | collective-permute-start | bytes 786440 | tf_op jit(solution)/shard_map/ppermute | solution.py:61
  132.0 42.1 %copy-start.7 = (bf16[512,1024]{1,0:T(8,128)(2,1)S(1)}, bf16[512,1024]{1,0:T(8,128)(2,1)}, u32[]{:S(2)}) copy-start(bf16[512,1024]{1,0:T(8,128)(2,1)} %copy-done.6) | copy-start | bytes 3145732
  132.0 42.1 %copy-start.9 = (bf16[512,1024]{1,0:T(8,128)(2,1)S(1)}, bf16[512,1024]{1,0:T(8,128)(2,1)}, u32[]{:S(2)}) copy-start(bf16[512,1024]{1,0:T(8,128)(2,1)} %copy-done.8) | copy-start | bytes 3145732
  166.7 14.8 %all-to-all-start.3 = ((bf16[16,32,256]{2,1,0:T(8,128)(2,1)}), bf16[16,32,256]{2,1,0:T(8,128)(2,1)S(1)}, u32[]{:S(2)}, u32[]{:S(2)}) async-start(bf16[16,32,256]{2,1,0:T(8,128)(2,1)} %convert_element_type.138), calls=%async_computation.3 | async-start | bytes 524288 | tf_op jit(solution)/shard_map/all_to_all | solution.py:120
  174.1 9.8 %copy-start.1 = (bf16[128,2048]{1,0:T(8,128)(2,1)S(1)}, bf16[128,2048]{1,0:T(8,128)(2,1)}, u32[]{:S(2)}) copy-start(bf16[128,2048]{1,0:T(8,128)(2,1)} %param.6) | copy-start | bytes 1572868
where the time goes:
time: 185 us; the launch traced here: 184 us
  waiting for transfers between devices  67.6 us (37%)
  starting transfers between devices  42.8 us (23%)
  local copies, waits for them, and re-layouts  35.9 us (19%)
  other arithmetic  20.7 us (11%)
  matrix products  15.7 us (8%)
    ppermute x7, waiting for transfers between devices, reduce_over_rep(): lax.ppermute(blocks[:, k], 'z', [(j, (j + k) % n_z) for j in range(n_z)])  35.6 us
    all_to_all x2, waiting for transfers between devices, dispatch_rows(): lax.all_to_all(sent.reshape(n_exp, capacity, share), 'exp', split_axis=0,...  23.3 us
    ppermute x7, starting transfers between devices, reduce_over_rep(): lax.ppermute(blocks[:, k], 'z', [(j, (j + k) % n_z) for j in range(n_z)])  16.7 us
    all_to_all x2, starting transfers between devices, dispatch_rows(): lax.all_to_all(sent.reshape(n_exp, capacity, share), 'exp', split_axis=0,...  13.5 us
    convert_element_type x1, local copies, waits for them, and re-layouts, local(): parts = jnp.stack([out_part, dx_part], axis=1).astype(jnp.bfloat16)  12.1 us
    convert_element_type x1, other arithmetic, reduce_over_rep(): halves[:, 0].astype(jnp.float32) + got.astype(jnp.float32)  8.97 us
    all_to_all x1, starting transfers between devices, local(): lax.all_to_all(both.reshape(n_exp, capacity, 2 * cols), 'exp', split_axis...  7.33 us
    unnamed x48, local copies, waits for them, and re-layouts  6.34 us
  transfers between devices with their start and end apart: 14, of which 9 were waited for; matrix products, arithmetic and copies ran while one was open for 11% of the time, Pallas kernels for 0%

commit v1 on v0

--- a/solution.py
+++ b/solution.py
@@ -17,17 +17,16 @@
     return (placed, counts)
 
 
-def expert_math(rows_in, rows_grad, live_mask, up_weight, down_weight, up_perm, down_perm):
+def expert_math(rows_in, rows_grad, up_weight, down_weight, up_perm, down_perm):
     preact = jnp.dot(rows_in, up_weight, preferred_element_type=jnp.float32)
     sigmoid_val = jax.nn.sigmoid(preact)
-    keep = live_mask[:, None]
-    hidden_units = jnp.where(keep, preact * sigmoid_val, 0.0).astype(jnp.bfloat16)
+    hidden_units = (preact * sigmoid_val).astype(jnp.bfloat16)
     out_part = jnp.dot(hidden_units, down_perm, preferred_element_type=jnp.float32)
     grad_hidden = lax.dot_general(
         rows_grad, down_weight, (((1,), (1,)), ((), ())), preferred_element_type=jnp.float32
     )
     slope = sigmoid_val * (1.0 + preact * (1.0 - sigmoid_val))
-    gradient_before_activation = jnp.where(keep, grad_hidden * slope, 0.0).astype(jnp.bfloat16)
+    gradient_before_activation = (grad_hidden * slope).astype(jnp.bfloat16)
     dx_part = lax.dot_general(
         gradient_before_activation,
         up_perm,
@@ -50,31 +49,48 @@
     return lax.dynamic_index_in_dim(stacked, index, axis=axis, keepdims=False)
 
 
-def reduce_over_rep(part, n_z, n_core, cols):
-    slots = part.shape[0]
-    halves = part.reshape(slots, n_core, n_z * cols)
-    got = lax.ppermute(halves[:, 1], "core", [(j, (j + 1) % n_core) for j in range(n_core)])
-    pair_sum = (halves[:, 0].astype(jnp.float32) + got.astype(jnp.float32)).astype(jnp.bfloat16)
-    blocks = pair_sum.reshape(slots, n_z, cols)
-    acc = blocks[:, 0].astype(jnp.float32)
+def reduce_over_rep(parts, n_z, n_core, cols):
+    share = n_z * cols
+    got = lax.ppermute(
+        jnp.concatenate([p[:, share:] for p in parts], axis=0),
+        "core",
+        [(j, (j + 1) % n_core) for j in range(n_core)],
+    )
+    own = jnp.concatenate([p[:, :share] for p in parts], axis=0)
+    pair_sum = (own.astype(jnp.float32) + got.astype(jnp.float32)).astype(jnp.bfloat16)
+    acc = pair_sum[:, :cols].astype(jnp.float32)
     for k in range(1, n_z):
-        moved = lax.ppermute(blocks[:, k], "z", [(j, (j + k) % n_z) for j in range(n_z)])
+        piece = pair_sum[:, k * cols : (k + 1) * cols]
+        moved = lax.ppermute(piece, "z", [(j, (j + k) % n_z) for j in range(n_z)])
         acc = acc + moved.astype(jnp.float32)
     return acc
 
 
-def dispatch_rows(placed_rows, source, n_exp, capacity, n_core):
+def dispatch_rows(placements, sources, n_exp, capacity, n_core):
     core = lax.axis_index("core")
-    width = source.shape[1]
+    width = sources[0].shape[1]
     share = width // n_core
-    mine = lax.dynamic_slice_in_dim(source, core * share, share, 1)
-    sent = jnp.dot(placed_rows, mine, preferred_element_type=jnp.float32).astype(jnp.bfloat16)
+    sent = jnp.concatenate(
+        [
+            jnp.dot(
+                placed_rows,
+                lax.dynamic_slice_in_dim(source, core * share, share, 1),
+                preferred_element_type=jnp.float32,
+            ).astype(jnp.bfloat16)
+            for placed_rows, source in zip(placements, sources)
+        ],
+        axis=1,
+    )
     got = lax.all_to_all(
-        sent.reshape(n_exp, capacity, share), "exp", split_axis=0, concat_axis=0, tiled=True
-    ).reshape(n_exp * capacity, share)
+        sent.reshape(n_exp, capacity, sent.shape[1]), "exp", split_axis=0, concat_axis=0, tiled=True
+    ).reshape(n_exp * capacity, sent.shape[1])
     other = lax.ppermute(got, "core", [(j, (j + 1) % n_core) for j in range(n_core)])
     pair = jnp.stack([got, other])
-    return jnp.concatenate([pick(pair, core, 0), pick(pair, 1 - core, 0)], axis=1)
+    first, second = pick(pair, core, 0), pick(pair, 1 - core, 0)
+    return [
+        jnp.concatenate([first[:, i * share : (i + 1) * share], second[:, i * share : (i + 1) * share]], axis=1)
+        for i in range(len(sources))
+    ]
 
 
 def local(tokens, expert_ids, gate_values, grad_out, w_up, w_down):
@@ -102,21 +118,15 @@
     grad_rows = grad_rows.reshape(pair_count, width)
     placed, counts = plan_slots(expert_ids, n_exp, capacity)
     summed = placed.reshape(n_exp * capacity, tok_count, top_k).sum(axis=2)
-    count_parts = jnp.stack([counts // 16, counts % 16], axis=1).astype(jnp.bfloat16)
-    got_counts = lax.all_to_all(count_parts, "exp", split_axis=0, concat_axis=0, tiled=True)
-    count_values = got_counts[:, 0].astype(jnp.float32) * 16.0 + got_counts[:, 1].astype(
-        jnp.float32
+    rows_in, rows_grad = dispatch_rows((summed, placed), (tokens, grad_rows), n_exp, capacity, n_core)
+    out_part, dx_part, grad_up_e, grad_down_e = expert_math(
+        rows_in, rows_grad, up_weight, down_weight, up_perm, down_perm
     )
-    slot_mask = jnp.arange(capacity, dtype=jnp.float32)[None, :] < count_values[:, None]
-    live_mask = slot_mask.reshape(-1)
-    rows_in = dispatch_rows(summed, tokens, n_exp, capacity, n_core)
-    rows_grad = dispatch_rows(placed, grad_rows, n_exp, capacity, n_core)
-    out_part, dx_part, grad_up_e, grad_down_e = expert_math(
-        rows_in, rows_grad, live_mask, up_weight, down_weight, up_perm, down_perm
+    acc = reduce_over_rep(
+        (out_part.astype(jnp.bfloat16), dx_part.astype(jnp.bfloat16)), n_z, n_core, cols
     )
-    parts = jnp.stack([out_part, dx_part], axis=1).astype(jnp.bfloat16)
-    both = reduce_over_rep(parts.reshape(n_exp * capacity * 2, width), n_z, n_core, cols)
-    both = both.reshape(n_exp * capacity, 2 * cols).astype(jnp.bfloat16)
+    slots = n_exp * capacity
+    both = jnp.concatenate([acc[:slots], acc[slots:]], axis=1).astype(jnp.bfloat16)
     back_both = lax.all_to_all(
         both.reshape(n_exp, capacity, 2 * cols), "exp", split_axis=0, concat_axis=0, tiled=True
     ).reshape(n_exp * capacity, 2 * cols)

time: 185 us -> 152 us (0.82)
  the two profiles are of different devices: /device:TPU:2 before, /device:TPU:32 now
where the time goes in v1:
time: 152 us; the launch traced here: 151 us
  waiting for transfers between devices  49.5 us (33%)
  blocking collectives  35.2 us (23%)
  starting transfers between devices  21.1 us (14%)
  local copies, waits for them, and re-layouts  18.9 us (12%)
  matrix products  13.4 us (9%)
  other arithmetic  12.1 us (8%)
    ppermute x7, waiting for transfers between devices, reduce_over_rep(): moved = lax.ppermute(piece, 'z', [(j, (j + k) % n_z) for j in range(n_z)])  39.2 us
    all_to_all x1, blocking collectives, dispatch_rows(): lax.all_to_all(sent.reshape(n_exp, capacity, sent.shape[1]), 'exp', split...  35.2 us
    ppermute x7, starting transfers between devices, reduce_over_rep(): moved = lax.ppermute(piece, 'z', [(j, (j + k) % n_z) for j in range(n_z)])  17 us
    unnamed x17, local copies, waits for them, and re-layouts  9.26 us
    all_to_all x1, waiting for transfers between devices, local(): lax.all_to_all(both.reshape(n_exp, capacity, 2 * cols), 'exp', split_axis...  6.48 us
    mul x3, local copies, waits for them, and re-layouts, local(): gate_values[:, :, None] * grad_out[:, None, :].astype(jnp.float32)  4.67 us
    ppermute x1, waiting for transfers between devices, reduce_over_rep(): lax.ppermute(jnp.concatenate([p[:, share:] for p in parts], axis=0), 'cor...  3.79 us
    all_to_all x1, starting transfers between devices, local(): lax.all_to_all(both.reshape(n_exp, capacity, 2 * cols), 'exp', split_axis...  3.53 us
  transfers between devices with their start and end apart: 10, of which 6 were waited for; matrix products, arithmetic and copies ran while one was open for 11% of the time, Pallas kernels for 0%

profile of v1, /device:TPU:32, one launch (start us, length us, event | category | flops | bytes accessed | tf_op | source)
XLA Modules:
  0.0 151.1 jit_solution(7245402498469686608)
XLA Ops:
  0.6 0.0 copy-start
  0.6 0.8 copy.41
  1.5 0.1 eq.55
  1.6 0.1 reshape.78
  1.8 0.6 reduce-window.6
  2.4 0.2 slice_reduce_fusion
  2.6 0.1 fusion.37
  2.7 0.1 reduce_sum.42
  2.9 0.8 copy.40
  3.6 0.1 mul.67
  3.8 2.1 %mul.69 = f32[128,2,2048]{2,1,0:T(2,128)S(1)} broadcast(bf16[128,2048]{1,0:T(8,128)(2,1)} %param.9), dimensions={0,2} | broadcast | bytes 2621440 | tf_op jit(solution)/shard_map/mul | solution.py:115
  5.9 2.4 %mul.70 = f32[256,2048]{1,0:T(8,128)} reshape(f32[128,2,2048]{2,1,0:T(2,128)S(1)} %mul.69) | data formatting | bytes 4194304 | tf_op jit(solution)/shard_map/mul | solution.py:115
  8.3 0.1 copy.44
  8.4 0.1 fusion.28
  8.5 0.4 convolution_convert_fusion.4
  8.9 1.8 %convolution_convert_fusion.5 = bf16[512,1024]{1,0:T(8,128)(2,1)S(1)} fusion(f32[256,2048]{1,0:T(8,128)} %mul.70, s32[]{:T(128)S(6)} %select_n.46, f32[256]{0:T(256)S(1)} %mul.67, s32[256]{0:T(256)S(1)} %multiply_add_fusion.1), kind=kOutput, calls=%fused_computation.38 | convolution fusion | flops 269615104 | bytes 2099204 | tf_op jit(solution)/shard_map/dot_general | solution.py:75
  10.7 0.2 pad_maximum_fusion
  10.9 35.2 %all_to_all.10 = bf16[16,32,2048]{2,1,0:T(8,128)(2,1)S(1)} all-to-all(bf16[16,32,2048]{2,1,0:T(8,128)(2,1)S(1)} %bitcast.62), channel_id=1, replica_groups=mesh['z'=8,'core'=2,'exp'=16] {'exp'}, dimensions={0} | all-to-all | bytes 4194304 | tf_op jit(solution)/shard_map/all_to_all | solution.py:84
  46.1 3.9 %copy.46 = bf16[1,512,2048]{1,2,0:T(8,128)(2,1)} copy(bf16[1,512,2048]{2,1,0:T(8,128)(2,1)} %param.11) | data formatting | bytes 4194304 | tf_op args[5]
  50.0 2.3 %fusion.7 = bf16[512,8,2,128]{0,3,2,1:T(8,128)(2,1)S(1)} fusion(s32[]{:T(128)S(6)} %select_n.50, bf16[512,8,2,128]{0,3,2,1:T(8,128)(2,1)} %bitcast.61), kind=kLoop, calls=%fused_computation.24 | loop fusion | flops 1048576 | bytes 4194308 | tf_op jit(solution)/shard_map/jit(_roll_dynamic)/concatenate | solution.py:111
  52.3 0.8 fusion.6
  53.1 1.5 %copy.47 = bf16[512,2,8,128]{0,3,2,1:T(8,128)(2,1)} copy(bf16[512,2,8,128]{0,3,1,2:T(8,128)(2,1)S(1)} %fusion.6) | data formatting | bytes 4194304 | tf_op jit(solution)/shard_map/transpose | solution.py:112
  54.6 0.8 copy-done.1
  55.4 0.8 fusion.4
  56.2 0.8 fusion.3
  56.9 1.5 %copy.48 = bf16[2,8,128,512]{3,2,1,0:T(8,128)(2,1)} copy(bf16[2,8,128,512]{3,2,0,1:T(8,128)(2,1)S(1)} %fusion.3) | data formatting | bytes 4194304 | tf_op jit(solution)/shard_map/transpose | solution.py:114
  58.5 2.8 %fusion.11 = (bf16[512,2048]{1,0:T(8,128)(2,1)S(1)}, bf16[512,2048]{1,0:T(8,128)(2,1)S(1)}) fusion(s32[]{:T(128)S(6)} %select_n.47, bf16[1,512,2048]{2,1,0:T(8,128)(2,1)S(1)} %bitcast.60, bf16[1,512,2048]{2,1,0:T(8,128)(2,1)} %bitcast.4, s32[]{:T(128)S(6)} %select_n.48), kind=kLoop, calls=%fused_computation.28 | loop fusion | flops 2097152 | bytes 8388616 | tf_op jit(solution)/shard_map/jit(dynamic_index_in_dim)/squeeze | solution.py:49
  61.2 0.6 fusion.48
  61.8 1.0 copy-done.2
  62.8 1.2 fusion.14
  64.1 0.3 copy-done.5
  64.4 1.3 convolution_convert_fusion.3
  65.7 0.2 fusion.46
  65.9 1.4 copy-done.3
  67.3 1.4 fusion.19
  68.8 0.1 copy-done.4
  68.9 1.3 convolution_convert_fusion.2
  70.2 0.2 fusion.47
  70.4 0.2 pad_maximum_fusion.3
  70.6 0.6 collective-permute-start.1
  71.2 3.8 %collective-permute-done.1 = bf16[1024,1024]{1,0:T(8,128)(2,1)S(1)} collective-permute-done((bf16[1024,1024]{1,0:T(8,128)(2,1)S(1)}, bf16[1024,1024]{1,0:T(8,128)(2,1)S(1)}, u32[]{:S(2)}, u32[]{:S(2)}) %collective-permute-start.1) | collective-permute-done | bytes 2097184 | tf_op jit(solution)/shard_map/ppermute | solution.py:54
  75.0 1.0 add_convert_fusion
  76.0 0.3 fusion.45
  76.3 2.2 %collective-permute-start.2 = (bf16[1024,128]{1,0:T(8,128)(2,1)S(1)}, bf16[1024,128]{1,0:T(8,128)(2,1)S(1)}, u32[]{:S(2)}, u32[]{:S(2)}) collective-permute-start(bf16[1024,128]{1,0:T(8,128)(2,1)S(1)} %get-tuple-element.6), channel_id=1, source_target_pairs={{0,32},{32,64},{64,96},{96,128},{128,160},{160,192},{192,224},{224... | collective-permute-start | bytes 786440 | tf_op jit(solution)/shard_map/ppermute | solution.py:64
  78.5 4.5 %collective-permute-start.3 = (bf16[1024,128]{1,0:T(8,128)(2,1)S(1)}, bf16[1024,128]{1,0:T(8,128)(2,1)S(1)}, u32[]{:S(2)}, u32[]{:S(2)}) collective-permute-start(bf16[1024,128]{1,0:T(8,128)(2,1)S(1)} %get-tuple-element.12), channel_id=1, source_target_pairs={{0,64},{32,96},{64,128},{96,160},{128,192},{160,224},{192,0},{224,... | collective-permute-start | bytes 786440 | tf_op jit(solution)/shard_map/ppermute | solution.py:64
  83.0 2.0 %collective-permute-start.4 = (bf16[1024,128]{1,0:T(8,128)(2,1)S(1)}, bf16[1024,128]{1,0:T(8,128)(2,1)S(1)}, u32[]{:S(2)}, u32[]{:S(2)}) collective-permute-start(bf16[1024,128]{1,0:T(8,128)(2,1)S(1)} %get-tuple-element.11), channel_id=1, source_target_pairs={{0,96},{32,128},{64,160},{96,192},{128,224},{160,0},{192,32},{224,... | collective-permute-start | bytes 786440 | tf_op jit(solution)/shard_map/ppermute | solution.py:64
  85.0 1.4 collective-permute-start.5
  86.4 3.2 %collective-permute-start.6 = (bf16[1024,128]{1,0:T(8,128)(2,1)S(1)}, bf16[1024,128]{1,0:T(8,128)(2,1)S(1)}, u32[]{:S(2)}, u32[]{:S(2)}) collective-permute-start(bf16[1024,128]{1,0:T(8,128)(2,1)S(1)} %get-tuple-element.9), channel_id=1, source_target_pairs={{0,160},{32,192},{64,224},{96,0},{128,32},{160,64},{192,96},{224,1... | collective-permute-start | bytes 786440 | tf_op jit(solution)/shard_map/ppermute | solution.py:64
  89.6 2.4 %collective-permute-start.7 = (bf16[1024,128]{1,0:T(8,128)(2,1)S(1)}, bf16[1024,128]{1,0:T(8,128)(2,1)S(1)}, u32[]{:S(2)}, u32[]{:S(2)}) collective-permute-start(bf16[1024,128]{1,0:T(8,128)(2,1)S(1)} %get-tuple-element.8), channel_id=1, source_target_pairs={{0,192},{32,224},{64,0},{96,32},{128,64},{160,96},{192,128},{224,1... | collective-permute-start | bytes 786440 | tf_op jit(solution)/shard_map/ppermute | solution.py:64
  91.9 10.4 %collective-permute-done.3 = bf16[1024,128]{1,0:T(8,128)(2,1)S(1)} collective-permute-done((bf16[1024,128]{1,0:T(8,128)(2,1)S(1)}, bf16[1024,128]{1,0:T(8,128)(2,1)S(1)}, u32[]{:S(2)}, u32[]{:S(2)}) %collective-permute-start.3) | collective-permute-done | bytes 262176 | tf_op jit(solution)/shard_map/ppermute | solution.py:64
  102.3 1.3 collective-permute-start.8
  103.6 2.7 %fusion.1 = bf16[1,512,2048]{2,1,0:T(8,128)(2,1)} fusion(bf16[512,1024]{1,0:T(8,128)(2,1)S(1)} %get-tuple-element.23, bf16[512,1024]{1,0:T(8,128)(2,1)S(1)} %get-tuple-element.18, f32[512,512]{1,0:T(8,128)S(1)} %fusion.14), kind=kOutput, calls=%fused_computation.18 | convolution fusion | flops 1080295424 | bytes 5242880 | tf_op jit(solution)/shard_map/dot_general | solution.py:36
  106.3 18.1 %collective-permute-done.4 = bf16[1024,128]{1,0:T(8,128)(2,1)S(1)} collective-permute-done((bf16[1024,128]{1,0:T(8,128)(2,1)S(1)}, bf16[1024,128]{1,0:T(8,128)(2,1)S(1)}, u32[]{:S(2)}, u32[]{:S(2)}) %collective-permute-start.4) | collective-permute-done | bytes 262176 | tf_op jit(solution)/shard_map/ppermute | solution.py:64
  124.4 6.5 %collective-permute-done.7 = bf16[1024,128]{1,0:T(8,128)(2,1)S(1)} collective-permute-done((bf16[1024,128]{1,0:T(8,128)(2,1)S(1)}, bf16[1024,128]{1,0:T(8,128)(2,1)S(1)}, u32[]{:S(2)}, u32[]{:S(2)}) %collective-permute-start.7) | collective-permute-done | bytes 262176 | tf_op jit(solution)/shard_map/ppermute | solution.py:64
  130.9 4.2 %collective-permute-done.8 = bf16[1024,128]{1,0:T(8,128)(2,1)S(1)} collective-permute-done((bf16[1024,128]{1,0:T(8,128)(2,1)S(1)}, bf16[1024,128]{1,0:T(8,128)(2,1)S(1)}, u32[]{:S(2)}, u32[]{:S(2)}) %collective-permute-start.8) | collective-permute-done | bytes 262176 | tf_op jit(solution)/shard_map/ppermute | solution.py:64
  135.1 0.3 add_convert_fusion.1
  135.4 0.7 pad_maximum_fusion.10
  136.2 3.5 %all-to-all-start.1 = ((bf16[16,32,256]{2,1,0:T(8,128)(2,1)}), bf16[16,32,256]{2,1,0:T(8,128)(2,1)S(1)}, u32[]{:S(2)}, u32[]{:S(2)}) async-start(bf16[16,32,256]{2,1,0:T(8,128)(2,1)} %pad_maximum_fusion.10), calls=%async_computation.1 | async-start | bytes 524288 | tf_op jit(solution)/shard_map/all_to_all | solution.py:130
  139.7 2.6 %fusion = bf16[1,2048,512]{2,1,0:T(8,128)(2,1)} fusion(bf16[512,512]{1,0:T(8,128)(2,1)S(1)} %fusion.19, bf16[512,1024]{1,0:T(8,128)(2,1)S(1)} %get-tuple-element.24, bf16[512,1024]{1,0:T(8,128)(2,1)S(1)} %get-tuple-element.17), kind=kOutput, calls=%fused_computation.17 | convolution fusion | flops 1078984704 | bytes 4718592 | tf_op jit(solution)/shard_map/dot_general | solution.py:39
  142.3 6.5 %all-to-all-done.1 = bf16[16,32,256]{2,1,0:T(8,128)(2,1)S(1)} async-done(((bf16[16,32,256]{2,1,0:T(8,128)(2,1)}), bf16[16,32,256]{2,1,0:T(8,128)(2,1)S(1)}, u32[]{:S(2)}, u32[]{:S(2)}) %all-to-all-start.1) | async-done | bytes 262176 | tf_op jit(solution)/shard_map/all_to_all | solution.py:130
  148.8 0.3 fusion.25
  149.1 0.3 fusion.26
  149.5 0.9 multiply_reduce_fusion
  150.3 0.8 reduce_sum.45
  (19 shorter events, 0.1 us)
Async XLA Ops:
  0.6 7.9 %copy-start = (bf16[128,2048]{1,0:T(8,128)(2,1)S(1)}, bf16[128,2048]{1,0:T(8,128)(2,1)}, u32[]{:S(2)}) copy-start(bf16[128,2048]{1,0:T(8,128)(2,1)} %param.6) | copy-start | bytes 1572868
  5.9 2.5 %copy-start.6 = (s32[128,2]{0,1:T(2,128)S(1)}, s32[128,2]{0,1:T(2,128)}, u32[]{:S(2)}) copy-start(s32[128,2]{0,1:T(2,128)} %param.7) | copy-start | bytes 3076
  46.1 12.3 %collective-permute-start = (bf16[512,2048]{1,0:T(8,128)(2,1)S(1)}, bf16[512,2048]{1,0:T(8,128)(2,1)}, u32[]{:S(2)}, u32[]{:S(2)}) collective-permute-start(bf16[512,2048]{1,0:T(8,128)(2,1)S(1)} %bitcast.59), channel_id=1, source_target_pairs={{0,16},{16,0},{1,17},{17,1},{2,18},{18,2},{3,19},{19,3},{4,20},{20... | collective-permute-start | bytes 6291464 | tf_op jit(solution)/shard_map/ppermute | solution.py:87
  53.0 2.4 %copy-start.1 = (bf16[1,2048,512]{2,1,0:T(8,128)(2,1)S(1)}, bf16[1,2048,512]{2,1,0:T(8,128)(2,1)}, u32[]{:S(2)}) copy-start(bf16[1,2048,512]{2,1,0:T(8,128)(2,1)} %param.10) | copy-start | bytes 6291460
  61.2 1.6 %copy-start.2 = (bf16[1,2048,512]{2,1,0:T(8,128)(2,1)S(1)}, bf16[1,2048,512]{2,1,0:T(8,128)(2,1)}, u32[]{:S(2)}) copy-start(bf16[1,2048,512]{2,1,0:T(8,128)(2,1)} %param.10) | copy-start | bytes 6291460
  62.8 1.6 %copy-start.5 = (bf16[512,2,8,128]{0,3,2,1:T(8,128)(2,1)S(1)}, bf16[512,2,8,128]{0,3,2,1:T(8,128)(2,1)}, u32[]{:S(2)}) copy-start(bf16[512,2,8,128]{0,3,2,1:T(8,128)(2,1)} %copy.47) | copy-start | bytes 6291460
  65.7 1.6 %copy-start.3 = (bf16[1,512,2048]{2,1,0:T(8,128)(2,1)S(1)}, bf16[1,512,2048]{2,1,0:T(8,128)(2,1)}, u32[]{:S(2)}) copy-start(bf16[1,512,2048]{2,1,0:T(8,128)(2,1)} %param.11) | copy-start | bytes 6291460
  67.3 1.6 %copy-start.4 = (bf16[2,8,128,512]{3,2,1,0:T(8,128)(2,1)S(1)}, bf16[2,8,128,512]{3,2,1,0:T(8,128)(2,1)}, u32[]{:S(2)}) copy-start(bf16[2,8,128,512]{3,2,1,0:T(8,128)(2,1)} %copy.48) | copy-start | bytes 6291460
  70.6 4.4 %collective-permute-start.1 = (bf16[1024,1024]{1,0:T(8,128)(2,1)S(1)}, bf16[1024,1024]{1,0:T(8,128)(2,1)S(1)}, u32[]{:S(2)}, u32[]{:S(2)}) collective-permute-start(bf16[1024,1024]{1,0:T(8,128)(2,1)S(1)} %pad_maximum_fusion.3), channel_id=1, source_target_pairs={{0,16},{16,0},{1,17},{17,1},{2,18},{18,2},{3,19},{19,3},{4,20},{20... | collective-permute-start | bytes 6291464 | tf_op jit(solution)/shard_map/ppermute | solution.py:54
  76.3 13.3 %collective-permute-start.2 = (bf16[1024,128]{1,0:T(8,128)(2,1)S(1)}, bf16[1024,128]{1,0:T(8,128)(2,1)S(1)}, u32[]{:S(2)}, u32[]{:S(2)}) collective-permute-start(bf16[1024,128]{1,0:T(8,128)(2,1)S(1)} %get-tuple-element.6), channel_id=1, source_target_pairs={{0,32},{32,64},{64,96},{96,128},{128,160},{160,192},{192,224},{224... | collective-permute-start | bytes 786440 | tf_op jit(solution)/shard_map/ppermute | solution.py:64
  78.5 23.8 %collective-permute-start.3 = (bf16[1024,128]{1,0:T(8,128)(2,1)S(1)}, bf16[1024,128]{1,0:T(8,128)(2,1)S(1)}, u32[]{:S(2)}, u32[]{:S(2)}) collective-permute-start(bf16[1024,128]{1,0:T(8,128)(2,1)S(1)} %get-tuple-element.12), channel_id=1, source_target_pairs={{0,64},{32,96},{64,128},{96,160},{128,192},{160,224},{192,0},{224,... | collective-permute-start | bytes 786440 | tf_op jit(solution)/shard_map/ppermute | solution.py:64
  83.0 41.4 %collective-permute-start.4 = (bf16[1024,128]{1,0:T(8,128)(2,1)S(1)}, bf16[1024,128]{1,0:T(8,128)(2,1)S(1)}, u32[]{:S(2)}, u32[]{:S(2)}) collective-permute-start(bf16[1024,128]{1,0:T(8,128)(2,1)S(1)} %get-tuple-element.11), channel_id=1, source_target_pairs={{0,96},{32,128},{64,160},{96,192},{128,224},{160,0},{192,32},{224,... | collective-permute-start | bytes 786440 | tf_op jit(solution)/shard_map/ppermute | solution.py:64
  85.0 39.4 %collective-permute-start.5 = (bf16[1024,128]{1,0:T(8,128)(2,1)S(1)}, bf16[1024,128]{1,0:T(8,128)(2,1)S(1)}, u32[]{:S(2)}, u32[]{:S(2)}) collective-permute-start(bf16[1024,128]{1,0:T(8,128)(2,1)S(1)} %get-tuple-element.10), channel_id=1, source_target_pairs={{0,128},{32,160},{64,192},{96,224},{128,0},{160,32},{192,64},{224,... | collective-permute-start | bytes 786440 | tf_op jit(solution)/shard_map/ppermute | solution.py:64
  86.4 38.0 %collective-permute-start.6 = (bf16[1024,128]{1,0:T(8,128)(2,1)S(1)}, bf16[1024,128]{1,0:T(8,128)(2,1)S(1)}, u32[]{:S(2)}, u32[]{:S(2)}) collective-permute-start(bf16[1024,128]{1,0:T(8,128)(2,1)S(1)} %get-tuple-element.9), channel_id=1, source_target_pairs={{0,160},{32,192},{64,224},{96,0},{128,32},{160,64},{192,96},{224,1... | collective-permute-start | bytes 786440 | tf_op jit(solution)/shard_map/ppermute | solution.py:64
  89.6 41.3 %collective-permute-start.7 = (bf16[1024,128]{1,0:T(8,128)(2,1)S(1)}, bf16[1024,128]{1,0:T(8,128)(2,1)S(1)}, u32[]{:S(2)}, u32[]{:S(2)}) collective-permute-start(bf16[1024,128]{1,0:T(8,128)(2,1)S(1)} %get-tuple-element.8), channel_id=1, source_target_pairs={{0,192},{32,224},{64,0},{96,32},{128,64},{160,96},{192,128},{224,1... | collective-permute-start | bytes 786440 | tf_op jit(solution)/shard_map/ppermute | solution.py:64
  102.3 32.8 %collective-permute-start.8 = (bf16[1024,128]{1,0:T(8,128)(2,1)S(1)}, bf16[1024,128]{1,0:T(8,128)(2,1)S(1)}, u32[]{:S(2)}, u32[]{:S(2)}) collective-permute-start(bf16[1024,128]{1,0:T(8,128)(2,1)S(1)} %get-tuple-element.7), channel_id=1, source_target_pairs={{0,224},{32,0},{64,32},{96,64},{128,96},{160,128},{192,160},{224,1... | collective-permute-start | bytes 786440 | tf_op jit(solution)/shard_map/ppermute | solution.py:64
  136.2 12.6 %all-to-all-start.1 = ((bf16[16,32,256]{2,1,0:T(8,128)(2,1)}), bf16[16,32,256]{2,1,0:T(8,128)(2,1)S(1)}, u32[]{:S(2)}, u32[]{:S(2)}) async-start(bf16[16,32,256]{2,1,0:T(8,128)(2,1)} %pad_maximum_fusion.10), calls=%async_computation.1 | async-start | bytes 524288 | tf_op jit(solution)/shard_map/all_to_all | solution.py:130

commit v2 on v1

--- a/solution.py
+++ b/solution.py
@@ -58,11 +58,31 @@
     )
     own = jnp.concatenate([p[:, :share] for p in parts], axis=0)
     pair_sum = (own.astype(jnp.float32) + got.astype(jnp.float32)).astype(jnp.bfloat16)
-    acc = pair_sum[:, :cols].astype(jnp.float32)
-    for k in range(1, n_z):
-        piece = pair_sum[:, k * cols : (k + 1) * cols]
-        moved = lax.ppermute(piece, "z", [(j, (j + k) % n_z) for j in range(n_z)])
-        acc = acc + moved.astype(jnp.float32)
+    block = [pair_sum[:, k * cols : (k + 1) * cols] for k in range(n_z)]
+    acc = block[0].astype(jnp.float32)
+    if n_z != 8:
+        for k in range(1, n_z):
+            moved = lax.ppermute(block[k], "z", [(j, (j + k) % n_z) for j in range(n_z)])
+            acc = acc + moved.astype(jnp.float32)
+        return acc
+
+    def shift(x, k):
+        return lax.ppermute(x, "z", [(j, (j + k) % n_z) for j in range(n_z)]).astype(jnp.float32)
+
+    rows = pair_sum.shape[0]
+    top = rows // 2
+    near_up = shift(block[1], 1)
+    near_down = shift(block[7], -1)
+    via_up = shift(block[3], 1)
+    via_down = shift(block[5], -1)
+    far_up = shift(block[4][:top], 2)
+    far_down = shift(block[4][top:], -2)
+    zeros = jnp.zeros((rows - top, cols), jnp.float32)
+    agg_up = block[2].astype(jnp.float32) + via_up + jnp.concatenate([far_up, zeros], axis=0)
+    agg_down = block[6].astype(jnp.float32) + via_down + jnp.concatenate([zeros, far_down], axis=0)
+    acc = acc + near_up + near_down
+    acc = acc + shift(agg_up.astype(jnp.bfloat16), 2)
+    acc = acc + shift(agg_down.astype(jnp.bfloat16), -2)
     return acc
 
 

time: 152 us -> 130 us (0.86)
  the two profiles are of different devices: /device:TPU:32 before, /device:TPU:2 now
where the time goes in v2:
time: 130 us; the launch traced here: 129 us
  blocking collectives  34.3 us (26%)
  waiting for transfers between devices  28.2 us (22%)
  starting transfers between devices  21.5 us (17%)
  local copies, waits for them, and re-layouts  18.9 us (15%)
  matrix products  13.4 us (10%)
  other arithmetic  12.3 us (9%)
    all_to_all x1, blocking collectives, dispatch_rows(): lax.all_to_all(sent.reshape(n_exp, capacity, sent.shape[1]), 'exp', split...  34.3 us
    ppermute x8, waiting for transfers between devices, shift(): lax.ppermute(x, 'z', [(j, (j + k) % n_z) for j in range(n_z)])  19.6 us
    ppermute x8, starting transfers between devices, shift(): lax.ppermute(x, 'z', [(j, (j + k) % n_z) for j in range(n_z)])  16.1 us
    unnamed x17, local copies, waits for them, and re-layouts  9.26 us
    all_to_all x1, waiting for transfers between devices, local(): lax.all_to_all(both.reshape(n_exp, capacity, 2 * cols), 'exp', split_axis...  4.79 us
    all_to_all x1, starting transfers between devices, local(): lax.all_to_all(both.reshape(n_exp, capacity, 2 * cols), 'exp', split_axis...  4.78 us
    mul x3, local copies, waits for them, and re-layouts, local(): gate_values[:, :, None] * grad_out[:, None, :].astype(jnp.float32)  4.67 us
    ppermute x1, waiting for transfers between devices, reduce_over_rep(): lax.ppermute(jnp.concatenate([p[:, share:] for p in parts], axis=0), 'cor...  3.79 us
  transfers between devices with their start and end apart: 11, of which 6 were waited for; matrix products, arithmetic and copies ran while one was open for 13% of the time, Pallas kernels for 0%

profile of v2, /device:TPU:2, one launch (start us, length us, event | category | flops | bytes accessed | tf_op | source)
XLA Modules:
  0.0 129.3 jit_solution(3055087217733191267)
XLA Ops:
  0.6 0.8 copy.41
  1.5 0.1 eq.55
  1.6 0.1 reshape.78
  1.8 0.6 reduce-window.6
  2.4 0.2 slice_reduce_fusion
  2.6 0.1 fusion.37
  2.7 0.1 reduce_sum.42
  2.9 0.8 copy.40
  3.6 0.1 mul.67
  3.8 2.1 %mul.69 = f32[128,2,2048]{2,1,0:T(2,128)S(1)} broadcast(bf16[128,2048]{1,0:T(8,128)(2,1)} %param.9), dimensions={0,2} | broadcast | bytes 2621440 | tf_op jit(solution)/shard_map/mul | solution.py:135
  5.9 2.4 %mul.70 = f32[256,2048]{1,0:T(8,128)} reshape(f32[128,2,2048]{2,1,0:T(2,128)S(1)} %mul.69) | data formatting | bytes 4194304 | tf_op jit(solution)/shard_map/mul | solution.py:135
  8.4 0.1 fusion.28
  8.5 0.4 convolution_convert_fusion.4
  8.9 1.8 %convolution_convert_fusion.5 = bf16[512,1024]{1,0:T(8,128)(2,1)S(1)} fusion(f32[256,2048]{1,0:T(8,128)} %mul.70, s32[]{:T(128)S(6)} %select_n.46, f32[256]{0:T(256)S(1)} %mul.67, s32[256]{0:T(256)S(1)} %multiply_add_fusion.1), kind=kOutput, calls=%fused_computation.38 | convolution fusion | flops 269615104 | bytes 2099204 | tf_op jit(solution)/shard_map/dot_general | solution.py:95
  10.7 0.2 pad_maximum_fusion
  10.9 34.3 %all_to_all.10 = bf16[16,32,2048]{2,1,0:T(8,128)(2,1)S(1)} all-to-all(bf16[16,32,2048]{2,1,0:T(8,128)(2,1)S(1)} %bitcast.62), channel_id=1, replica_groups=mesh['z'=8,'core'=2,'exp'=16] {'exp'}, dimensions={0} | all-to-all | bytes 4194304 | tf_op jit(solution)/shard_map/all_to_all | solution.py:104
  45.2 3.9 %copy.46 = bf16[1,512,2048]{1,2,0:T(8,128)(2,1)} copy(bf16[1,512,2048]{2,1,0:T(8,128)(2,1)} %param.11) | data formatting | bytes 4194304 | tf_op args[5]
  49.1 2.3 %fusion.7 = bf16[512,8,2,128]{0,3,2,1:T(8,128)(2,1)S(1)} fusion(s32[]{:T(128)S(6)} %select_n.50, bf16[512,8,2,128]{0,3,2,1:T(8,128)(2,1)} %bitcast.61), kind=kLoop, calls=%fused_computation.24 | loop fusion | flops 1048576 | bytes 4194308 | tf_op jit(solution)/shard_map/jit(_roll_dynamic)/concatenate | solution.py:131
  51.4 0.8 fusion.6
  52.2 1.5 %copy.47 = bf16[512,2,8,128]{0,3,2,1:T(8,128)(2,1)} copy(bf16[512,2,8,128]{0,3,1,2:T(8,128)(2,1)S(1)} %fusion.6) | data formatting | bytes 4194304 | tf_op jit(solution)/shard_map/transpose | solution.py:132
  53.8 0.8 copy-done.1
  54.6 0.8 fusion.4
  55.3 0.8 fusion.3
  56.1 1.5 %copy.48 = bf16[2,8,128,512]{3,2,1,0:T(8,128)(2,1)} copy(bf16[2,8,128,512]{3,2,0,1:T(8,128)(2,1)S(1)} %fusion.3) | data formatting | bytes 4194304 | tf_op jit(solution)/shard_map/transpose | solution.py:134
  57.6 2.8 %fusion.11 = (bf16[512,2048]{1,0:T(8,128)(2,1)S(1)}, bf16[512,2048]{1,0:T(8,128)(2,1)S(1)}) fusion(s32[]{:T(128)S(6)} %select_n.47, bf16[1,512,2048]{2,1,0:T(8,128)(2,1)S(1)} %bitcast.60, bf16[1,512,2048]{2,1,0:T(8,128)(2,1)} %bitcast.4, s32[]{:T(128)S(6)} %select_n.48), kind=kLoop, calls=%fused_computation.28 | loop fusion | flops 2097152 | bytes 8388616 | tf_op jit(solution)/shard_map/jit(dynamic_index_in_dim)/squeeze | solution.py:49
  60.4 0.6 fusion.49
  61.0 1.0 copy-done.2
  62.0 1.2 fusion.14
  63.2 0.3 copy-done.5
  63.6 1.3 %convolution_convert_fusion.3 = bf16[512,2048]{1,0:T(8,128)(2,1)S(1)} fusion(bf16[512,2048]{0,1:T(8,128)(2,1)S(1)} %bitcast.65, f32[512,512]{1,0:T(8,128)S(1)} %fusion.14), kind=kOutput, calls=%fused_computation.16 | convolution fusion | flops 1076101120 | bytes 5242880 | tf_op jit(solution)/shard_map/dot_general | solution.py:24
  64.9 0.2 fusion.47
  65.1 1.4 %copy-done.3 = bf16[1,512,2048]{2,1,0:T(8,128)(2,1)S(1)} copy-done((bf16[1,512,2048]{2,1,0:T(8,128)(2,1)S(1)}, bf16[1,512,2048]{2,1,0:T(8,128)(2,1)}, u32[]{:S(2)}) %copy-start.3) | copy-done | bytes 2097176
  66.5 1.4 %fusion.19 = bf16[512,512]{1,0:T(8,128)(2,1)S(1)} fusion(bf16[1,512,2048]{2,1,0:T(8,128)(2,1)S(1)} %copy-done.3, bf16[512,1024]{1,0:T(8,128)(2,1)S(1)} %get-tuple-element.24, bf16[512,1024]{1,0:T(8,128)(2,1)S(1)} %get-tuple-element.19, f32[512,512]{1,0:T(8,128)S(1)} %fusion.14), kind=kOutput, calls=%fused_computation.40 | convolution fusion | flops 1080295424 | bytes 5767168 | tf_op jit(solution)/shard_map/dot_general | solution.py:25
  67.9 0.1 copy-done.4
  68.1 1.3 convolution_convert_fusion.2
  69.4 0.2 fusion.48
  69.6 0.2 pad_maximum_fusion.3
  69.7 0.6 collective-permute-start.1
  70.3 3.8 %collective-permute-done.1 = bf16[1024,1024]{1,0:T(8,128)(2,1)S(1)} collective-permute-done((bf16[1024,1024]{1,0:T(8,128)(2,1)S(1)}, bf16[1024,1024]{1,0:T(8,128)(2,1)S(1)}, u32[]{:S(2)}, u32[]{:S(2)}) %collective-permute-start.1) | collective-permute-done | bytes 2097184 | tf_op jit(solution)/shard_map/ppermute | solution.py:54
  74.1 1.0 add_convert_fusion
  75.1 0.2 fusion.45
  75.3 2.1 %collective-permute-start.4 = (bf16[1024,128]{1,0:T(8,128)(2,1)S(1)}, bf16[1024,128]{1,0:T(8,128)(2,1)S(1)}, u32[]{:S(2)}, u32[]{:S(2)}) collective-permute-start(bf16[1024,128]{1,0:T(8,128)(2,1)S(1)} %get-tuple-element.8), channel_id=1, source_target_pairs={{0,32},{32,64},{64,96},{96,128},{128,160},{160,192},{192,224},{224... | collective-permute-start | bytes 786440 | tf_op jit(solution)/shard_map/ppermute | solution.py:70
  77.4 4.1 %collective-permute-start.7 = (bf16[1024,128]{1,0:T(8,128)(2,1)S(1)}, bf16[1024,128]{1,0:T(8,128)(2,1)S(1)}, u32[]{:S(2)}, u32[]{:S(2)}) collective-permute-start(bf16[1024,128]{1,0:T(8,128)(2,1)S(1)} %get-tuple-element.7), channel_id=1, source_target_pairs={{0,224},{32,0},{64,32},{96,64},{128,96},{160,128},{192,160},{224,1... | collective-permute-start | bytes 786440 | tf_op jit(solution)/shard_map/ppermute | solution.py:70
  81.6 0.1 fusion.46
  81.6 0.1 collective-permute-start.5
  81.7 4.1 %collective-permute-start.8 = (bf16[512,128]{1,0:T(8,128)(2,1)S(1)}, bf16[512,128]{1,0:T(8,128)(2,1)S(1)}, u32[]{:S(2)}, u32[]{:S(2)}) collective-permute-start(bf16[512,128]{1,0:T(8,128)(2,1)S(1)} %get-tuple-element.13), channel_id=1, source_target_pairs={{0,192},{32,224},{64,0},{96,32},{128,64},{160,96},{192,128},{224,1... | collective-permute-start | bytes 393224 | tf_op jit(solution)/shard_map/ppermute | solution.py:70
  85.9 9.4 %collective-permute-done.5 = bf16[512,128]{1,0:T(8,128)(2,1)S(1)} collective-permute-done((bf16[512,128]{1,0:T(8,128)(2,1)S(1)}, bf16[512,128]{1,0:T(8,128)(2,1)S(1)}, u32[]{:S(2)}, u32[]{:S(2)}) %collective-permute-start.5) | collective-permute-done | bytes 131104 | tf_op jit(solution)/shard_map/ppermute | solution.py:70
  95.3 1.4 %collective-permute-start.3 = (bf16[1024,128]{1,0:T(8,128)(2,1)S(1)}, bf16[1024,128]{1,0:T(8,128)(2,1)S(1)}, u32[]{:S(2)}, u32[]{:S(2)}) collective-permute-start(bf16[1024,128]{1,0:T(8,128)(2,1)S(1)} %get-tuple-element.9), channel_id=1, source_target_pairs={{0,224},{32,0},{64,32},{96,64},{128,96},{160,128},{192,160},{224,1... | collective-permute-start | bytes 786440 | tf_op jit(solution)/shard_map/ppermute | solution.py:70
  96.7 0.2 add_convert_fusion.3
  96.9 2.2 %collective-permute-start.6 = (bf16[1024,128]{1,0:T(8,128)(2,1)S(1)}, bf16[1024,128]{1,0:T(8,128)(2,1)S(1)}, u32[]{:S(2)}, u32[]{:S(2)}) collective-permute-start(bf16[1024,128]{1,0:T(8,128)(2,1)S(1)} %get-tuple-element.10), channel_id=1, source_target_pairs={{0,64},{32,96},{64,128},{96,160},{128,192},{160,224},{192,0},{224,... | collective-permute-start | bytes 786440 | tf_op jit(solution)/shard_map/ppermute | solution.py:70
  99.1 2.0 %collective-permute-start.9 = (bf16[1024,128]{1,0:T(8,128)(2,1)S(1)}, bf16[1024,128]{1,0:T(8,128)(2,1)S(1)}, u32[]{:S(2)}, u32[]{:S(2)}) collective-permute-start(bf16[1024,128]{1,0:T(8,128)(2,1)S(1)} %get-tuple-element.11), channel_id=1, source_target_pairs={{0,192},{32,224},{64,0},{96,32},{128,64},{160,96},{192,128},{224,1... | collective-permute-start | bytes 786440 | tf_op jit(solution)/shard_map/ppermute | solution.py:70
  101.1 2.6 %fusion.1 = bf16[1,512,2048]{2,1,0:T(8,128)(2,1)} fusion(bf16[512,1024]{1,0:T(8,128)(2,1)S(1)} %get-tuple-element.24, bf16[512,1024]{1,0:T(8,128)(2,1)S(1)} %get-tuple-element.19, f32[512,512]{1,0:T(8,128)S(1)} %fusion.14), kind=kOutput, calls=%fused_computation.18 | convolution fusion | flops 1080295424 | bytes 5242880 | tf_op jit(solution)/shard_map/dot_general | solution.py:36
  103.8 2.6 %collective-permute-done.3 = bf16[1024,128]{1,0:T(8,128)(2,1)S(1)} collective-permute-done((bf16[1024,128]{1,0:T(8,128)(2,1)S(1)}, bf16[1024,128]{1,0:T(8,128)(2,1)S(1)}, u32[]{:S(2)}, u32[]{:S(2)}) %collective-permute-start.3) | collective-permute-done | bytes 262176 | tf_op jit(solution)/shard_map/ppermute | solution.py:70
  106.3 4.5 %collective-permute-done.6 = bf16[1024,128]{1,0:T(8,128)(2,1)S(1)} collective-permute-done((bf16[1024,128]{1,0:T(8,128)(2,1)S(1)}, bf16[1024,128]{1,0:T(8,128)(2,1)S(1)}, u32[]{:S(2)}, u32[]{:S(2)}) %collective-permute-start.6) | collective-permute-done | bytes 262176 | tf_op jit(solution)/shard_map/ppermute | solution.py:70
  110.8 3.1 %collective-permute-done.9 = bf16[1024,128]{1,0:T(8,128)(2,1)S(1)} collective-permute-done((bf16[1024,128]{1,0:T(8,128)(2,1)S(1)}, bf16[1024,128]{1,0:T(8,128)(2,1)S(1)}, u32[]{:S(2)}, u32[]{:S(2)}) %collective-permute-start.9) | collective-permute-done | bytes 262176 | tf_op jit(solution)/shard_map/ppermute | solution.py:70
  113.9 0.2 add_convert_fusion.1
  114.1 0.7 pad_maximum_fusion.10
  114.8 4.8 %all-to-all-start.1 = ((bf16[16,32,256]{2,1,0:T(8,128)(2,1)}), bf16[16,32,256]{2,1,0:T(8,128)(2,1)S(1)}, u32[]{:S(2)}, u32[]{:S(2)}) async-start(bf16[16,32,256]{2,1,0:T(8,128)(2,1)} %pad_maximum_fusion.10), calls=%async_computation.1 | async-start | bytes 524288 | tf_op jit(solution)/shard_map/all_to_all | solution.py:150
  119.6 2.6 %fusion = bf16[1,2048,512]{2,1,0:T(8,128)(2,1)} fusion(bf16[512,512]{1,0:T(8,128)(2,1)S(1)} %fusion.19, bf16[512,1024]{1,0:T(8,128)(2,1)S(1)} %get-tuple-element.25, bf16[512,1024]{1,0:T(8,128)(2,1)S(1)} %get-tuple-element.18), kind=kOutput, calls=%fused_computation.17 | convolution fusion | flops 1078984704 | bytes 4718592 | tf_op jit(solution)/shard_map/dot_general | solution.py:39
  122.2 4.8 %all-to-all-done.1 = bf16[16,32,256]{2,1,0:T(8,128)(2,1)S(1)} async-done(((bf16[16,32,256]{2,1,0:T(8,128)(2,1)}), bf16[16,32,256]{2,1,0:T(8,128)(2,1)S(1)}, u32[]{:S(2)}, u32[]{:S(2)}) %all-to-all-start.1) | async-done | bytes 262176 | tf_op jit(solution)/shard_map/all_to_all | solution.py:150
  127.0 0.3 fusion.25
  127.4 0.3 fusion.26
  127.7 0.9 multiply_reduce_fusion
  128.6 0.8 reduce_sum.45
  (23 shorter events, 0.2 us)
Async XLA Ops:
  0.6 7.9 %copy-start = (bf16[128,2048]{1,0:T(8,128)(2,1)S(1)}, bf16[128,2048]{1,0:T(8,128)(2,1)}, u32[]{:S(2)}) copy-start(bf16[128,2048]{1,0:T(8,128)(2,1)} %param.6) | copy-start | bytes 1572868
  5.9 2.5 %copy-start.6 = (s32[128,2]{0,1:T(2,128)S(1)}, s32[128,2]{0,1:T(2,128)}, u32[]{:S(2)}) copy-start(s32[128,2]{0,1:T(2,128)} %param.7) | copy-start | bytes 3076
  45.2 12.4 %collective-permute-start = (bf16[512,2048]{1,0:T(8,128)(2,1)S(1)}, bf16[512,2048]{1,0:T(8,128)(2,1)}, u32[]{:S(2)}, u32[]{:S(2)}) collective-permute-start(bf16[512,2048]{1,0:T(8,128)(2,1)S(1)} %bitcast.59), channel_id=1, source_target_pairs={{0,16},{16,0},{1,17},{17,1},{2,18},{18,2},{3,19},{19,3},{4,20},{20... | collective-permute-start | bytes 6291464 | tf_op jit(solution)/shard_map/ppermute | solution.py:107
  52.2 2.4 %copy-start.1 = (bf16[1,2048,512]{2,1,0:T(8,128)(2,1)S(1)}, bf16[1,2048,512]{2,1,0:T(8,128)(2,1)}, u32[]{:S(2)}) copy-start(bf16[1,2048,512]{2,1,0:T(8,128)(2,1)} %param.10) | copy-start | bytes 6291460
  60.4 1.6 %copy-start.2 = (bf16[1,2048,512]{2,1,0:T(8,128)(2,1)S(1)}, bf16[1,2048,512]{2,1,0:T(8,128)(2,1)}, u32[]{:S(2)}) copy-start(bf16[1,2048,512]{2,1,0:T(8,128)(2,1)} %param.10) | copy-start | bytes 6291460
  62.0 1.6 %copy-start.5 = (bf16[512,2,8,128]{0,3,2,1:T(8,128)(2,1)S(1)}, bf16[512,2,8,128]{0,3,2,1:T(8,128)(2,1)}, u32[]{:S(2)}) copy-start(bf16[512,2,8,128]{0,3,2,1:T(8,128)(2,1)} %copy.47) | copy-start | bytes 6291460
  64.9 1.6 %copy-start.3 = (bf16[1,512,2048]{2,1,0:T(8,128)(2,1)S(1)}, bf16[1,512,2048]{2,1,0:T(8,128)(2,1)}, u32[]{:S(2)}) copy-start(bf16[1,512,2048]{2,1,0:T(8,128)(2,1)} %param.11) | copy-start | bytes 6291460
  66.5 1.6 %copy-start.4 = (bf16[2,8,128,512]{3,2,1,0:T(8,128)(2,1)S(1)}, bf16[2,8,128,512]{3,2,1,0:T(8,128)(2,1)}, u32[]{:S(2)}) copy-start(bf16[2,8,128,512]{3,2,1,0:T(8,128)(2,1)} %copy.48) | copy-start | bytes 6291460
  69.7 4.4 %collective-permute-start.1 = (bf16[1024,1024]{1,0:T(8,128)(2,1)S(1)}, bf16[1024,1024]{1,0:T(8,128)(2,1)S(1)}, u32[]{:S(2)}, u32[]{:S(2)}) collective-permute-start(bf16[1024,1024]{1,0:T(8,128)(2,1)S(1)} %pad_maximum_fusion.3), channel_id=1, source_target_pairs={{0,16},{16,0},{1,17},{17,1},{2,18},{18,2},{3,19},{19,3},{4,20},{20... | collective-permute-start | bytes 6291464 | tf_op jit(solution)/shard_map/ppermute | solution.py:54
  75.3 21.4 %collective-permute-start.4 = (bf16[1024,128]{1,0:T(8,128)(2,1)S(1)}, bf16[1024,128]{1,0:T(8,128)(2,1)S(1)}, u32[]{:S(2)}, u32[]{:S(2)}) collective-permute-start(bf16[1024,128]{1,0:T(8,128)(2,1)S(1)} %get-tuple-element.8), channel_id=1, source_target_pairs={{0,32},{32,64},{64,96},{96,128},{128,160},{160,192},{192,224},{224... | collective-permute-start | bytes 786440 | tf_op jit(solution)/shard_map/ppermute | solution.py:70
  77.4 19.3 %collective-permute-start.7 = (bf16[1024,128]{1,0:T(8,128)(2,1)S(1)}, bf16[1024,128]{1,0:T(8,128)(2,1)S(1)}, u32[]{:S(2)}, u32[]{:S(2)}) collective-permute-start(bf16[1024,128]{1,0:T(8,128)(2,1)S(1)} %get-tuple-element.7), channel_id=1, source_target_pairs={{0,224},{32,0},{64,32},{96,64},{128,96},{160,128},{192,160},{224,1... | collective-permute-start | bytes 786440 | tf_op jit(solution)/shard_map/ppermute | solution.py:70
  81.6 13.6 %collective-permute-start.5 = (bf16[512,128]{1,0:T(8,128)(2,1)S(1)}, bf16[512,128]{1,0:T(8,128)(2,1)S(1)}, u32[]{:S(2)}, u32[]{:S(2)}) collective-permute-start(bf16[512,128]{1,0:T(8,128)(2,1)S(1)} %get-tuple-element.12), channel_id=1, source_target_pairs={{0,64},{32,96},{64,128},{96,160},{128,192},{160,224},{192,0},{224,... | collective-permute-start | bytes 393224 | tf_op jit(solution)/shard_map/ppermute | solution.py:70
  81.7 15.0 %collective-permute-start.8 = (bf16[512,128]{1,0:T(8,128)(2,1)S(1)}, bf16[512,128]{1,0:T(8,128)(2,1)S(1)}, u32[]{:S(2)}, u32[]{:S(2)}) collective-permute-start(bf16[512,128]{1,0:T(8,128)(2,1)S(1)} %get-tuple-element.13), channel_id=1, source_target_pairs={{0,192},{32,224},{64,0},{96,32},{128,64},{160,96},{192,128},{224,1... | collective-permute-start | bytes 393224 | tf_op jit(solution)/shard_map/ppermute | solution.py:70
  85.9 17.9 %collective-permute-start.2 = (bf16[1024,128]{1,0:T(8,128)(2,1)S(1)}, bf16[1024,128]{1,0:T(8,128)(2,1)S(1)}, u32[]{:S(2)}, u32[]{:S(2)}) collective-permute-start(bf16[1024,128]{1,0:T(8,128)(2,1)S(1)} %get-tuple-element.6), channel_id=1, source_target_pairs={{0,32},{32,64},{64,96},{96,128},{128,160},{160,192},{192,224},{224... | collective-permute-start | bytes 786440 | tf_op jit(solution)/shard_map/ppermute | solution.py:70
  95.3 11.1 %collective-permute-start.3 = (bf16[1024,128]{1,0:T(8,128)(2,1)S(1)}, bf16[1024,128]{1,0:T(8,128)(2,1)S(1)}, u32[]{:S(2)}, u32[]{:S(2)}) collective-permute-start(bf16[1024,128]{1,0:T(8,128)(2,1)S(1)} %get-tuple-element.9), channel_id=1, source_target_pairs={{0,224},{32,0},{64,32},{96,64},{128,96},{160,128},{192,160},{224,1... | collective-permute-start | bytes 786440 | tf_op jit(solution)/shard_map/ppermute | solution.py:70
  96.9 13.9 %collective-permute-start.6 = (bf16[1024,128]{1,0:T(8,128)(2,1)S(1)}, bf16[1024,128]{1,0:T(8,128)(2,1)S(1)}, u32[]{:S(2)}, u32[]{:S(2)}) collective-permute-start(bf16[1024,128]{1,0:T(8,128)(2,1)S(1)} %get-tuple-element.10), channel_id=1, source_target_pairs={{0,64},{32,96},{64,128},{96,160},{128,192},{160,224},{192,0},{224,... | collective-permute-start | bytes 786440 | tf_op jit(solution)/shard_map/ppermute | solution.py:70
  99.1 14.8 %collective-permute-start.9 = (bf16[1024,128]{1,0:T(8,128)(2,1)S(1)}, bf16[1024,128]{1,0:T(8,128)(2,1)S(1)}, u32[]{:S(2)}, u32[]{:S(2)}) collective-permute-start(bf16[1024,128]{1,0:T(8,128)(2,1)S(1)} %get-tuple-element.11), channel_id=1, source_target_pairs={{0,192},{32,224},{64,0},{96,32},{128,64},{160,96},{192,128},{224,1... | collective-permute-start | bytes 786440 | tf_op jit(solution)/shard_map/ppermute | solution.py:70
  114.8 12.2 %all-to-all-start.1 = ((bf16[16,32,256]{2,1,0:T(8,128)(2,1)}), bf16[16,32,256]{2,1,0:T(8,128)(2,1)S(1)}, u32[]{:S(2)}, u32[]{:S(2)}) async-start(bf16[16,32,256]{2,1,0:T(8,128)(2,1)} %pad_maximum_fusion.10), calls=%async_computation.1 | async-start | bytes 524288 | tf_op jit(solution)/shard_map/all_to_all | solution.py:150

commit v3 on v2

--- a/solution.py
+++ b/solution.py
@@ -88,15 +88,10 @@
 
 def dispatch_rows(placements, sources, n_exp, capacity, n_core):
     core = lax.axis_index("core")
-    width = sources[0].shape[1]
-    share = width // n_core
+    share = sources[0].shape[1]
     sent = jnp.concatenate(
         [
-            jnp.dot(
-                placed_rows,
-                lax.dynamic_slice_in_dim(source, core * share, share, 1),
-                preferred_element_type=jnp.float32,
-            ).astype(jnp.bfloat16)
+            jnp.dot(placed_rows, source, preferred_element_type=jnp.float32).astype(jnp.bfloat16)
             for placed_rows, source in zip(placements, sources)
         ],
         axis=1,
@@ -132,38 +127,46 @@
     down_perm = down_blocks.transpose(0, 2, 1, 3).reshape(ff_local, width)
     up_blocks = jnp.roll(up_weight.reshape(n_z, n_core, cols, ff_local), (-zi, -core), (0, 1))
     up_perm = up_blocks.transpose(1, 0, 2, 3).reshape(width, ff_local)
-    grad_rows = (gate_values[:, :, None] * grad_out[:, None, :].astype(jnp.float32)).astype(
+    share = width // n_core
+    tok_half = lax.dynamic_slice_in_dim(tokens, core * share, share, 1)
+    grad_half = lax.dynamic_slice_in_dim(grad_out, core * share, share, 1)
+    grad_rows = (gate_values[:, :, None] * grad_half[:, None, :].astype(jnp.float32)).astype(
         jnp.bfloat16
     )
-    grad_rows = grad_rows.reshape(pair_count, width)
-    placed, counts = plan_slots(expert_ids, n_exp, capacity)
+    grad_rows = grad_rows.reshape(pair_count, share)
+    placed, _ = plan_slots(expert_ids, n_exp, capacity)
     summed = placed.reshape(n_exp * capacity, tok_count, top_k).sum(axis=2)
-    rows_in, rows_grad = dispatch_rows((summed, placed), (tokens, grad_rows), n_exp, capacity, n_core)
-    out_part, dx_part, grad_up_e, grad_down_e = expert_math(
-        rows_in, rows_grad, up_weight, down_weight, up_perm, down_perm
-    )
-    acc = reduce_over_rep(
-        (out_part.astype(jnp.bfloat16), dx_part.astype(jnp.bfloat16)), n_z, n_core, cols
-    )
-    slots = n_exp * capacity
-    both = jnp.concatenate([acc[:slots], acc[slots:]], axis=1).astype(jnp.bfloat16)
-    back_both = lax.all_to_all(
-        both.reshape(n_exp, capacity, 2 * cols), "exp", split_axis=0, concat_axis=0, tiled=True
-    ).reshape(n_exp * capacity, 2 * cols)
-    back_out = back_both[:, :cols]
-    back_dx = back_both[:, cols:]
-    pair_out = jnp.einsum(
-        "st,sd->td",
-        placed,
-        back_out,
-        preferred_element_type=jnp.float32,
-    )
-    pair_dx = jnp.einsum(
-        "st,sd->td",
-        placed,
-        back_dx,
-        preferred_element_type=jnp.float32,
-    )
+    n_chunks = 2 if capacity % 2 == 0 else 1
+    chunk_cap = capacity // n_chunks
+    slots = n_exp * chunk_cap
+    placed_blocks = placed.reshape(n_exp, capacity, pair_count)
+    summed_blocks = summed.reshape(n_exp, capacity, tok_count)
+    grad_up_e = grad_down_e = pair_out = pair_dx = 0.0
+    for c in range(n_chunks):
+        span = slice(c * chunk_cap, (c + 1) * chunk_cap)
+        placed_c = placed_blocks[:, span].reshape(slots, pair_count)
+        summed_c = summed_blocks[:, span].reshape(slots, tok_count)
+        rows_in, rows_grad = dispatch_rows(
+            (summed_c, placed_c), (tok_half, grad_rows), n_exp, chunk_cap, n_core
+        )
+        out_part, dx_part, grad_up_c, grad_down_c = expert_math(
+            rows_in, rows_grad, up_weight, down_weight, up_perm, down_perm
+        )
+        grad_up_e = grad_up_e + grad_up_c
+        grad_down_e = grad_down_e + grad_down_c
+        acc = reduce_over_rep(
+            (out_part.astype(jnp.bfloat16), dx_part.astype(jnp.bfloat16)), n_z, n_core, cols
+        )
+        both = jnp.concatenate([acc[:slots], acc[slots:]], axis=1).astype(jnp.bfloat16)
+        back_both = lax.all_to_all(
+            both.reshape(n_exp, chunk_cap, 2 * cols), "exp", split_axis=0, concat_axis=0, tiled=True
+        ).reshape(slots, 2 * cols)
+        pair_out = pair_out + jnp.einsum(
+            "st,sd->td", placed_c, back_both[:, :cols], preferred_element_type=jnp.float32
+        )
+        pair_dx = pair_dx + jnp.einsum(
+            "st,sd->td", placed_c, back_both[:, cols:], preferred_element_type=jnp.float32
+        )
     mixed = jnp.sum(gate_values[:, :, None] * pair_out.reshape(tok_count, top_k, cols), axis=1)
     grad_tokens = jnp.sum(pair_dx.reshape(tok_count, top_k, cols), axis=1)
     return (

time: 130 us -> 149 us (1.15)
  the two profiles are of different devices: /device:TPU:2 before, /device:TPU:32 now
where the time goes in v3:
time: 149 us; the launch traced here: 148 us
  waiting for transfers between devices  58.6 us (39%)
  starting transfers between devices  44.2 us (30%)
  other arithmetic  17.1 us (11%)
  matrix products  14.1 us (9%)
  local copies, waits for them, and re-layouts  12.8 us (9%)
    all_to_all x2, waiting for transfers between devices, dispatch_rows(): lax.all_to_all(sent.reshape(n_exp, capacity, sent.shape[1]), 'exp', split...  31.9 us
    ppermute x16, starting transfers between devices, shift(): lax.ppermute(x, 'z', [(j, (j + k) % n_z) for j in range(n_z)])  24.8 us
    all_to_all x2, waiting for transfers between devices, local(): lax.all_to_all(both.reshape(n_exp, chunk_cap, 2 * cols), 'exp', split_axi...  14.6 us
    ppermute x16, waiting for transfers between devices, shift(): lax.ppermute(x, 'z', [(j, (j + k) % n_z) for j in range(n_z)])  12.1 us
    all_to_all x2, starting transfers between devices, dispatch_rows(): lax.all_to_all(sent.reshape(n_exp, capacity, sent.shape[1]), 'exp', split...  11.4 us
    unnamed x15, local copies, waits for them, and re-layouts  9.31 us
    all_to_all x2, starting transfers between devices, local(): lax.all_to_all(both.reshape(n_exp, chunk_cap, 2 * cols), 'exp', split_axi...  7.02 us
    squeeze x1, other arithmetic, pick(): return lax.dynamic_index_in_dim(stacked, index, axis=axis, keepdims=False)  3.06 us
  transfers between devices with their start and end apart: 24, of which 7 were waited for; matrix products, arithmetic and copies ran while one was open for 14% of the time, Pallas kernels for 0%

profile of v3, /device:TPU:32, one launch (start us, length us, event | category | flops | bytes accessed | tf_op | source)
XLA Modules:
  0.0 147.9 jit_solution(4217234031197997145)
XLA Ops:
  0.7 0.8 copy.42
  1.8 0.6 reduce-window.6
  2.9 0.8 copy.41
  3.7 0.7 multiply_add_fusion.1
  4.7 1.0 dynamic-slice_convert_fusion
  5.7 0.4 multiply_convert_fusion
  6.6 0.3 convolution_convert_fusion.5
  7.0 1.1 pad_maximum_fusion
  8.0 7.1 %all-to-all-start = ((bf16[16,16,2048]{2,1,0:T(8,128)(2,1)}), bf16[16,16,2048]{2,1,0:T(8,128)(2,1)}, u32[]{:S(2)}, u32[]{:S(2)}) async-start(bf16[16,16,2048]{2,1,0:T(8,128)(2,1)} %bitcast.4), calls=%async_computation | async-start | bytes 2097152 | tf_op jit(solution)/shard_map/all_to_all | solution.py:99
  15.7 1.1 pad_maximum_fusion.4
  16.8 16.0 %all-to-all-done = bf16[16,16,2048]{2,1,0:T(8,128)(2,1)} async-done(((bf16[16,16,2048]{2,1,0:T(8,128)(2,1)}), bf16[16,16,2048]{2,1,0:T(8,128)(2,1)}, u32[]{:S(2)}, u32[]{:S(2)}) %all-to-all-start) | async-done | bytes 1048608 | tf_op jit(solution)/shard_map/all_to_all | solution.py:99
  32.8 4.3 %all-to-all-start.2 = ((bf16[16,16,2048]{2,1,0:T(8,128)(2,1)}), bf16[16,16,2048]{2,1,0:T(8,128)(2,1)}, u32[]{:S(2)}, u32[]{:S(2)}) async-start(bf16[16,16,2048]{2,1,0:T(8,128)(2,1)} %bitcast.23), calls=%async_computation.2 | async-start | bytes 2097152 | tf_op jit(solution)/shard_map/all_to_all | solution.py:99
  37.3 15.8 %all-to-all-done.2 = bf16[16,16,2048]{2,1,0:T(8,128)(2,1)} async-done(((bf16[16,16,2048]{2,1,0:T(8,128)(2,1)}), bf16[16,16,2048]{2,1,0:T(8,128)(2,1)}, u32[]{:S(2)}, u32[]{:S(2)}) %all-to-all-start.2) | async-done | bytes 1048608 | tf_op jit(solution)/shard_map/all_to_all | solution.py:99
  53.1 0.8 fusion.4
  53.9 0.8 fusion.3
  54.8 3.9 %copy.47 = bf16[1,512,2048]{1,2,0:T(8,128)(2,1)} copy(bf16[1,512,2048]{2,1,0:T(8,128)(2,1)} %param.11) | data formatting | bytes 4194304 | tf_op args[5]
  58.8 2.3 %fusion.7 = bf16[512,8,2,128]{0,3,2,1:T(8,128)(2,1)S(1)} fusion(s32[]{:T(128)S(6)} %select_n.52, bf16[512,8,2,128]{0,3,2,1:T(8,128)(2,1)} %bitcast.98), kind=kLoop, calls=%fused_computation.29 | loop fusion | flops 1048576 | bytes 4194308 | tf_op jit(solution)/shard_map/jit(_roll_dynamic)/concatenate | solution.py:126
  61.0 0.8 fusion.6
  61.8 1.5 %copy.48 = bf16[512,2,8,128]{0,3,2,1:T(8,128)(2,1)} copy(bf16[512,2,8,128]{0,3,1,2:T(8,128)(2,1)S(1)} %fusion.6) | data formatting | bytes 4194304 | tf_op jit(solution)/shard_map/transpose | solution.py:127
  63.3 3.1 %fusion.31 = (bf16[256,2048]{1,0:T(8,128)(2,1)S(1)}, bf16[256,2048]{1,0:T(8,128)(2,1)S(1)}, bf16[256,2048]{1,0:T(8,128)(2,1)S(1)}, bf16[256,2048]{1,0:T(8,128)(2,1)S(1)}) fusion(s32[]{:T(128)S(6)} %select_n.49, bf16[1,256,2048]{2,1,0:T(8,128)(2,1)} %bitcast.24, bf16[1,256,2048]{2,1,0:T(8,128)(2,1)} %bitcast.26, s32[]{:T(128)S(6)} %select_n.50, ...), kind=kLoop, calls=%fused_computation.53 | loop fusion | flops 2097152 | bytes 8388616 | tf_op jit(solution)/shard_map/jit(dynamic_index_in_dim)/squeeze | solution.py:49
  66.6 1.4 copy-done.3
  68.0 0.7 fusion.14
  68.7 0.9 copy-done.4
  69.6 0.9 fusion.25
  70.4 0.8 fusion.36
  71.4 1.4 copy-done.5
  72.8 0.7 convolution_convert_fusion.3
  73.6 0.7 fusion.12
  74.3 0.8 convolution_convert_fusion.1
  75.1 0.8 fusion.22
  75.9 0.8 convolution_convert_fusion
  76.6 0.8 convolution_convert_fusion.2
  77.8 0.6 collective-permute-start.1
  78.5 0.3 collective-permute-start.11
  78.8 0.8 fusion.37
  79.6 2.1 %fusion.1 = bf16[1,512,2048]{2,1,0:T(8,128)(2,1)} fusion(f32[512,2048]{1,0:T(8,128)S(1)} %fusion.36, bf16[256,1024]{1,0:T(8,128)(2,1)S(1)} %get-tuple-element.23, bf16[256,1024]{1,0:T(8,128)(2,1)S(1)} %get-tuple-element.21, f32[256,512]{1,0:T(8,128)S(1)} %fusion.12), kind=kOutput, calls=%fused_computation.11 | convolution fusion | flops 541720576 | bytes 7864320 | tf_op jit(solution)/shard_map/dot_general | solution.py:36
  81.7 2.1 %fusion = bf16[1,2048,512]{2,1,0:T(8,128)(2,1)} fusion(f32[2048,512]{1,0:T(8,128)S(1)} %fusion.37, bf16[256,512]{1,0:T(8,128)(2,1)S(1)} %fusion.22, bf16[256,1024]{1,0:T(8,128)(2,1)S(1)} %get-tuple-element.22, bf16[256,1024]{1,0:T(8,128)(2,1)S(1)} %get-tuple-element.20), kind=kOutput, calls=%fused_computation.10 | convolution fusion | flops 541065216 | bytes 7602176 | tf_op jit(solution)/shard_map/dot_general | solution.py:39
  83.8 0.4 add_convert_fusion.3
  84.2 3.4 %collective-permute-start.5 = (bf16[256,128]{1,0:T(8,128)(2,1)S(1)}, bf16[256,128]{1,0:T(8,128)(2,1)S(1)}, u32[]{:S(2)}, u32[]{:S(2)}) collective-permute-start(bf16[256,128]{1,0:T(8,128)(2,1)S(1)} %get-tuple-element.30), channel_id=1, source_target_pairs={{0,64},{32,96},{64,128},{96,160},{128,192},{160,224},{192,0},{224,... | collective-permute-start | bytes 196616 | tf_op jit(solution)/shard_map/ppermute | solution.py:70
  87.6 2.3 %collective-permute-start.8 = (bf16[256,128]{1,0:T(8,128)(2,1)S(1)}, bf16[256,128]{1,0:T(8,128)(2,1)S(1)}, u32[]{:S(2)}, u32[]{:S(2)}) collective-permute-start(bf16[256,128]{1,0:T(8,128)(2,1)S(1)} %get-tuple-element.31), channel_id=1, source_target_pairs={{0,192},{32,224},{64,0},{96,32},{128,64},{160,96},{192,128},{224,1... | collective-permute-start | bytes 196616 | tf_op jit(solution)/shard_map/ppermute | solution.py:70
  90.0 1.1 collective-permute-start.7
  91.1 1.0 collective-permute-start.4
  92.1 0.4 add_convert_fusion.2
  92.7 0.9 collective-permute-start.2
  93.6 0.4 collective-permute-done.5
  94.0 3.8 %collective-permute-start.15 = (bf16[256,128]{1,0:T(8,128)(2,1)S(1)}, bf16[256,128]{1,0:T(8,128)(2,1)S(1)}, u32[]{:S(2)}, u32[]{:S(2)}) collective-permute-start(bf16[256,128]{1,0:T(8,128)(2,1)S(1)} %get-tuple-element.14), channel_id=1, source_target_pairs={{0,64},{32,96},{64,128},{96,160},{128,192},{160,224},{192,0},{224,... | collective-permute-start | bytes 196616 | tf_op jit(solution)/shard_map/ppermute | solution.py:70
  97.8 0.4 collective-permute-start.18
  98.1 1.1 collective-permute-start.17
  99.2 0.9 collective-permute-start.14
  100.3 5.2 %collective-permute-done.15 = bf16[256,128]{1,0:T(8,128)(2,1)S(1)} collective-permute-done((bf16[256,128]{1,0:T(8,128)(2,1)S(1)}, bf16[256,128]{1,0:T(8,128)(2,1)S(1)}, u32[]{:S(2)}, u32[]{:S(2)}) %collective-permute-start.15) | collective-permute-done | bytes 65568 | tf_op jit(solution)/shard_map/ppermute | solution.py:70
  105.5 2.0 %collective-permute-start.12 = (bf16[512,128]{1,0:T(8,128)(2,1)S(1)}, bf16[512,128]{1,0:T(8,128)(2,1)S(1)}, u32[]{:S(2)}, u32[]{:S(2)}) collective-permute-start(bf16[512,128]{1,0:T(8,128)(2,1)S(1)} %get-tuple-element.8), channel_id=1, source_target_pairs={{0,32},{32,64},{64,96},{96,128},{128,160},{160,192},{192,224},{224... | collective-permute-start | bytes 393224 | tf_op jit(solution)/shard_map/ppermute | solution.py:70
  107.5 2.1 %collective-permute-start.6 = (bf16[512,128]{1,0:T(8,128)(2,1)S(1)}, bf16[512,128]{1,0:T(8,128)(2,1)S(1)}, u32[]{:S(2)}, u32[]{:S(2)}) collective-permute-start(bf16[512,128]{1,0:T(8,128)(2,1)S(1)} %get-tuple-element.28), channel_id=1, source_target_pairs={{0,64},{32,96},{64,128},{96,160},{128,192},{160,224},{192,0},{224,... | collective-permute-start | bytes 393224 | tf_op jit(solution)/shard_map/ppermute | solution.py:70
  109.6 2.0 %collective-permute-start.9 = (bf16[512,128]{1,0:T(8,128)(2,1)S(1)}, bf16[512,128]{1,0:T(8,128)(2,1)S(1)}, u32[]{:S(2)}, u32[]{:S(2)}) collective-permute-start(bf16[512,128]{1,0:T(8,128)(2,1)S(1)} %get-tuple-element.29), channel_id=1, source_target_pairs={{0,192},{32,224},{64,0},{96,32},{128,64},{160,96},{192,128},{224,1... | collective-permute-start | bytes 393224 | tf_op jit(solution)/shard_map/ppermute | solution.py:70
  111.8 1.0 collective-permute-start.13
  112.9 6.5 %collective-permute-done.6 = bf16[512,128]{1,0:T(8,128)(2,1)S(1)} collective-permute-done((bf16[512,128]{1,0:T(8,128)(2,1)S(1)}, bf16[512,128]{1,0:T(8,128)(2,1)S(1)}, u32[]{:S(2)}, u32[]{:S(2)}) %collective-permute-start.6) | collective-permute-done | bytes 131104 | tf_op jit(solution)/shard_map/ppermute | solution.py:70
  119.4 2.6 %collective-permute-start.19 = (bf16[512,128]{1,0:T(8,128)(2,1)S(1)}, bf16[512,128]{1,0:T(8,128)(2,1)S(1)}, u32[]{:S(2)}, u32[]{:S(2)}) collective-permute-start(bf16[512,128]{1,0:T(8,128)(2,1)S(1)} %get-tuple-element.13), channel_id=1, source_target_pairs={{0,192},{32,224},{64,0},{96,32},{128,64},{160,96},{192,128},{224,1... | collective-permute-start | bytes 393224 | tf_op jit(solution)/shard_map/ppermute | solution.py:70
  122.1 0.7 pad_maximum_fusion.16
  122.8 3.5 %all-to-all-start.1 = ((bf16[16,16,256]{2,1,0:T(8,128)(2,1)}), bf16[16,16,256]{2,1,0:T(8,128)(2,1)S(1)}, u32[]{:S(2)}, u32[]{:S(2)}) async-start(bf16[16,16,256]{2,1,0:T(8,128)(2,1)} %pad_maximum_fusion.16), calls=%async_computation.1 | async-start | bytes 262144 | tf_op jit(solution)/shard_map/all_to_all | solution.py:161
  126.5 0.7 pad_maximum_fusion.17
  127.2 7.1 %all-to-all-done.1 = bf16[16,16,256]{2,1,0:T(8,128)(2,1)S(1)} async-done(((bf16[16,16,256]{2,1,0:T(8,128)(2,1)}), bf16[16,16,256]{2,1,0:T(8,128)(2,1)S(1)}, u32[]{:S(2)}, u32[]{:S(2)}) %all-to-all-start.1) | async-done | bytes 131104 | tf_op jit(solution)/shard_map/all_to_all | solution.py:161
  134.3 3.5 %all-to-all-start.3 = ((bf16[16,16,256]{2,1,0:T(8,128)(2,1)}), bf16[16,16,256]{2,1,0:T(8,128)(2,1)S(1)}, u32[]{:S(2)}, u32[]{:S(2)}) async-start(bf16[16,16,256]{2,1,0:T(8,128)(2,1)} %pad_maximum_fusion.17), calls=%async_computation.3 | async-start | bytes 262144 | tf_op jit(solution)/shard_map/all_to_all | solution.py:161
  138.3 7.4 %all-to-all-done.3 = bf16[16,16,256]{2,1,0:T(8,128)(2,1)S(1)} async-done(((bf16[16,16,256]{2,1,0:T(8,128)(2,1)}), bf16[16,16,256]{2,1,0:T(8,128)(2,1)S(1)}, u32[]{:S(2)}, u32[]{:S(2)}) %all-to-all-start.3) | async-done | bytes 131104 | tf_op jit(solution)/shard_map/all_to_all | solution.py:161
  146.3 0.9 multiply_reduce_fusion
  147.1 0.8 reduce_sum.45
  (74 shorter events, 5.1 us)
Async XLA Ops:
  0.6 5.7 %copy-start = (bf16[128,2048]{1,0:T(8,128)(2,1)S(1)}, bf16[128,2048]{1,0:T(8,128)(2,1)}, u32[]{:S(2)}) copy-start(bf16[128,2048]{1,0:T(8,128)(2,1)} %param.6) | copy-start | bytes 1572868
  8.0 24.8 %all-to-all-start = ((bf16[16,16,2048]{2,1,0:T(8,128)(2,1)}), bf16[16,16,2048]{2,1,0:T(8,128)(2,1)}, u32[]{:S(2)}, u32[]{:S(2)}) async-start(bf16[16,16,2048]{2,1,0:T(8,128)(2,1)} %bitcast.4), calls=%async_computation | async-start | bytes 2097152 | tf_op jit(solution)/shard_map/all_to_all | solution.py:99
  15.7 37.4 %copy-start.2 = (bf16[1,2048,512]{2,1,0:T(8,128)(2,1)S(1)}, bf16[1,2048,512]{2,1,0:T(8,128)(2,1)}, u32[]{:S(2)}) copy-start(bf16[1,2048,512]{2,1,0:T(8,128)(2,1)} %param.10) | copy-start | bytes 6291460
  32.8 20.3 %all-to-all-start.2 = ((bf16[16,16,2048]{2,1,0:T(8,128)(2,1)}), bf16[16,16,2048]{2,1,0:T(8,128)(2,1)}, u32[]{:S(2)}, u32[]{:S(2)}) async-start(bf16[16,16,2048]{2,1,0:T(8,128)(2,1)} %bitcast.23), calls=%async_computation.2 | async-start | bytes 2097152 | tf_op jit(solution)/shard_map/all_to_all | solution.py:99
  37.2 26.1 %collective-permute-start = (bf16[256,2048]{1,0:T(8,128)(2,1)}, bf16[256,2048]{1,0:T(8,128)(2,1)}, u32[]{:S(2)}, u32[]{:S(2)}) collective-permute-start(bf16[256,2048]{1,0:T(8,128)(2,1)} %bitcast.6), channel_id=1, source_target_pairs={{0,16},{16,0},{1,17},{17,1},{2,18},{18,2},{3,19},{19,3},{4,20},{20... | collective-permute-start | bytes 3145736 | tf_op jit(solution)/shard_map/ppermute | solution.py:102
  53.1 10.2 %collective-permute-start.10 = (bf16[256,2048]{1,0:T(8,128)(2,1)}, bf16[256,2048]{1,0:T(8,128)(2,1)}, u32[]{:S(2)}, u32[]{:S(2)}) collective-permute-start(bf16[256,2048]{1,0:T(8,128)(2,1)} %bitcast.25), channel_id=1, source_target_pairs={{0,16},{16,0},{1,17},{17,1},{2,18},{18,2},{3,19},{19,3},{4,20},{20... | collective-permute-start | bytes 3145736 | tf_op jit(solution)/shard_map/ppermute | solution.py:102
  66.4 1.6 %copy-start.3 = (bf16[1,2048,512]{2,1,0:T(8,128)(2,1)S(1)}, bf16[1,2048,512]{2,1,0:T(8,128)(2,1)}, u32[]{:S(2)}) copy-start(bf16[1,2048,512]{2,1,0:T(8,128)(2,1)} %param.10) | copy-start | bytes 6291460
  68.0 1.6 %copy-start.4 = (bf16[1,512,2048]{2,1,0:T(8,128)(2,1)S(1)}, bf16[1,512,2048]{2,1,0:T(8,128)(2,1)}, u32[]{:S(2)}) copy-start(bf16[1,512,2048]{2,1,0:T(8,128)(2,1)} %param.11) | copy-start | bytes 6291460
  71.2 1.6 %copy-start.5 = (bf16[512,2,8,128]{0,3,2,1:T(8,128)(2,1)S(1)}, bf16[512,2,8,128]{0,3,2,1:T(8,128)(2,1)}, u32[]{:S(2)}) copy-start(bf16[512,2,8,128]{0,3,2,1:T(8,128)(2,1)} %copy.48) | copy-start | bytes 6291460
  77.8 5.9 %collective-permute-start.1 = (bf16[512,1024]{1,0:T(8,128)(2,1)S(1)}, bf16[512,1024]{1,0:T(8,128)(2,1)S(1)}, u32[]{:S(2)}, u32[]{:S(2)}) collective-permute-start(bf16[512,1024]{1,0:T(8,128)(2,1)S(1)} %pad_maximum_fusion.3), channel_id=1, source_target_pairs={{0,16},{16,0},{1,17},{17,1},{2,18},{18,2},{3,19},{19,3},{4,20},{20... | collective-permute-start | bytes 3145736 | tf_op jit(solution)/shard_map/ppermute | solution.py:54
  78.5 13.6 %collective-permute-start.11 = (bf16[512,1024]{1,0:T(8,128)(2,1)S(1)}, bf16[512,1024]{1,0:T(8,128)(2,1)S(1)}, u32[]{:S(2)}, u32[]{:S(2)}) collective-permute-start(bf16[512,1024]{1,0:T(8,128)(2,1)S(1)} %pad_maximum_fusion.7), channel_id=1, source_target_pairs={{0,16},{16,0},{1,17},{17,1},{2,18},{18,2},{3,19},{19,3},{4,20},{20... | collective-permute-start | bytes 3145736 | tf_op jit(solution)/shard_map/ppermute | solution.py:54
  84.2 9.7 %collective-permute-start.5 = (bf16[256,128]{1,0:T(8,128)(2,1)S(1)}, bf16[256,128]{1,0:T(8,128)(2,1)S(1)}, u32[]{:S(2)}, u32[]{:S(2)}) collective-permute-start(bf16[256,128]{1,0:T(8,128)(2,1)S(1)} %get-tuple-element.30), channel_id=1, source_target_pairs={{0,64},{32,96},{64,128},{96,160},{128,192},{160,224},{192,0},{224,... | collective-permute-start | bytes 196616 | tf_op jit(solution)/shard_map/ppermute | solution.py:70
  87.6 10.1 %collective-permute-start.8 = (bf16[256,128]{1,0:T(8,128)(2,1)S(1)}, bf16[256,128]{1,0:T(8,128)(2,1)S(1)}, u32[]{:S(2)}, u32[]{:S(2)}) collective-permute-start(bf16[256,128]{1,0:T(8,128)(2,1)S(1)} %get-tuple-element.31), channel_id=1, source_target_pairs={{0,192},{32,224},{64,0},{96,32},{128,64},{160,96},{192,128},{224,1... | collective-permute-start | bytes 196616 | tf_op jit(solution)/shard_map/ppermute | solution.py:70
  90.0 8.1 %collective-permute-start.7 = (bf16[512,128]{1,0:T(8,128)(2,1)S(1)}, bf16[512,128]{1,0:T(8,128)(2,1)S(1)}, u32[]{:S(2)}, u32[]{:S(2)}) collective-permute-start(bf16[512,128]{1,0:T(8,128)(2,1)S(1)} %get-tuple-element.25), channel_id=1, source_target_pairs={{0,224},{32,0},{64,32},{96,64},{128,96},{160,128},{192,160},{224,1... | collective-permute-start | bytes 393224 | tf_op jit(solution)/shard_map/ppermute | solution.py:70
  91.1 8.1 %collective-permute-start.4 = (bf16[512,128]{1,0:T(8,128)(2,1)S(1)}, bf16[512,128]{1,0:T(8,128)(2,1)S(1)}, u32[]{:S(2)}, u32[]{:S(2)}) collective-permute-start(bf16[512,128]{1,0:T(8,128)(2,1)S(1)} %get-tuple-element.26), channel_id=1, source_target_pairs={{0,32},{32,64},{64,96},{96,128},{128,160},{160,192},{192,224},{224... | collective-permute-start | bytes 393224 | tf_op jit(solution)/shard_map/ppermute | solution.py:70
  92.7 19.1 %collective-permute-start.2 = (bf16[512,128]{1,0:T(8,128)(2,1)S(1)}, bf16[512,128]{1,0:T(8,128)(2,1)S(1)}, u32[]{:S(2)}, u32[]{:S(2)}) collective-permute-start(bf16[512,128]{1,0:T(8,128)(2,1)S(1)} %get-tuple-element.24), channel_id=1, source_target_pairs={{0,32},{32,64},{64,96},{96,128},{128,160},{160,192},{192,224},{224... | collective-permute-start | bytes 393224 | tf_op jit(solution)/shard_map/ppermute | solution.py:70
  94.0 11.5 %collective-permute-start.15 = (bf16[256,128]{1,0:T(8,128)(2,1)S(1)}, bf16[256,128]{1,0:T(8,128)(2,1)S(1)}, u32[]{:S(2)}, u32[]{:S(2)}) collective-permute-start(bf16[256,128]{1,0:T(8,128)(2,1)S(1)} %get-tuple-element.14), channel_id=1, source_target_pairs={{0,64},{32,96},{64,128},{96,160},{128,192},{160,224},{192,0},{224,... | collective-permute-start | bytes 196616 | tf_op jit(solution)/shard_map/ppermute | solution.py:70
  97.8 7.7 %collective-permute-start.18 = (bf16[256,128]{1,0:T(8,128)(2,1)S(1)}, bf16[256,128]{1,0:T(8,128)(2,1)S(1)}, u32[]{:S(2)}, u32[]{:S(2)}) collective-permute-start(bf16[256,128]{1,0:T(8,128)(2,1)S(1)} %get-tuple-element.15), channel_id=1, source_target_pairs={{0,192},{32,224},{64,0},{96,32},{128,64},{160,96},{192,128},{224,1... | collective-permute-start | bytes 196616 | tf_op jit(solution)/shard_map/ppermute | solution.py:70
  98.1 9.4 %collective-permute-start.17 = (bf16[512,128]{1,0:T(8,128)(2,1)S(1)}, bf16[512,128]{1,0:T(8,128)(2,1)S(1)}, u32[]{:S(2)}, u32[]{:S(2)}) collective-permute-start(bf16[512,128]{1,0:T(8,128)(2,1)S(1)} %get-tuple-element.9), channel_id=1, source_target_pairs={{0,224},{32,0},{64,32},{96,64},{128,96},{160,128},{192,160},{224,1... | collective-permute-start | bytes 393224 | tf_op jit(solution)/shard_map/ppermute | solution.py:70
  99.2 10.4 %collective-permute-start.14 = (bf16[512,128]{1,0:T(8,128)(2,1)S(1)}, bf16[512,128]{1,0:T(8,128)(2,1)S(1)}, u32[]{:S(2)}, u32[]{:S(2)}) collective-permute-start(bf16[512,128]{1,0:T(8,128)(2,1)S(1)} %get-tuple-element.10), channel_id=1, source_target_pairs={{0,32},{32,64},{64,96},{96,128},{128,160},{160,192},{192,224},{224... | collective-permute-start | bytes 393224 | tf_op jit(solution)/shard_map/ppermute | solution.py:70
  105.5 7.3 %collective-permute-start.3 = (bf16[512,128]{1,0:T(8,128)(2,1)S(1)}, bf16[512,128]{1,0:T(8,128)(2,1)S(1)}, u32[]{:S(2)}, u32[]{:S(2)}) collective-permute-start(bf16[512,128]{1,0:T(8,128)(2,1)S(1)} %get-tuple-element.27), channel_id=1, source_target_pairs={{0,224},{32,0},{64,32},{96,64},{128,96},{160,128},{192,160},{224,1... | collective-permute-start | bytes 393224 | tf_op jit(solution)/shard_map/ppermute | solution.py:70
  105.5 20.8 %collective-permute-start.12 = (bf16[512,128]{1,0:T(8,128)(2,1)S(1)}, bf16[512,128]{1,0:T(8,128)(2,1)S(1)}, u32[]{:S(2)}, u32[]{:S(2)}) collective-permute-start(bf16[512,128]{1,0:T(8,128)(2,1)S(1)} %get-tuple-element.8), channel_id=1, source_target_pairs={{0,32},{32,64},{64,96},{96,128},{128,160},{160,192},{192,224},{224... | collective-permute-start | bytes 393224 | tf_op jit(solution)/shard_map/ppermute | solution.py:70
  107.5 11.9 %collective-permute-start.6 = (bf16[512,128]{1,0:T(8,128)(2,1)S(1)}, bf16[512,128]{1,0:T(8,128)(2,1)S(1)}, u32[]{:S(2)}, u32[]{:S(2)}) collective-permute-start(bf16[512,128]{1,0:T(8,128)(2,1)S(1)} %get-tuple-element.28), channel_id=1, source_target_pairs={{0,64},{32,96},{64,128},{96,160},{128,192},{160,224},{192,0},{224,... | collective-permute-start | bytes 393224 | tf_op jit(solution)/shard_map/ppermute | solution.py:70
  109.6 12.4 %collective-permute-start.9 = (bf16[512,128]{1,0:T(8,128)(2,1)S(1)}, bf16[512,128]{1,0:T(8,128)(2,1)S(1)}, u32[]{:S(2)}, u32[]{:S(2)}) collective-permute-start(bf16[512,128]{1,0:T(8,128)(2,1)S(1)} %get-tuple-element.29), channel_id=1, source_target_pairs={{0,192},{32,224},{64,0},{96,32},{128,64},{160,96},{192,128},{224,1... | collective-permute-start | bytes 393224 | tf_op jit(solution)/shard_map/ppermute | solution.py:70
  111.8 14.6 %collective-permute-start.13 = (bf16[512,128]{1,0:T(8,128)(2,1)S(1)}, bf16[512,128]{1,0:T(8,128)(2,1)S(1)}, u32[]{:S(2)}, u32[]{:S(2)}) collective-permute-start(bf16[512,128]{1,0:T(8,128)(2,1)S(1)} %get-tuple-element.11), channel_id=1, source_target_pairs={{0,224},{32,0},{64,32},{96,64},{128,96},{160,128},{192,160},{224,1... | collective-permute-start | bytes 393224 | tf_op jit(solution)/shard_map/ppermute | solution.py:70
  112.8 13.6 %collective-permute-start.16 = (bf16[512,128]{1,0:T(8,128)(2,1)S(1)}, bf16[512,128]{1,0:T(8,128)(2,1)S(1)}, u32[]{:S(2)}, u32[]{:S(2)}) collective-permute-start(bf16[512,128]{1,0:T(8,128)(2,1)S(1)} %get-tuple-element.12), channel_id=1, source_target_pairs={{0,64},{32,96},{64,128},{96,160},{128,192},{160,224},{192,0},{224,... | collective-permute-start | bytes 393224 | tf_op jit(solution)/shard_map/ppermute | solution.py:70
  119.4 6.9 %collective-permute-start.19 = (bf16[512,128]{1,0:T(8,128)(2,1)S(1)}, bf16[512,128]{1,0:T(8,128)(2,1)S(1)}, u32[]{:S(2)}, u32[]{:S(2)}) collective-permute-start(bf16[512,128]{1,0:T(8,128)(2,1)S(1)} %get-tuple-element.13), channel_id=1, source_target_pairs={{0,192},{32,224},{64,0},{96,32},{128,64},{160,96},{192,128},{224,1... | collective-permute-start | bytes 393224 | tf_op jit(solution)/shard_map/ppermute | solution.py:70
  122.0 25.9 %copy-start.1 = (bf16[128,2048]{1,0:T(8,128)(2,1)S(1)}, bf16[128,2048]{1,0:T(8,128)(2,1)}, u32[]{:S(2)}) copy-start(bf16[128,2048]{1,0:T(8,128)(2,1)} %param.6) | copy-start | bytes 1572868
  122.8 11.5 %all-to-all-start.1 = ((bf16[16,16,256]{2,1,0:T(8,128)(2,1)}), bf16[16,16,256]{2,1,0:T(8,128)(2,1)S(1)}, u32[]{:S(2)}, u32[]{:S(2)}) async-start(bf16[16,16,256]{2,1,0:T(8,128)(2,1)} %pad_maximum_fusion.16), calls=%async_computation.1 | async-start | bytes 262144 | tf_op jit(solution)/shard_map/all_to_all | solution.py:161
  134.3 11.5 %all-to-all-start.3 = ((bf16[16,16,256]{2,1,0:T(8,128)(2,1)}), bf16[16,16,256]{2,1,0:T(8,128)(2,1)S(1)}, u32[]{:S(2)}, u32[]{:S(2)}) async-start(bf16[16,16,256]{2,1,0:T(8,128)(2,1)} %pad_maximum_fusion.17), calls=%async_computation.3 | async-start | bytes 262144 | tf_op jit(solution)/shard_map/all_to_all | solution.py:161

commit v4 on v2

--- a/solution.py
+++ b/solution.py
@@ -88,15 +88,10 @@
 
 def dispatch_rows(placements, sources, n_exp, capacity, n_core):
     core = lax.axis_index("core")
-    width = sources[0].shape[1]
-    share = width // n_core
+    share = sources[0].shape[1]
     sent = jnp.concatenate(
         [
-            jnp.dot(
-                placed_rows,
-                lax.dynamic_slice_in_dim(source, core * share, share, 1),
-                preferred_element_type=jnp.float32,
-            ).astype(jnp.bfloat16)
+            jnp.dot(placed_rows, source, preferred_element_type=jnp.float32).astype(jnp.bfloat16)
             for placed_rows, source in zip(placements, sources)
         ],
         axis=1,
@@ -132,13 +127,16 @@
     down_perm = down_blocks.transpose(0, 2, 1, 3).reshape(ff_local, width)
     up_blocks = jnp.roll(up_weight.reshape(n_z, n_core, cols, ff_local), (-zi, -core), (0, 1))
     up_perm = up_blocks.transpose(1, 0, 2, 3).reshape(width, ff_local)
-    grad_rows = (gate_values[:, :, None] * grad_out[:, None, :].astype(jnp.float32)).astype(
+    share = width // n_core
+    tok_half = lax.dynamic_slice_in_dim(tokens, core * share, share, 1)
+    grad_half = lax.dynamic_slice_in_dim(grad_out, core * share, share, 1)
+    grad_rows = (gate_values[:, :, None] * grad_half[:, None, :].astype(jnp.float32)).astype(
         jnp.bfloat16
     )
-    grad_rows = grad_rows.reshape(pair_count, width)
-    placed, counts = plan_slots(expert_ids, n_exp, capacity)
+    grad_rows = grad_rows.reshape(pair_count, share)
+    placed, _ = plan_slots(expert_ids, n_exp, capacity)
     summed = placed.reshape(n_exp * capacity, tok_count, top_k).sum(axis=2)
-    rows_in, rows_grad = dispatch_rows((summed, placed), (tokens, grad_rows), n_exp, capacity, n_core)
+    rows_in, rows_grad = dispatch_rows((summed, placed), (tok_half, grad_rows), n_exp, capacity, n_core)
     out_part, dx_part, grad_up_e, grad_down_e = expert_math(
         rows_in, rows_grad, up_weight, down_weight, up_perm, down_perm
     )

time: 130 us -> 126 us (0.969)
  local copies, waits for them, and re-layouts: 18.9 us -> 14.7 us
  matrix products: 13.4 us -> 12.1 us
    mul x3, local copies, waits for them, and re-layouts: 4.67 us -> 1.22 us  [local(): gate_values[:, :, None] * grad_half[:, None, :].astype(jnp.float32)]
    unnamed x17 -> x19, local copies, waits for them, and re-layouts: 9.26 us -> 8.6 us
  transfers between devices with their start and end apart: 11 -> 11, of which waited for: 6 -> 6; matrix products, arithmetic and copies ran while one was open for 13% -> 14% of each run, Pallas kernels for 0% -> 0%
where the time goes in v4:
time: 126 us; the launch traced here: 125 us
  blocking collectives  34.3 us (27%)
  waiting for transfers between devices  28.2 us (22%)
  starting transfers between devices  21.5 us (17%)
  local copies, waits for them, and re-layouts  14.7 us (12%)
  other arithmetic  13.3 us (11%)
  matrix products  12.1 us (10%)
    all_to_all x1, blocking collectives, dispatch_rows(): lax.all_to_all(sent.reshape(n_exp, capacity, sent.shape[1]), 'exp', split...  34.3 us
    ppermute x8, waiting for transfers between devices, shift(): lax.ppermute(x, 'z', [(j, (j + k) % n_z) for j in range(n_z)])  19.6 us
    ppermute x8, starting transfers between devices, shift(): lax.ppermute(x, 'z', [(j, (j + k) % n_z) for j in range(n_z)])  16.1 us
    unnamed x19, local copies, waits for them, and re-layouts  8.6 us
    all_to_all x1, waiting for transfers between devices, local(): lax.all_to_all(both.reshape(n_exp, capacity, 2 * cols), 'exp', split_axis...  4.79 us
    all_to_all x1, starting transfers between devices, local(): lax.all_to_all(both.reshape(n_exp, capacity, 2 * cols), 'exp', split_axis...  4.78 us
    ppermute x1, waiting for transfers between devices, reduce_over_rep(): lax.ppermute(jnp.concatenate([p[:, share:] for p in parts], axis=0), 'cor...  3.79 us
    squeeze x1, other arithmetic, pick(): return lax.dynamic_index_in_dim(stacked, index, axis=axis, keepdims=False)  2.75 us
  transfers between devices with their start and end apart: 11, of which 6 were waited for; matrix products, arithmetic and copies ran while one was open for 14% of the time, Pallas kernels for 0%

profile of v4, /device:TPU:2, one launch (start us, length us, event | category | flops | bytes accessed | tf_op | source)
XLA Modules:
  0.0 125.0 jit_solution(10576730675597665639)
XLA Ops:
  0.6 0.8 copy.41
  1.5 0.1 eq.55
  1.6 0.1 reshape.78
  1.8 0.6 reduce-window.6
  2.4 0.2 slice_reduce_fusion
  2.6 0.1 fusion.35
  2.7 0.1 reduce_sum.42
  2.9 1.0 dynamic-slice_convert_fusion
  3.9 0.4 mul.69
  4.3 0.7 mul.70
  5.0 0.1 copy.40
  5.1 0.1 mul.67
  5.3 0.1 fusion.26
  5.4 0.4 convolution_convert_fusion.4
  5.9 0.5 convolution_convert_fusion.5
  6.4 0.2 pad_maximum_fusion
  6.6 34.3 %all_to_all.10 = bf16[16,32,2048]{2,1,0:T(8,128)(2,1)S(1)} all-to-all(bf16[16,32,2048]{2,1,0:T(8,128)(2,1)S(1)} %bitcast.62), channel_id=1, replica_groups=mesh['z'=8,'core'=2,'exp'=16] {'exp'}, dimensions={0} | all-to-all | bytes 4194304 | tf_op jit(solution)/shard_map/all_to_all | solution.py:99
  40.9 3.9 %copy.46 = bf16[1,512,2048]{1,2,0:T(8,128)(2,1)} copy(bf16[1,512,2048]{2,1,0:T(8,128)(2,1)} %param.11) | data formatting | bytes 4194304 | tf_op args[5]
  44.8 2.3 %fusion.7 = bf16[512,8,2,128]{0,3,2,1:T(8,128)(2,1)S(1)} fusion(s32[]{:T(128)S(6)} %select_n.50, bf16[512,8,2,128]{0,3,2,1:T(8,128)(2,1)} %bitcast.61), kind=kLoop, calls=%fused_computation.24 | loop fusion | flops 1048576 | bytes 4194308 | tf_op jit(solution)/shard_map/jit(_roll_dynamic)/concatenate | solution.py:126
  47.1 0.8 fusion.6
  47.9 1.5 %copy.47 = bf16[512,2,8,128]{0,3,2,1:T(8,128)(2,1)} copy(bf16[512,2,8,128]{0,3,1,2:T(8,128)(2,1)S(1)} %fusion.6) | data formatting | bytes 4194304 | tf_op jit(solution)/shard_map/transpose | solution.py:127
  49.4 0.8 copy-done.1
  50.3 0.8 fusion.4
  51.0 0.8 fusion.3
  51.8 1.5 %copy.48 = bf16[2,8,128,512]{3,2,1,0:T(8,128)(2,1)} copy(bf16[2,8,128,512]{3,2,0,1:T(8,128)(2,1)S(1)} %fusion.3) | data formatting | bytes 4194304 | tf_op jit(solution)/shard_map/transpose | solution.py:129
  53.3 2.8 %fusion.11 = (bf16[512,2048]{1,0:T(8,128)(2,1)S(1)}, bf16[512,2048]{1,0:T(8,128)(2,1)S(1)}) fusion(s32[]{:T(128)S(6)} %select_n.47, bf16[1,512,2048]{2,1,0:T(8,128)(2,1)S(1)} %bitcast.60, bf16[1,512,2048]{2,1,0:T(8,128)(2,1)} %bitcast.4, s32[]{:T(128)S(6)} %select_n.48), kind=kLoop, calls=%fused_computation.28 | loop fusion | flops 2097152 | bytes 8388616 | tf_op jit(solution)/shard_map/jit(dynamic_index_in_dim)/squeeze | solution.py:49
  56.1 0.6 fusion.46
  56.7 1.0 copy-done.2
  57.7 1.2 fusion.14
  58.9 0.3 copy-done.5
  59.3 1.3 %convolution_convert_fusion.3 = bf16[512,2048]{1,0:T(8,128)(2,1)S(1)} fusion(bf16[512,2048]{0,1:T(8,128)(2,1)S(1)} %bitcast.65, f32[512,512]{1,0:T(8,128)S(1)} %fusion.14), kind=kOutput, calls=%fused_computation.16 | convolution fusion | flops 1076101120 | bytes 5242880 | tf_op jit(solution)/shard_map/dot_general | solution.py:24
  60.6 0.2 fusion.44
  60.8 1.4 %copy-done.3 = bf16[1,512,2048]{2,1,0:T(8,128)(2,1)S(1)} copy-done((bf16[1,512,2048]{2,1,0:T(8,128)(2,1)S(1)}, bf16[1,512,2048]{2,1,0:T(8,128)(2,1)}, u32[]{:S(2)}) %copy-start.3) | copy-done | bytes 2097176
  62.2 1.4 %fusion.19 = bf16[512,512]{1,0:T(8,128)(2,1)S(1)} fusion(bf16[1,512,2048]{2,1,0:T(8,128)(2,1)S(1)} %copy-done.3, bf16[512,1024]{1,0:T(8,128)(2,1)S(1)} %get-tuple-element.24, bf16[512,1024]{1,0:T(8,128)(2,1)S(1)} %get-tuple-element.19, f32[512,512]{1,0:T(8,128)S(1)} %fusion.14), kind=kOutput, calls=%fused_computation.40 | convolution fusion | flops 1080295424 | bytes 5767168 | tf_op jit(solution)/shard_map/dot_general | solution.py:25
  63.6 0.1 copy-done.4
  63.8 1.3 %convolution_convert_fusion.2 = bf16[512,2048]{1,0:T(8,128)(2,1)S(1)} fusion(bf16[512,512]{1,0:T(8,128)(2,1)S(1)} %fusion.19, bf16[2048,512]{1,0:T(8,128)(2,1)S(1)} %bitcast.64), kind=kOutput, calls=%fused_computation.15 | convolution fusion | flops 1074790400 | bytes 4718592 | tf_op jit(solution)/shard_map/dot_general | solution.py:30
  65.1 0.2 fusion.45
  65.2 0.2 pad_maximum_fusion.3
  65.4 0.6 collective-permute-start.1
  66.0 3.8 %collective-permute-done.1 = bf16[1024,1024]{1,0:T(8,128)(2,1)S(1)} collective-permute-done((bf16[1024,1024]{1,0:T(8,128)(2,1)S(1)}, bf16[1024,1024]{1,0:T(8,128)(2,1)S(1)}, u32[]{:S(2)}, u32[]{:S(2)}) %collective-permute-start.1) | collective-permute-done | bytes 2097184 | tf_op jit(solution)/shard_map/ppermute | solution.py:54
  69.8 1.0 add_convert_fusion
  70.8 0.2 fusion.42
  71.0 2.1 %collective-permute-start.4 = (bf16[1024,128]{1,0:T(8,128)(2,1)S(1)}, bf16[1024,128]{1,0:T(8,128)(2,1)S(1)}, u32[]{:S(2)}, u32[]{:S(2)}) collective-permute-start(bf16[1024,128]{1,0:T(8,128)(2,1)S(1)} %get-tuple-element.8), channel_id=1, source_target_pairs={{0,32},{32,64},{64,96},{96,128},{128,160},{160,192},{192,224},{224... | collective-permute-start | bytes 786440 | tf_op jit(solution)/shard_map/ppermute | solution.py:70
  73.1 4.1 %collective-permute-start.7 = (bf16[1024,128]{1,0:T(8,128)(2,1)S(1)}, bf16[1024,128]{1,0:T(8,128)(2,1)S(1)}, u32[]{:S(2)}, u32[]{:S(2)}) collective-permute-start(bf16[1024,128]{1,0:T(8,128)(2,1)S(1)} %get-tuple-element.7), channel_id=1, source_target_pairs={{0,224},{32,0},{64,32},{96,64},{128,96},{160,128},{192,160},{224,1... | collective-permute-start | bytes 786440 | tf_op jit(solution)/shard_map/ppermute | solution.py:70
  77.3 0.1 collective-permute-start.5
  77.4 4.1 %collective-permute-start.8 = (bf16[512,128]{1,0:T(8,128)(2,1)S(1)}, bf16[512,128]{1,0:T(8,128)(2,1)S(1)}, u32[]{:S(2)}, u32[]{:S(2)}) collective-permute-start(bf16[512,128]{1,0:T(8,128)(2,1)S(1)} %get-tuple-element.13), channel_id=1, source_target_pairs={{0,192},{32,224},{64,0},{96,32},{128,64},{160,96},{192,128},{224,1... | collective-permute-start | bytes 393224 | tf_op jit(solution)/shard_map/ppermute | solution.py:70
  81.5 9.4 %collective-permute-done.5 = bf16[512,128]{1,0:T(8,128)(2,1)S(1)} collective-permute-done((bf16[512,128]{1,0:T(8,128)(2,1)S(1)}, bf16[512,128]{1,0:T(8,128)(2,1)S(1)}, u32[]{:S(2)}, u32[]{:S(2)}) %collective-permute-start.5) | collective-permute-done | bytes 131104 | tf_op jit(solution)/shard_map/ppermute | solution.py:70
  91.0 1.4 %collective-permute-start.3 = (bf16[1024,128]{1,0:T(8,128)(2,1)S(1)}, bf16[1024,128]{1,0:T(8,128)(2,1)S(1)}, u32[]{:S(2)}, u32[]{:S(2)}) collective-permute-start(bf16[1024,128]{1,0:T(8,128)(2,1)S(1)} %get-tuple-element.9), channel_id=1, source_target_pairs={{0,224},{32,0},{64,32},{96,64},{128,96},{160,128},{192,160},{224,1... | collective-permute-start | bytes 786440 | tf_op jit(solution)/shard_map/ppermute | solution.py:70
  92.4 0.2 add_convert_fusion.3
  92.6 2.2 %collective-permute-start.6 = (bf16[1024,128]{1,0:T(8,128)(2,1)S(1)}, bf16[1024,128]{1,0:T(8,128)(2,1)S(1)}, u32[]{:S(2)}, u32[]{:S(2)}) collective-permute-start(bf16[1024,128]{1,0:T(8,128)(2,1)S(1)} %get-tuple-element.10), channel_id=1, source_target_pairs={{0,64},{32,96},{64,128},{96,160},{128,192},{160,224},{192,0},{224,... | collective-permute-start | bytes 786440 | tf_op jit(solution)/shard_map/ppermute | solution.py:70
  94.8 2.0 %collective-permute-start.9 = (bf16[1024,128]{1,0:T(8,128)(2,1)S(1)}, bf16[1024,128]{1,0:T(8,128)(2,1)S(1)}, u32[]{:S(2)}, u32[]{:S(2)}) collective-permute-start(bf16[1024,128]{1,0:T(8,128)(2,1)S(1)} %get-tuple-element.11), channel_id=1, source_target_pairs={{0,192},{32,224},{64,0},{96,32},{128,64},{160,96},{192,128},{224,1... | collective-permute-start | bytes 786440 | tf_op jit(solution)/shard_map/ppermute | solution.py:70
  96.8 2.7 %fusion.1 = bf16[1,512,2048]{2,1,0:T(8,128)(2,1)} fusion(bf16[512,1024]{1,0:T(8,128)(2,1)S(1)} %get-tuple-element.24, bf16[512,1024]{1,0:T(8,128)(2,1)S(1)} %get-tuple-element.19, f32[512,512]{1,0:T(8,128)S(1)} %fusion.14), kind=kOutput, calls=%fused_computation.18 | convolution fusion | flops 1080295424 | bytes 5242880 | tf_op jit(solution)/shard_map/dot_general | solution.py:36
  99.5 2.6 %collective-permute-done.3 = bf16[1024,128]{1,0:T(8,128)(2,1)S(1)} collective-permute-done((bf16[1024,128]{1,0:T(8,128)(2,1)S(1)}, bf16[1024,128]{1,0:T(8,128)(2,1)S(1)}, u32[]{:S(2)}, u32[]{:S(2)}) %collective-permute-start.3) | collective-permute-done | bytes 262176 | tf_op jit(solution)/shard_map/ppermute | solution.py:70
  102.0 4.5 %collective-permute-done.6 = bf16[1024,128]{1,0:T(8,128)(2,1)S(1)} collective-permute-done((bf16[1024,128]{1,0:T(8,128)(2,1)S(1)}, bf16[1024,128]{1,0:T(8,128)(2,1)S(1)}, u32[]{:S(2)}, u32[]{:S(2)}) %collective-permute-start.6) | collective-permute-done | bytes 262176 | tf_op jit(solution)/shard_map/ppermute | solution.py:70
  106.5 3.1 %collective-permute-done.9 = bf16[1024,128]{1,0:T(8,128)(2,1)S(1)} collective-permute-done((bf16[1024,128]{1,0:T(8,128)(2,1)S(1)}, bf16[1024,128]{1,0:T(8,128)(2,1)S(1)}, u32[]{:S(2)}, u32[]{:S(2)}) %collective-permute-start.9) | collective-permute-done | bytes 262176 | tf_op jit(solution)/shard_map/ppermute | solution.py:70
  109.6 0.2 add_convert_fusion.1
  109.8 0.7 pad_maximum_fusion.10
  110.5 4.8 %all-to-all-start.1 = ((bf16[16,32,256]{2,1,0:T(8,128)(2,1)}), bf16[16,32,256]{2,1,0:T(8,128)(2,1)S(1)}, u32[]{:S(2)}, u32[]{:S(2)}) async-start(bf16[16,32,256]{2,1,0:T(8,128)(2,1)} %pad_maximum_fusion.10), calls=%async_computation.1 | async-start | bytes 524288 | tf_op jit(solution)/shard_map/all_to_all | solution.py:148
  115.3 2.6 %fusion = bf16[1,2048,512]{2,1,0:T(8,128)(2,1)} fusion(bf16[512,512]{1,0:T(8,128)(2,1)S(1)} %fusion.19, bf16[512,1024]{1,0:T(8,128)(2,1)S(1)} %get-tuple-element.25, bf16[512,1024]{1,0:T(8,128)(2,1)S(1)} %get-tuple-element.18), kind=kOutput, calls=%fused_computation.17 | convolution fusion | flops 1078984704 | bytes 4718592 | tf_op jit(solution)/shard_map/dot_general | solution.py:39
  117.9 4.8 %all-to-all-done.1 = bf16[16,32,256]{2,1,0:T(8,128)(2,1)S(1)} async-done(((bf16[16,32,256]{2,1,0:T(8,128)(2,1)}), bf16[16,32,256]{2,1,0:T(8,128)(2,1)S(1)}, u32[]{:S(2)}, u32[]{:S(2)}) %all-to-all-start.1) | async-done | bytes 262176 | tf_op jit(solution)/shard_map/all_to_all | solution.py:148
  122.7 0.3 fusion.23
  123.1 0.3 fusion.24
  123.4 0.9 multiply_reduce_fusion
  124.2 0.8 reduce_sum.45
  (26 shorter events, 0.3 us)
Async XLA Ops:
  0.6 4.8 %copy-start = (bf16[128,2048]{1,0:T(8,128)(2,1)S(1)}, bf16[128,2048]{1,0:T(8,128)(2,1)}, u32[]{:S(2)}) copy-start(bf16[128,2048]{1,0:T(8,128)(2,1)} %param.6) | copy-start | bytes 1572868
  2.9 2.1 %copy-start.7 = (f32[128,2]{0,1:T(2,128)S(1)}, f32[128,2]{0,1:T(2,128)}, u32[]{:S(2)}) copy-start(f32[128,2]{0,1:T(2,128)} %param.8) | copy-start | bytes 3076
  3.9 1.4 %copy-start.6 = (s32[128,2]{0,1:T(2,128)S(1)}, s32[128,2]{0,1:T(2,128)}, u32[]{:S(2)}) copy-start(s32[128,2]{0,1:T(2,128)} %param.7) | copy-start | bytes 3076
  40.9 12.4 %collective-permute-start = (bf16[512,2048]{1,0:T(8,128)(2,1)S(1)}, bf16[512,2048]{1,0:T(8,128)(2,1)}, u32[]{:S(2)}, u32[]{:S(2)}) collective-permute-start(bf16[512,2048]{1,0:T(8,128)(2,1)S(1)} %bitcast.59), channel_id=1, source_target_pairs={{0,16},{16,0},{1,17},{17,1},{2,18},{18,2},{3,19},{19,3},{4,20},{20... | collective-permute-start | bytes 6291464 | tf_op jit(solution)/shard_map/ppermute | solution.py:102
  47.9 2.4 %copy-start.1 = (bf16[1,2048,512]{2,1,0:T(8,128)(2,1)S(1)}, bf16[1,2048,512]{2,1,0:T(8,128)(2,1)}, u32[]{:S(2)}) copy-start(bf16[1,2048,512]{2,1,0:T(8,128)(2,1)} %param.10) | copy-start | bytes 6291460
  56.1 1.6 %copy-start.2 = (bf16[1,2048,512]{2,1,0:T(8,128)(2,1)S(1)}, bf16[1,2048,512]{2,1,0:T(8,128)(2,1)}, u32[]{:S(2)}) copy-start(bf16[1,2048,512]{2,1,0:T(8,128)(2,1)} %param.10) | copy-start | bytes 6291460
  57.7 1.6 %copy-start.5 = (bf16[512,2,8,128]{0,3,2,1:T(8,128)(2,1)S(1)}, bf16[512,2,8,128]{0,3,2,1:T(8,128)(2,1)}, u32[]{:S(2)}) copy-start(bf16[512,2,8,128]{0,3,2,1:T(8,128)(2,1)} %copy.47) | copy-start | bytes 6291460
  60.6 1.6 %copy-start.3 = (bf16[1,512,2048]{2,1,0:T(8,128)(2,1)S(1)}, bf16[1,512,2048]{2,1,0:T(8,128)(2,1)}, u32[]{:S(2)}) copy-start(bf16[1,512,2048]{2,1,0:T(8,128)(2,1)} %param.11) | copy-start | bytes 6291460
  62.2 1.6 %copy-start.4 = (bf16[2,8,128,512]{3,2,1,0:T(8,128)(2,1)S(1)}, bf16[2,8,128,512]{3,2,1,0:T(8,128)(2,1)}, u32[]{:S(2)}) copy-start(bf16[2,8,128,512]{3,2,1,0:T(8,128)(2,1)} %copy.48) | copy-start | bytes 6291460
  65.4 4.4 %collective-permute-start.1 = (bf16[1024,1024]{1,0:T(8,128)(2,1)S(1)}, bf16[1024,1024]{1,0:T(8,128)(2,1)S(1)}, u32[]{:S(2)}, u32[]{:S(2)}) collective-permute-start(bf16[1024,1024]{1,0:T(8,128)(2,1)S(1)} %pad_maximum_fusion.3), channel_id=1, source_target_pairs={{0,16},{16,0},{1,17},{17,1},{2,18},{18,2},{3,19},{19,3},{4,20},{20... | collective-permute-start | bytes 6291464 | tf_op jit(solution)/shard_map/ppermute | solution.py:54
  71.0 21.4 %collective-permute-start.4 = (bf16[1024,128]{1,0:T(8,128)(2,1)S(1)}, bf16[1024,128]{1,0:T(8,128)(2,1)S(1)}, u32[]{:S(2)}, u32[]{:S(2)}) collective-permute-start(bf16[1024,128]{1,0:T(8,128)(2,1)S(1)} %get-tuple-element.8), channel_id=1, source_target_pairs={{0,32},{32,64},{64,96},{96,128},{128,160},{160,192},{192,224},{224... | collective-permute-start | bytes 786440 | tf_op jit(solution)/shard_map/ppermute | solution.py:70
  73.1 19.3 %collective-permute-start.7 = (bf16[1024,128]{1,0:T(8,128)(2,1)S(1)}, bf16[1024,128]{1,0:T(8,128)(2,1)S(1)}, u32[]{:S(2)}, u32[]{:S(2)}) collective-permute-start(bf16[1024,128]{1,0:T(8,128)(2,1)S(1)} %get-tuple-element.7), channel_id=1, source_target_pairs={{0,224},{32,0},{64,32},{96,64},{128,96},{160,128},{192,160},{224,1... | collective-permute-start | bytes 786440 | tf_op jit(solution)/shard_map/ppermute | solution.py:70
  77.3 13.6 %collective-permute-start.5 = (bf16[512,128]{1,0:T(8,128)(2,1)S(1)}, bf16[512,128]{1,0:T(8,128)(2,1)S(1)}, u32[]{:S(2)}, u32[]{:S(2)}) collective-permute-start(bf16[512,128]{1,0:T(8,128)(2,1)S(1)} %get-tuple-element.12), channel_id=1, source_target_pairs={{0,64},{32,96},{64,128},{96,160},{128,192},{160,224},{192,0},{224,... | collective-permute-start | bytes 393224 | tf_op jit(solution)/shard_map/ppermute | solution.py:70
  77.4 15.0 %collective-permute-start.8 = (bf16[512,128]{1,0:T(8,128)(2,1)S(1)}, bf16[512,128]{1,0:T(8,128)(2,1)S(1)}, u32[]{:S(2)}, u32[]{:S(2)}) collective-permute-start(bf16[512,128]{1,0:T(8,128)(2,1)S(1)} %get-tuple-element.13), channel_id=1, source_target_pairs={{0,192},{32,224},{64,0},{96,32},{128,64},{160,96},{192,128},{224,1... | collective-permute-start | bytes 393224 | tf_op jit(solution)/shard_map/ppermute | solution.py:70
  81.5 17.9 %collective-permute-start.2 = (bf16[1024,128]{1,0:T(8,128)(2,1)S(1)}, bf16[1024,128]{1,0:T(8,128)(2,1)S(1)}, u32[]{:S(2)}, u32[]{:S(2)}) collective-permute-start(bf16[1024,128]{1,0:T(8,128)(2,1)S(1)} %get-tuple-element.6), channel_id=1, source_target_pairs={{0,32},{32,64},{64,96},{96,128},{128,160},{160,192},{192,224},{224... | collective-permute-start | bytes 786440 | tf_op jit(solution)/shard_map/ppermute | solution.py:70
  91.0 11.1 %collective-permute-start.3 = (bf16[1024,128]{1,0:T(8,128)(2,1)S(1)}, bf16[1024,128]{1,0:T(8,128)(2,1)S(1)}, u32[]{:S(2)}, u32[]{:S(2)}) collective-permute-start(bf16[1024,128]{1,0:T(8,128)(2,1)S(1)} %get-tuple-element.9), channel_id=1, source_target_pairs={{0,224},{32,0},{64,32},{96,64},{128,96},{160,128},{192,160},{224,1... | collective-permute-start | bytes 786440 | tf_op jit(solution)/shard_map/ppermute | solution.py:70
  92.6 13.9 %collective-permute-start.6 = (bf16[1024,128]{1,0:T(8,128)(2,1)S(1)}, bf16[1024,128]{1,0:T(8,128)(2,1)S(1)}, u32[]{:S(2)}, u32[]{:S(2)}) collective-permute-start(bf16[1024,128]{1,0:T(8,128)(2,1)S(1)} %get-tuple-element.10), channel_id=1, source_target_pairs={{0,64},{32,96},{64,128},{96,160},{128,192},{160,224},{192,0},{224,... | collective-permute-start | bytes 786440 | tf_op jit(solution)/shard_map/ppermute | solution.py:70
  94.8 14.8 %collective-permute-start.9 = (bf16[1024,128]{1,0:T(8,128)(2,1)S(1)}, bf16[1024,128]{1,0:T(8,128)(2,1)S(1)}, u32[]{:S(2)}, u32[]{:S(2)}) collective-permute-start(bf16[1024,128]{1,0:T(8,128)(2,1)S(1)} %get-tuple-element.11), channel_id=1, source_target_pairs={{0,192},{32,224},{64,0},{96,32},{128,64},{160,96},{192,128},{224,1... | collective-permute-start | bytes 786440 | tf_op jit(solution)/shard_map/ppermute | solution.py:70
  110.5 12.2 %all-to-all-start.1 = ((bf16[16,32,256]{2,1,0:T(8,128)(2,1)}), bf16[16,32,256]{2,1,0:T(8,128)(2,1)S(1)}, u32[]{:S(2)}, u32[]{:S(2)}) async-start(bf16[16,32,256]{2,1,0:T(8,128)(2,1)} %pad_maximum_fusion.10), calls=%async_computation.1 | async-start | bytes 524288 | tf_op jit(solution)/shard_map/all_to_all | solution.py:148

commit v5 on v4

--- a/solution.py
+++ b/solution.py
@@ -71,10 +71,10 @@
 
     rows = pair_sum.shape[0]
     top = rows // 2
-    near_up = shift(block[1], 1)
-    near_down = shift(block[7], -1)
-    via_up = shift(block[3], 1)
-    via_down = shift(block[5], -1)
+    up_pair = shift(jnp.concatenate([block[1], block[3]], axis=0), 1)
+    down_pair = shift(jnp.concatenate([block[7], block[5]], axis=0), -1)
+    near_up, via_up = up_pair[:rows], up_pair[rows:]
+    near_down, via_down = down_pair[:rows], down_pair[rows:]
     far_up = shift(block[4][:top], 2)
     far_down = shift(block[4][top:], -2)
     zeros = jnp.zeros((rows - top, cols), jnp.float32)

time: 126 us -> 129 us (1.024)
  waiting for transfers between devices: 28.2 us -> 31.2 us
    ppermute x8 -> x6, waiting for transfers between devices: 19.6 us -> 22.7 us  [shift(): lax.ppermute(x, 'z', [(j, (j + k) % n_z) for j in range(n_z)])]
    ppermute x8 -> x6, starting transfers between devices: 16.1 us -> 15.8 us  [shift(): lax.ppermute(x, 'z', [(j, (j + k) % n_z) for j in range(n_z)])]
    unnamed x19 -> x21, local copies, waits for them, and re-layouts: 8.6 us -> 8.6 us
  transfers between devices with their start and end apart: 11 -> 9, of which waited for: 6 -> 8; matrix products, arithmetic and copies ran while one was open for 14% -> 13% of each run, Pallas kernels for 0% -> 0%
where the time goes in v5:
time: 129 us; the launch traced here: 128 us
  blocking collectives  34.3 us (27%)
  waiting for transfers between devices  31.2 us (24%)
  starting transfers between devices  21.2 us (16%)
  local copies, waits for them, and re-layouts  14.7 us (11%)
  other arithmetic  13.5 us (10%)
  matrix products  12.1 us (9%)
    all_to_all x1, blocking collectives, dispatch_rows(): lax.all_to_all(sent.reshape(n_exp, capacity, sent.shape[1]), 'exp', split...  34.3 us
    ppermute x6, waiting for transfers between devices, shift(): lax.ppermute(x, 'z', [(j, (j + k) % n_z) for j in range(n_z)])  22.7 us
    ppermute x6, starting transfers between devices, shift(): lax.ppermute(x, 'z', [(j, (j + k) % n_z) for j in range(n_z)])  15.8 us
    unnamed x21, local copies, waits for them, and re-layouts  8.6 us
    all_to_all x1, waiting for transfers between devices, local(): lax.all_to_all(both.reshape(n_exp, capacity, 2 * cols), 'exp', split_axis...  4.79 us
    all_to_all x1, starting transfers between devices, local(): lax.all_to_all(both.reshape(n_exp, capacity, 2 * cols), 'exp', split_axis...  4.78 us
    ppermute x1, waiting for transfers between devices, reduce_over_rep(): lax.ppermute(jnp.concatenate([p[:, share:] for p in parts], axis=0), 'cor...  3.79 us
    squeeze x1, other arithmetic, pick(): return lax.dynamic_index_in_dim(stacked, index, axis=axis, keepdims=False)  2.75 us
  transfers between devices with their start and end apart: 9, of which 8 were waited for; matrix products, arithmetic and copies ran while one was open for 13% of the time, Pallas kernels for 0%

profile of v5, /device:TPU:2, one launch (start us, length us, event | category | flops | bytes accessed | tf_op | source)
XLA Modules:
  0.0 128.0 jit_solution(6338459455274239534)
XLA Ops:
  0.7 0.8 copy.41
  1.5 0.1 eq.55
  1.6 0.1 reshape.78
  1.8 0.6 reduce-window.6
  2.4 0.2 slice_reduce_fusion
  2.6 0.1 fusion.42
  2.7 0.1 reduce_sum.42
  2.9 1.0 dynamic-slice_convert_fusion
  3.9 0.4 mul.69
  4.3 0.7 mul.70
  5.0 0.1 copy.40
  5.1 0.1 mul.67
  5.3 0.1 fusion.33
  5.4 0.4 convolution_convert_fusion.4
  5.9 0.5 convolution_convert_fusion.5
  6.4 0.2 pad_maximum_fusion
  6.6 34.3 %all_to_all.10 = bf16[16,32,2048]{2,1,0:T(8,128)(2,1)S(1)} all-to-all(bf16[16,32,2048]{2,1,0:T(8,128)(2,1)S(1)} %bitcast.62), channel_id=1, replica_groups=mesh['z'=8,'core'=2,'exp'=16] {'exp'}, dimensions={0} | all-to-all | bytes 4194304 | tf_op jit(solution)/shard_map/all_to_all | solution.py:99
  40.9 3.9 %copy.46 = bf16[1,512,2048]{1,2,0:T(8,128)(2,1)} copy(bf16[1,512,2048]{2,1,0:T(8,128)(2,1)} %param.11) | data formatting | bytes 4194304 | tf_op args[5]
  44.8 2.3 %fusion.7 = bf16[512,8,2,128]{0,3,2,1:T(8,128)(2,1)S(1)} fusion(s32[]{:T(128)S(6)} %select_n.50, bf16[512,8,2,128]{0,3,2,1:T(8,128)(2,1)} %bitcast.61), kind=kLoop, calls=%fused_computation.24 | loop fusion | flops 1048576 | bytes 4194308 | tf_op jit(solution)/shard_map/jit(_roll_dynamic)/concatenate | solution.py:126
  47.1 0.8 fusion.6
  47.9 1.5 %copy.47 = bf16[512,2,8,128]{0,3,2,1:T(8,128)(2,1)} copy(bf16[512,2,8,128]{0,3,1,2:T(8,128)(2,1)S(1)} %fusion.6) | data formatting | bytes 4194304 | tf_op jit(solution)/shard_map/transpose | solution.py:127
  49.4 0.8 copy-done.2
  50.3 0.8 fusion.4
  51.0 0.8 fusion.3
  51.8 1.5 %copy.48 = bf16[2,8,128,512]{3,2,1,0:T(8,128)(2,1)} copy(bf16[2,8,128,512]{3,2,0,1:T(8,128)(2,1)S(1)} %fusion.3) | data formatting | bytes 4194304 | tf_op jit(solution)/shard_map/transpose | solution.py:129
  53.3 2.8 %fusion.11 = (bf16[512,2048]{1,0:T(8,128)(2,1)S(1)}, bf16[512,2048]{1,0:T(8,128)(2,1)S(1)}) fusion(s32[]{:T(128)S(6)} %select_n.47, bf16[1,512,2048]{2,1,0:T(8,128)(2,1)S(1)} %bitcast.60, bf16[1,512,2048]{2,1,0:T(8,128)(2,1)} %bitcast.4, s32[]{:T(128)S(6)} %select_n.48), kind=kLoop, calls=%fused_computation.28 | loop fusion | flops 2097152 | bytes 8388616 | tf_op jit(solution)/shard_map/jit(dynamic_index_in_dim)/squeeze | solution.py:49
  56.1 0.6 fusion.53
  56.7 1.0 copy-done.3
  57.7 1.2 fusion.14
  58.9 0.3 copy-done.6
  59.3 1.3 %convolution_convert_fusion.3 = bf16[512,2048]{1,0:T(8,128)(2,1)S(1)} fusion(bf16[512,2048]{0,1:T(8,128)(2,1)S(1)} %bitcast.65, f32[512,512]{1,0:T(8,128)S(1)} %fusion.14), kind=kOutput, calls=%fused_computation.16 | convolution fusion | flops 1076101120 | bytes 5242880 | tf_op jit(solution)/shard_map/dot_general | solution.py:24
  60.6 0.2 fusion.51
  60.8 1.4 %copy-done.4 = bf16[1,512,2048]{2,1,0:T(8,128)(2,1)S(1)} copy-done((bf16[1,512,2048]{2,1,0:T(8,128)(2,1)S(1)}, bf16[1,512,2048]{2,1,0:T(8,128)(2,1)}, u32[]{:S(2)}) %copy-start.4) | copy-done | bytes 2097176
  62.2 1.4 %fusion.19 = bf16[512,512]{1,0:T(8,128)(2,1)S(1)} fusion(bf16[1,512,2048]{2,1,0:T(8,128)(2,1)S(1)} %copy-done.4, bf16[512,1024]{1,0:T(8,128)(2,1)S(1)} %get-tuple-element.24, bf16[512,1024]{1,0:T(8,128)(2,1)S(1)} %get-tuple-element.19, f32[512,512]{1,0:T(8,128)S(1)} %fusion.14), kind=kOutput, calls=%fused_computation.40 | convolution fusion | flops 1080295424 | bytes 5767168 | tf_op jit(solution)/shard_map/dot_general | solution.py:25
  63.6 0.1 copy-done.5
  63.8 1.3 %convolution_convert_fusion.2 = bf16[512,2048]{1,0:T(8,128)(2,1)S(1)} fusion(bf16[512,512]{1,0:T(8,128)(2,1)S(1)} %fusion.19, bf16[2048,512]{1,0:T(8,128)(2,1)S(1)} %bitcast.64), kind=kOutput, calls=%fused_computation.15 | convolution fusion | flops 1074790400 | bytes 4718592 | tf_op jit(solution)/shard_map/dot_general | solution.py:30
  65.1 0.2 fusion.52
  65.2 0.2 pad_maximum_fusion.3
  65.4 0.6 collective-permute-start.1
  66.0 3.8 %collective-permute-done.1 = bf16[1024,1024]{1,0:T(8,128)(2,1)S(1)} collective-permute-done((bf16[1024,1024]{1,0:T(8,128)(2,1)S(1)}, bf16[1024,1024]{1,0:T(8,128)(2,1)S(1)}, u32[]{:S(2)}, u32[]{:S(2)}) %collective-permute-start.1) | collective-permute-done | bytes 2097184 | tf_op jit(solution)/shard_map/ppermute | solution.py:54
  69.8 1.0 add_convert_fusion
  70.8 0.2 fusion.50
  71.0 2.1 %collective-permute-start.2 = (bf16[2048,128]{1,0:T(8,128)(2,1)S(1)}, bf16[2048,128]{1,0:T(8,128)(2,1)S(1)}, u32[]{:S(2)}, u32[]{:S(2)}) collective-permute-start(bf16[2048,128]{1,0:T(8,128)(2,1)S(1)} %pad_maximum_fusion.10), channel_id=1, source_target_pairs={{0,32},{32,64},{64,96},{96,128},{128,160},{160,192},{192,224},{224... | collective-permute-start | bytes 1572872 | tf_op jit(solution)/shard_map/ppermute | solution.py:70
  73.2 4.1 %collective-permute-start.3 = (bf16[2048,128]{1,0:T(8,128)(2,1)S(1)}, bf16[2048,128]{1,0:T(8,128)(2,1)S(1)}, u32[]{:S(2)}, u32[]{:S(2)}) collective-permute-start(bf16[2048,128]{1,0:T(8,128)(2,1)S(1)} %pad_maximum_fusion.11), channel_id=1, source_target_pairs={{0,224},{32,0},{64,32},{96,64},{128,96},{160,128},{192,160},{224,1... | collective-permute-start | bytes 1572872 | tf_op jit(solution)/shard_map/ppermute | solution.py:70
  77.4 0.1 collective-permute-start.4
  77.5 4.1 %collective-permute-start.6 = (bf16[512,128]{1,0:T(8,128)(2,1)S(1)}, bf16[512,128]{1,0:T(8,128)(2,1)S(1)}, u32[]{:S(2)}, u32[]{:S(2)}) collective-permute-start(bf16[512,128]{1,0:T(8,128)(2,1)S(1)} %get-tuple-element.9), channel_id=1, source_target_pairs={{0,192},{32,224},{64,0},{96,32},{128,64},{160,96},{192,128},{224,1... | collective-permute-start | bytes 393224 | tf_op jit(solution)/shard_map/ppermute | solution.py:70
  81.6 8.4 %collective-permute-done.2 = bf16[2048,128]{1,0:T(8,128)(2,1)S(1)} collective-permute-done((bf16[2048,128]{1,0:T(8,128)(2,1)S(1)}, bf16[2048,128]{1,0:T(8,128)(2,1)S(1)}, u32[]{:S(2)}, u32[]{:S(2)}) %collective-permute-start.2) | collective-permute-done | bytes 524320 | tf_op jit(solution)/shard_map/ppermute | solution.py:70
  90.1 2.3 %collective-permute-done.3 = bf16[2048,128]{1,0:T(8,128)(2,1)S(1)} collective-permute-done((bf16[2048,128]{1,0:T(8,128)(2,1)S(1)}, bf16[2048,128]{1,0:T(8,128)(2,1)S(1)}, u32[]{:S(2)}, u32[]{:S(2)}) %collective-permute-start.3) | collective-permute-done | bytes 524320 | tf_op jit(solution)/shard_map/ppermute | solution.py:70
  92.4 1.8 %collective-permute-done.4 = bf16[512,128]{1,0:T(8,128)(2,1)S(1)} collective-permute-done((bf16[512,128]{1,0:T(8,128)(2,1)S(1)}, bf16[512,128]{1,0:T(8,128)(2,1)S(1)}, u32[]{:S(2)}, u32[]{:S(2)}) %collective-permute-start.4) | collective-permute-done | bytes 131104 | tf_op jit(solution)/shard_map/ppermute | solution.py:70
  94.2 0.5 collective-permute-done.6
  94.7 0.2 fusion.25
  94.9 5.3 %collective-permute-start.5 = (bf16[1024,128]{1,0:T(8,128)(2,1)S(1)}, bf16[1024,128]{1,0:T(8,128)(2,1)S(1)}, u32[]{:S(2)}, u32[]{:S(2)}) collective-permute-start(bf16[1024,128]{1,0:T(8,128)(2,1)S(1)} %get-tuple-element.6), channel_id=1, source_target_pairs={{0,64},{32,96},{64,128},{96,160},{128,192},{160,224},{192,0},{224,... | collective-permute-start | bytes 786440 | tf_op jit(solution)/shard_map/ppermute | solution.py:70
  100.2 2.7 %fusion.1 = bf16[1,512,2048]{2,1,0:T(8,128)(2,1)} fusion(bf16[512,1024]{1,0:T(8,128)(2,1)S(1)} %get-tuple-element.24, bf16[512,1024]{1,0:T(8,128)(2,1)S(1)} %get-tuple-element.19, f32[512,512]{1,0:T(8,128)S(1)} %fusion.14), kind=kOutput, calls=%fused_computation.18 | convolution fusion | flops 1080295424 | bytes 5242880 | tf_op jit(solution)/shard_map/dot_general | solution.py:36
  102.8 8.4 %collective-permute-done.5 = bf16[1024,128]{1,0:T(8,128)(2,1)S(1)} collective-permute-done((bf16[1024,128]{1,0:T(8,128)(2,1)S(1)}, bf16[1024,128]{1,0:T(8,128)(2,1)S(1)}, u32[]{:S(2)}, u32[]{:S(2)}) %collective-permute-start.5) | collective-permute-done | bytes 262176 | tf_op jit(solution)/shard_map/ppermute | solution.py:70
  111.2 1.4 %collective-permute-done.7 = bf16[1024,128]{1,0:T(8,128)(2,1)S(1)} collective-permute-done((bf16[1024,128]{1,0:T(8,128)(2,1)S(1)}, bf16[1024,128]{1,0:T(8,128)(2,1)S(1)}, u32[]{:S(2)}, u32[]{:S(2)}) %collective-permute-start.7) | collective-permute-done | bytes 262176 | tf_op jit(solution)/shard_map/ppermute | solution.py:70
  112.6 0.2 fusion.28
  112.8 0.7 pad_maximum_fusion.12
  113.5 4.8 %all-to-all-start.1 = ((bf16[16,32,256]{2,1,0:T(8,128)(2,1)}), bf16[16,32,256]{2,1,0:T(8,128)(2,1)S(1)}, u32[]{:S(2)}, u32[]{:S(2)}) async-start(bf16[16,32,256]{2,1,0:T(8,128)(2,1)} %pad_maximum_fusion.12), calls=%async_computation.1 | async-start | bytes 524288 | tf_op jit(solution)/shard_map/all_to_all | solution.py:148
  118.3 2.6 %fusion = bf16[1,2048,512]{2,1,0:T(8,128)(2,1)} fusion(bf16[512,512]{1,0:T(8,128)(2,1)S(1)} %fusion.19, bf16[512,1024]{1,0:T(8,128)(2,1)S(1)} %get-tuple-element.25, bf16[512,1024]{1,0:T(8,128)(2,1)S(1)} %get-tuple-element.18), kind=kOutput, calls=%fused_computation.17 | convolution fusion | flops 1078984704 | bytes 4718592 | tf_op jit(solution)/shard_map/dot_general | solution.py:39
  120.9 4.8 %all-to-all-done.1 = bf16[16,32,256]{2,1,0:T(8,128)(2,1)S(1)} async-done(((bf16[16,32,256]{2,1,0:T(8,128)(2,1)}), bf16[16,32,256]{2,1,0:T(8,128)(2,1)S(1)}, u32[]{:S(2)}, u32[]{:S(2)}) %all-to-all-start.1) | async-done | bytes 262176 | tf_op jit(solution)/shard_map/all_to_all | solution.py:148
  125.7 0.3 fusion.30
  126.0 0.3 fusion.31
  126.4 0.9 multiply_reduce_fusion
  127.2 0.8 reduce_sum.45
  (28 shorter events, 0.5 us)
Async XLA Ops:
  0.6 4.8 %copy-start = (bf16[128,2048]{1,0:T(8,128)(2,1)S(1)}, bf16[128,2048]{1,0:T(8,128)(2,1)}, u32[]{:S(2)}) copy-start(bf16[128,2048]{1,0:T(8,128)(2,1)} %param.6) | copy-start | bytes 1572868
  2.9 2.1 %copy-start.8 = (f32[128,2]{0,1:T(2,128)S(1)}, f32[128,2]{0,1:T(2,128)}, u32[]{:S(2)}) copy-start(f32[128,2]{0,1:T(2,128)} %param.8) | copy-start | bytes 3076
  3.9 1.4 %copy-start.7 = (s32[128,2]{0,1:T(2,128)S(1)}, s32[128,2]{0,1:T(2,128)}, u32[]{:S(2)}) copy-start(s32[128,2]{0,1:T(2,128)} %param.7) | copy-start | bytes 3076
  40.9 12.4 %collective-permute-start = (bf16[512,2048]{1,0:T(8,128)(2,1)S(1)}, bf16[512,2048]{1,0:T(8,128)(2,1)}, u32[]{:S(2)}, u32[]{:S(2)}) collective-permute-start(bf16[512,2048]{1,0:T(8,128)(2,1)S(1)} %bitcast.59), channel_id=1, source_target_pairs={{0,16},{16,0},{1,17},{17,1},{2,18},{18,2},{3,19},{19,3},{4,20},{20... | collective-permute-start | bytes 6291464 | tf_op jit(solution)/shard_map/ppermute | solution.py:102
  47.9 2.4 %copy-start.2 = (bf16[1,2048,512]{2,1,0:T(8,128)(2,1)S(1)}, bf16[1,2048,512]{2,1,0:T(8,128)(2,1)}, u32[]{:S(2)}) copy-start(bf16[1,2048,512]{2,1,0:T(8,128)(2,1)} %param.10) | copy-start | bytes 6291460
  56.1 1.6 %copy-start.3 = (bf16[1,2048,512]{2,1,0:T(8,128)(2,1)S(1)}, bf16[1,2048,512]{2,1,0:T(8,128)(2,1)}, u32[]{:S(2)}) copy-start(bf16[1,2048,512]{2,1,0:T(8,128)(2,1)} %param.10) | copy-start | bytes 6291460
  57.7 1.6 %copy-start.6 = (bf16[512,2,8,128]{0,3,2,1:T(8,128)(2,1)S(1)}, bf16[512,2,8,128]{0,3,2,1:T(8,128)(2,1)}, u32[]{:S(2)}) copy-start(bf16[512,2,8,128]{0,3,2,1:T(8,128)(2,1)} %copy.47) | copy-start | bytes 6291460
  60.6 1.6 %copy-start.4 = (bf16[1,512,2048]{2,1,0:T(8,128)(2,1)S(1)}, bf16[1,512,2048]{2,1,0:T(8,128)(2,1)}, u32[]{:S(2)}) copy-start(bf16[1,512,2048]{2,1,0:T(8,128)(2,1)} %param.11) | copy-start | bytes 6291460
  62.2 1.6 %copy-start.5 = (bf16[2,8,128,512]{3,2,1,0:T(8,128)(2,1)S(1)}, bf16[2,8,128,512]{3,2,1,0:T(8,128)(2,1)}, u32[]{:S(2)}) copy-start(bf16[2,8,128,512]{3,2,1,0:T(8,128)(2,1)} %copy.48) | copy-start | bytes 6291460
  65.4 4.4 %collective-permute-start.1 = (bf16[1024,1024]{1,0:T(8,128)(2,1)S(1)}, bf16[1024,1024]{1,0:T(8,128)(2,1)S(1)}, u32[]{:S(2)}, u32[]{:S(2)}) collective-permute-start(bf16[1024,1024]{1,0:T(8,128)(2,1)S(1)} %pad_maximum_fusion.3), channel_id=1, source_target_pairs={{0,16},{16,0},{1,17},{17,1},{2,18},{18,2},{3,19},{19,3},{4,20},{20... | collective-permute-start | bytes 6291464 | tf_op jit(solution)/shard_map/ppermute | solution.py:54
  71.0 18.9 %collective-permute-start.2 = (bf16[2048,128]{1,0:T(8,128)(2,1)S(1)}, bf16[2048,128]{1,0:T(8,128)(2,1)S(1)}, u32[]{:S(2)}, u32[]{:S(2)}) collective-permute-start(bf16[2048,128]{1,0:T(8,128)(2,1)S(1)} %pad_maximum_fusion.10), channel_id=1, source_target_pairs={{0,32},{32,64},{64,96},{96,128},{128,160},{160,192},{192,224},{224... | collective-permute-start | bytes 1572872 | tf_op jit(solution)/shard_map/ppermute | solution.py:70
  73.2 19.1 %collective-permute-start.3 = (bf16[2048,128]{1,0:T(8,128)(2,1)S(1)}, bf16[2048,128]{1,0:T(8,128)(2,1)S(1)}, u32[]{:S(2)}, u32[]{:S(2)}) collective-permute-start(bf16[2048,128]{1,0:T(8,128)(2,1)S(1)} %pad_maximum_fusion.11), channel_id=1, source_target_pairs={{0,224},{32,0},{64,32},{96,64},{128,96},{160,128},{192,160},{224,1... | collective-permute-start | bytes 1572872 | tf_op jit(solution)/shard_map/ppermute | solution.py:70
  77.4 16.8 %collective-permute-start.4 = (bf16[512,128]{1,0:T(8,128)(2,1)S(1)}, bf16[512,128]{1,0:T(8,128)(2,1)S(1)}, u32[]{:S(2)}, u32[]{:S(2)}) collective-permute-start(bf16[512,128]{1,0:T(8,128)(2,1)S(1)} %get-tuple-element.8), channel_id=1, source_target_pairs={{0,64},{32,96},{64,128},{96,160},{128,192},{160,224},{192,0},{224,... | collective-permute-start | bytes 393224 | tf_op jit(solution)/shard_map/ppermute | solution.py:70
  77.5 17.2 %collective-permute-start.6 = (bf16[512,128]{1,0:T(8,128)(2,1)S(1)}, bf16[512,128]{1,0:T(8,128)(2,1)S(1)}, u32[]{:S(2)}, u32[]{:S(2)}) collective-permute-start(bf16[512,128]{1,0:T(8,128)(2,1)S(1)} %get-tuple-element.9), channel_id=1, source_target_pairs={{0,192},{32,224},{64,0},{96,32},{128,64},{160,96},{192,128},{224,1... | collective-permute-start | bytes 393224 | tf_op jit(solution)/shard_map/ppermute | solution.py:70
  94.9 16.3 %collective-permute-start.5 = (bf16[1024,128]{1,0:T(8,128)(2,1)S(1)}, bf16[1024,128]{1,0:T(8,128)(2,1)S(1)}, u32[]{:S(2)}, u32[]{:S(2)}) collective-permute-start(bf16[1024,128]{1,0:T(8,128)(2,1)S(1)} %get-tuple-element.6), channel_id=1, source_target_pairs={{0,64},{32,96},{64,128},{96,160},{128,192},{160,224},{192,0},{224,... | collective-permute-start | bytes 786440 | tf_op jit(solution)/shard_map/ppermute | solution.py:70
  100.2 12.4 %collective-permute-start.7 = (bf16[1024,128]{1,0:T(8,128)(2,1)S(1)}, bf16[1024,128]{1,0:T(8,128)(2,1)S(1)}, u32[]{:S(2)}, u32[]{:S(2)}) collective-permute-start(bf16[1024,128]{1,0:T(8,128)(2,1)S(1)} %get-tuple-element.7), channel_id=1, source_target_pairs={{0,192},{32,224},{64,0},{96,32},{128,64},{160,96},{192,128},{224,1... | collective-permute-start | bytes 786440 | tf_op jit(solution)/shard_map/ppermute | solution.py:70
  113.5 12.2 %all-to-all-start.1 = ((bf16[16,32,256]{2,1,0:T(8,128)(2,1)}), bf16[16,32,256]{2,1,0:T(8,128)(2,1)S(1)}, u32[]{:S(2)}, u32[]{:S(2)}) async-start(bf16[16,32,256]{2,1,0:T(8,128)(2,1)} %pad_maximum_fusion.12), calls=%async_computation.1 | async-start | bytes 524288 | tf_op jit(solution)/shard_map/all_to_all | solution.py:148
  118.3 9.7 %copy-start.1 = (bf16[128,2048]{1,0:T(8,128)(2,1)S(1)}, bf16[128,2048]{1,0:T(8,128)(2,1)}, u32[]{:S(2)}) copy-start(bf16[128,2048]{1,0:T(8,128)(2,1)} %param.6) | copy-start | bytes 1572868

commit v6 on v4

--- a/solution.py
+++ b/solution.py
@@ -99,13 +99,14 @@
     got = lax.all_to_all(
         sent.reshape(n_exp, capacity, sent.shape[1]), "exp", split_axis=0, concat_axis=0, tiled=True
     ).reshape(n_exp * capacity, sent.shape[1])
-    other = lax.ppermute(got, "core", [(j, (j + 1) % n_core) for j in range(n_core)])
-    pair = jnp.stack([got, other])
-    first, second = pick(pair, core, 0), pick(pair, 1 - core, 0)
-    return [
-        jnp.concatenate([first[:, i * share : (i + 1) * share], second[:, i * share : (i + 1) * share]], axis=1)
-        for i in range(len(sources))
-    ]
+    swap = [(j, (j + 1) % n_core) for j in range(n_core)]
+    rows = []
+    for i in range(len(sources)):
+        mine = got[:, i * share : (i + 1) * share]
+        other = lax.ppermute(mine, "core", swap)
+        pair = jnp.stack([mine, other])
+        rows.append(jnp.concatenate([pick(pair, core, 0), pick(pair, 1 - core, 0)], axis=1))
+    return rows
 
 
 def local(tokens, expert_ids, gate_values, grad_out, w_up, w_down):

time: 126 us -> 127 us (level)
    unnamed x19 -> x23, local copies, waits for them, and re-layouts: 8.6 us -> 5.62 us
    slice x2, local copies, waits for them, and re-layouts: 0.75 us -> 2.38 us  [the longest x1 2.19 us: dispatch_rows(): mine = got[:, i * share:(i + 1) * share]]
    concatenate x1, other arithmetic: 2.34 us -> 0.76 us  [local(): jnp.roll(down_weight.reshape(ff_local, n_z, n_core, cols), (-zi, -core),...]
    squeeze x1 -> x2, other arithmetic: 2.75 us -> 4.26 us  [pick(): return lax.dynamic_index_in_dim(stacked, index, axis=axis, keepdims=False)]
  transfers between devices with their start and end apart: 11 -> 12, of which waited for: 6 -> 7; matrix products, arithmetic and copies ran while one was open for 14% -> 15% of each run, Pallas kernels for 0% -> 0%
where the time goes in v6:
time: 127 us; the launch traced here: 126 us
  blocking collectives  34.3 us (27%)
  waiting for transfers between devices  29.2 us (23%)
  starting transfers between devices  22.3 us (18%)
  other arithmetic  13.9 us (11%)
  local copies, waits for them, and re-layouts  13.6 us (11%)
  matrix products  12.2 us (10%)
    all_to_all x1, blocking collectives, dispatch_rows(): lax.all_to_all(sent.reshape(n_exp, capacity, sent.shape[1]), 'exp', split...  34.3 us
    ppermute x8, waiting for transfers between devices, shift(): lax.ppermute(x, 'z', [(j, (j + k) % n_z) for j in range(n_z)])  20.5 us
    ppermute x8, starting transfers between devices, shift(): lax.ppermute(x, 'z', [(j, (j + k) % n_z) for j in range(n_z)])  16.6 us
    unnamed x23, local copies, waits for them, and re-layouts  5.62 us
    all_to_all x1, starting transfers between devices, local(): lax.all_to_all(both.reshape(n_exp, capacity, 2 * cols), 'exp', split_axis...  4.79 us
    all_to_all x1, waiting for transfers between devices, local(): lax.all_to_all(both.reshape(n_exp, capacity, 2 * cols), 'exp', split_axis...  4.79 us
    squeeze x2, other arithmetic, pick(): return lax.dynamic_index_in_dim(stacked, index, axis=axis, keepdims=False)  4.26 us
    ppermute x1, waiting for transfers between devices, reduce_over_rep(): lax.ppermute(jnp.concatenate([p[:, share:] for p in parts], axis=0), 'cor...  3.89 us
  transfers between devices with their start and end apart: 12, of which 7 were waited for; matrix products, arithmetic and copies ran while one was open for 15% of the time, Pallas kernels for 0%

profile of v6, /device:TPU:2, one launch (start us, length us, event | category | flops | bytes accessed | tf_op | source)
XLA Modules:
  0.0 126.4 jit_solution(15325158250321026214)
XLA Ops:
  0.6 0.8 copy.41
  1.5 0.1 reshape.78
  1.6 0.1 eq.55
  1.8 0.6 reduce-window.6
  2.4 0.2 slice_reduce_fusion
  2.6 0.1 fusion.39
  2.7 0.1 reduce_sum.42
  2.9 0.8 copy.40
  3.6 0.1 mul.67
  3.8 0.7 multiply_add_fusion
  4.6 1.0 dynamic-slice_convert_fusion
  5.6 0.4 mul.69
  6.0 0.7 mul.70
  6.7 0.4 convolution_convert_fusion.4
  7.2 0.5 convolution_convert_fusion.5
  7.7 0.2 pad_maximum_fusion
  7.9 34.3 %all_to_all.10 = bf16[16,32,2048]{2,1,0:T(8,128)(2,1)S(1)} all-to-all(bf16[16,32,2048]{2,1,0:T(8,128)(2,1)S(1)} %bitcast.68), channel_id=1, replica_groups=mesh['z'=8,'core'=2,'exp'=16] {'exp'}, dimensions={0} | all-to-all | bytes 4194304 | tf_op jit(solution)/shard_map/all_to_all | solution.py:99
  42.2 2.2 %fusion.50 = (bf16[512,1024]{1,0:T(8,128)(2,1)}, bf16[1,512,1024]{2,1,0:T(8,128)(2,1)}, bf16[1,512,1024]{2,1,0:T(8,128)(2,1)}, bf16[512,1024]{1,0:T(8,128)(2,1)}) fusion(bf16[512,2048]{1,0:T(8,128)(2,1)S(1)} %bitcast.67), kind=kLoop, calls=%fused_computation.93 | loop fusion | bytes 6291456 | tf_op jit(solution)/shard_map/slice | solution.py:105
  44.4 0.3 copy-done.3
  44.7 0.8 fusion.4
  45.4 0.8 fusion.3
  46.2 1.5 %copy.48 = bf16[2,8,128,512]{3,2,1,0:T(8,128)(2,1)} copy(bf16[2,8,128,512]{3,2,0,1:T(8,128)(2,1)S(1)} %fusion.3) | data formatting | bytes 4194304 | tf_op jit(solution)/shard_map/transpose | solution.py:130
  47.7 2.9 %copy.46 = bf16[1,512,2048]{1,2,0:T(8,128)(2,1)S(1)} copy(bf16[1,512,2048]{2,1,0:T(8,128)(2,1)} %param.11) | data formatting | bytes 4194304 | tf_op args[5]
  50.6 0.8 fusion.7
  51.3 0.5 collective-permute-start.1
  51.8 0.7 fusion.6
  52.6 1.5 %copy.47 = bf16[512,2,8,128]{0,3,2,1:T(8,128)(2,1)} copy(bf16[512,2,8,128]{0,3,1,2:T(8,128)(2,1)S(1)} %fusion.6) | data formatting | bytes 4194304 | tf_op jit(solution)/shard_map/transpose | solution.py:128
  54.1 2.1 %fusion.25 = (bf16[512,1024]{1,0:T(8,128)(2,1)S(1)}, bf16[512,1024]{1,0:T(8,128)(2,1)S(1)}) fusion(s32[]{:T(128)S(6)} %select_n.49, bf16[1,512,1024]{2,1,0:T(8,128)(2,1)S(1)} %copy-done.2, bf16[1,512,1024]{2,1,0:T(8,128)(2,1)} %bitcast.4, s32[]{:T(128)S(6)} %select_n.50), kind=kLoop, calls=%fused_computation.48 | loop fusion | flops 1048576 | bytes 4194312 | tf_op jit(solution)/shard_map/jit(dynamic_index_in_dim)/squeeze | solution.py:49
  56.3 1.3 fusion.10
  57.6 0.7 copy-done.7
  58.3 1.3 %convolution_convert_fusion.3 = bf16[512,2048]{1,0:T(8,128)(2,1)S(1)} fusion(bf16[512,2048]{0,1:T(8,128)(2,1)S(1)} %bitcast.72, f32[512,512]{1,0:T(8,128)S(1)} %fusion.10), kind=kOutput, calls=%fused_computation.12 | convolution fusion | flops 1076101120 | bytes 5242880 | tf_op jit(solution)/shard_map/dot_general | solution.py:24
  59.6 2.1 %fusion.21 = (bf16[512,1024]{1,0:T(8,128)(2,1)S(1)}, bf16[512,1024]{1,0:T(8,128)(2,1)S(1)}) fusion(s32[]{:T(128)S(6)} %select_n.49, bf16[1,512,1024]{2,1,0:T(8,128)(2,1)S(1)} %copy-done.1, bf16[1,512,1024]{2,1,0:T(8,128)(2,1)} %bitcast.12, s32[]{:T(128)S(6)} %select_n.50), kind=kLoop, calls=%fused_computation.44 | loop fusion | flops 1048576 | bytes 4194312 | tf_op jit(solution)/shard_map/jit(dynamic_index_in_dim)/squeeze | solution.py:49
  61.8 1.5 %fusion.15 = bf16[512,512]{1,0:T(8,128)(2,1)S(1)} fusion(bf16[1,512,2048]{2,1,0:T(8,128)(2,1)S(1)} %copy-done.5, bf16[512,1024]{1,0:T(8,128)(2,1)S(1)} %get-tuple-element.23, bf16[512,1024]{1,0:T(8,128)(2,1)S(1)} %get-tuple-element.22, f32[512,512]{1,0:T(8,128)S(1)} %fusion.10), kind=kOutput, calls=%fused_computation.40 | convolution fusion | flops 1080295424 | bytes 5767168 | tf_op jit(solution)/shard_map/dot_general | solution.py:25
  63.2 0.1 copy-done.6
  63.4 1.3 %convolution_convert_fusion.2 = bf16[512,2048]{1,0:T(8,128)(2,1)S(1)} fusion(bf16[512,512]{1,0:T(8,128)(2,1)S(1)} %fusion.15, bf16[2048,512]{1,0:T(8,128)(2,1)S(1)} %bitcast.71), kind=kOutput, calls=%fused_computation.11 | convolution fusion | flops 1074790400 | bytes 4718592 | tf_op jit(solution)/shard_map/dot_general | solution.py:30
  64.7 0.6 fusion.48
  65.2 0.2 pad_maximum_fusion.3
  65.4 0.4 collective-permute-start.2
  65.8 3.9 %collective-permute-done.2 = bf16[1024,1024]{1,0:T(8,128)(2,1)S(1)} collective-permute-done((bf16[1024,1024]{1,0:T(8,128)(2,1)S(1)}, bf16[1024,1024]{1,0:T(8,128)(2,1)S(1)}, u32[]{:S(2)}, u32[]{:S(2)}) %collective-permute-start.2) | collective-permute-done | bytes 2097184 | tf_op jit(solution)/shard_map/ppermute | solution.py:54
  69.7 1.0 add_convert_fusion
  70.7 0.2 fusion.46
  70.9 5.9 %collective-permute-start.8 = (bf16[1024,128]{1,0:T(8,128)(2,1)S(1)}, bf16[1024,128]{1,0:T(8,128)(2,1)S(1)}, u32[]{:S(2)}, u32[]{:S(2)}) collective-permute-start(bf16[1024,128]{1,0:T(8,128)(2,1)S(1)} %get-tuple-element.5), channel_id=1, source_target_pairs={{0,224},{32,0},{64,32},{96,64},{128,96},{160,128},{192,160},{224,1... | collective-permute-start | bytes 786440 | tf_op jit(solution)/shard_map/ppermute | solution.py:70
  76.9 0.1 collective-permute-start.6
  77.0 4.1 %collective-permute-start.9 = (bf16[512,128]{1,0:T(8,128)(2,1)S(1)}, bf16[512,128]{1,0:T(8,128)(2,1)S(1)}, u32[]{:S(2)}, u32[]{:S(2)}) collective-permute-start(bf16[512,128]{1,0:T(8,128)(2,1)S(1)} %get-tuple-element.11), channel_id=1, source_target_pairs={{0,192},{32,224},{64,0},{96,32},{128,64},{160,96},{192,128},{224,1... | collective-permute-start | bytes 393224 | tf_op jit(solution)/shard_map/ppermute | solution.py:70
  81.1 0.9 collective-permute-start.3
  82.0 9.7 %collective-permute-done.6 = bf16[512,128]{1,0:T(8,128)(2,1)S(1)} collective-permute-done((bf16[512,128]{1,0:T(8,128)(2,1)S(1)}, bf16[512,128]{1,0:T(8,128)(2,1)S(1)}, u32[]{:S(2)}, u32[]{:S(2)}) %collective-permute-start.6) | collective-permute-done | bytes 131104 | tf_op jit(solution)/shard_map/ppermute | solution.py:70
  91.7 1.4 %collective-permute-start.4 = (bf16[1024,128]{1,0:T(8,128)(2,1)S(1)}, bf16[1024,128]{1,0:T(8,128)(2,1)S(1)}, u32[]{:S(2)}, u32[]{:S(2)}) collective-permute-start(bf16[1024,128]{1,0:T(8,128)(2,1)S(1)} %get-tuple-element.7), channel_id=1, source_target_pairs={{0,224},{32,0},{64,32},{96,64},{128,96},{160,128},{192,160},{224,1... | collective-permute-start | bytes 786440 | tf_op jit(solution)/shard_map/ppermute | solution.py:70
  93.1 0.2 add_convert_fusion.3
  93.3 2.8 %collective-permute-start.7 = (bf16[1024,128]{1,0:T(8,128)(2,1)S(1)}, bf16[1024,128]{1,0:T(8,128)(2,1)S(1)}, u32[]{:S(2)}, u32[]{:S(2)}) collective-permute-start(bf16[1024,128]{1,0:T(8,128)(2,1)S(1)} %get-tuple-element.8), channel_id=1, source_target_pairs={{0,64},{32,96},{64,128},{96,160},{128,192},{160,224},{192,0},{224,... | collective-permute-start | bytes 786440 | tf_op jit(solution)/shard_map/ppermute | solution.py:70
  96.0 1.5 %collective-permute-start.10 = (bf16[1024,128]{1,0:T(8,128)(2,1)S(1)}, bf16[1024,128]{1,0:T(8,128)(2,1)S(1)}, u32[]{:S(2)}, u32[]{:S(2)}) collective-permute-start(bf16[1024,128]{1,0:T(8,128)(2,1)S(1)} %get-tuple-element.9), channel_id=1, source_target_pairs={{0,192},{32,224},{64,0},{96,32},{128,64},{160,96},{192,128},{224,1... | collective-permute-start | bytes 786440 | tf_op jit(solution)/shard_map/ppermute | solution.py:70
  97.5 2.7 %fusion.1 = bf16[1,512,2048]{2,1,0:T(8,128)(2,1)} fusion(bf16[512,1024]{1,0:T(8,128)(2,1)S(1)} %get-tuple-element.23, bf16[512,1024]{1,0:T(8,128)(2,1)S(1)} %get-tuple-element.22, f32[512,512]{1,0:T(8,128)S(1)} %fusion.10), kind=kOutput, calls=%fused_computation.14 | convolution fusion | flops 1080295424 | bytes 5242880 | tf_op jit(solution)/shard_map/dot_general | solution.py:36
  100.1 0.3 collective-permute-done.3
  100.4 4.5 %collective-permute-done.4 = bf16[1024,128]{1,0:T(8,128)(2,1)S(1)} collective-permute-done((bf16[1024,128]{1,0:T(8,128)(2,1)S(1)}, bf16[1024,128]{1,0:T(8,128)(2,1)S(1)}, u32[]{:S(2)}, u32[]{:S(2)}) %collective-permute-start.4) | collective-permute-done | bytes 262176 | tf_op jit(solution)/shard_map/ppermute | solution.py:70
  104.9 0.1 collective-permute-done.7
  105.0 5.9 %collective-permute-done.10 = bf16[1024,128]{1,0:T(8,128)(2,1)S(1)} collective-permute-done((bf16[1024,128]{1,0:T(8,128)(2,1)S(1)}, bf16[1024,128]{1,0:T(8,128)(2,1)S(1)}, u32[]{:S(2)}, u32[]{:S(2)}) %collective-permute-start.10) | collective-permute-done | bytes 262176 | tf_op jit(solution)/shard_map/ppermute | solution.py:70
  110.9 0.2 add_convert_fusion.1
  111.1 0.7 pad_maximum_fusion.10
  111.9 4.8 %all-to-all-start.1 = ((bf16[16,32,256]{2,1,0:T(8,128)(2,1)}), bf16[16,32,256]{2,1,0:T(8,128)(2,1)S(1)}, u32[]{:S(2)}, u32[]{:S(2)}) async-start(bf16[16,32,256]{2,1,0:T(8,128)(2,1)} %pad_maximum_fusion.10), calls=%async_computation.1 | async-start | bytes 524288 | tf_op jit(solution)/shard_map/all_to_all | solution.py:149
  116.7 2.6 %fusion = bf16[1,2048,512]{2,1,0:T(8,128)(2,1)} fusion(bf16[512,512]{1,0:T(8,128)(2,1)S(1)} %fusion.15, bf16[512,1024]{1,0:T(8,128)(2,1)S(1)} %copy-done.9, bf16[512,1024]{1,0:T(8,128)(2,1)S(1)} %get-tuple-element.16), kind=kOutput, calls=%fused_computation.13 | convolution fusion | flops 1078984704 | bytes 4718592 | tf_op jit(solution)/shard_map/dot_general | solution.py:39
  119.3 4.8 %all-to-all-done.1 = bf16[16,32,256]{2,1,0:T(8,128)(2,1)S(1)} async-done(((bf16[16,32,256]{2,1,0:T(8,128)(2,1)}), bf16[16,32,256]{2,1,0:T(8,128)(2,1)S(1)}, u32[]{:S(2)}, u32[]{:S(2)}) %all-to-all-start.1) | async-done | bytes 262176 | tf_op jit(solution)/shard_map/all_to_all | solution.py:149
  124.1 0.3 fusion.27
  124.4 0.3 fusion.28
  124.7 0.9 multiply_reduce_fusion
  125.6 0.8 reduce_sum.45
  (32 shorter events, 0.3 us)
Async XLA Ops:
  0.6 6.1 %copy-start = (bf16[128,2048]{1,0:T(8,128)(2,1)S(1)}, bf16[128,2048]{1,0:T(8,128)(2,1)}, u32[]{:S(2)}) copy-start(bf16[128,2048]{1,0:T(8,128)(2,1)} %param.6) | copy-start | bytes 1572868
  42.2 2.5 %copy-start.3 = (bf16[1,2048,512]{2,1,0:T(8,128)(2,1)S(1)}, bf16[1,2048,512]{2,1,0:T(8,128)(2,1)}, u32[]{:S(2)}) copy-start(bf16[1,2048,512]{2,1,0:T(8,128)(2,1)} %param.10) | copy-start | bytes 6291460
  44.4 9.8 %collective-permute-start = (bf16[512,1024]{1,0:T(8,128)(2,1)}, bf16[512,1024]{1,0:T(8,128)(2,1)}, u32[]{:S(2)}, u32[]{:S(2)}) collective-permute-start(bf16[512,1024]{1,0:T(8,128)(2,1)} %get-tuple-element.18), channel_id=1, source_target_pairs={{0,16},{16,0},{1,17},{17,1},{2,18},{18,2},{3,19},{19,3},{4,20},{20... | collective-permute-start | bytes 3145736 | tf_op jit(solution)/shard_map/ppermute | solution.py:106
  51.3 8.3 %collective-permute-start.1 = (bf16[512,1024]{1,0:T(8,128)(2,1)}, bf16[512,1024]{1,0:T(8,128)(2,1)}, u32[]{:S(2)}, u32[]{:S(2)}) collective-permute-start(bf16[512,1024]{1,0:T(8,128)(2,1)} %get-tuple-element.21), channel_id=1, source_target_pairs={{0,16},{16,0},{1,17},{17,1},{2,18},{18,2},{3,19},{19,3},{4,20},{20... | collective-permute-start | bytes 3145736 | tf_op jit(solution)/shard_map/ppermute | solution.py:106
  52.6 1.5 %copy-start.2 = (bf16[1,512,1024]{2,1,0:T(8,128)(2,1)S(1)}, bf16[1,512,1024]{2,1,0:T(8,128)(2,1)}, u32[]{:S(2)}) copy-start(bf16[1,512,1024]{2,1,0:T(8,128)(2,1)} %get-tuple-element.19) | copy-start | bytes 3145732
  54.1 2.1 %copy-start.4 = (bf16[1,2048,512]{2,1,0:T(8,128)(2,1)S(1)}, bf16[1,2048,512]{2,1,0:T(8,128)(2,1)}, u32[]{:S(2)}) copy-start(bf16[1,2048,512]{2,1,0:T(8,128)(2,1)} %param.10) | copy-start | bytes 6291460
  56.3 1.3 %copy-start.8 = (bf16[512,1024]{1,0:T(8,128)(2,1)}, bf16[512,1024]{1,0:T(8,128)(2,1)S(1)}, u32[]{:S(2)}) copy-start(bf16[512,1024]{1,0:T(8,128)(2,1)S(1)} %get-tuple-element.17) | copy-start | bytes 3145732
  56.3 2.0 %copy-start.7 = (bf16[512,2,8,128]{0,3,2,1:T(8,128)(2,1)S(1)}, bf16[512,2,8,128]{0,3,2,1:T(8,128)(2,1)}, u32[]{:S(2)}) copy-start(bf16[512,2,8,128]{0,3,2,1:T(8,128)(2,1)} %copy.47) | copy-start | bytes 6291460
  58.3 1.3 %copy-start.1 = (bf16[1,512,1024]{2,1,0:T(8,128)(2,1)S(1)}, bf16[1,512,1024]{2,1,0:T(8,128)(2,1)}, u32[]{:S(2)}) copy-start(bf16[1,512,1024]{2,1,0:T(8,128)(2,1)} %get-tuple-element.20) | copy-start | bytes 3145732
  59.6 2.2 %copy-start.5 = (bf16[1,512,2048]{2,1,0:T(8,128)(2,1)S(1)}, bf16[1,512,2048]{2,1,0:T(8,128)(2,1)}, u32[]{:S(2)}) copy-start(bf16[1,512,2048]{2,1,0:T(8,128)(2,1)} %param.11) | copy-start | bytes 6291460
  61.8 1.6 %copy-start.6 = (bf16[2,8,128,512]{3,2,1,0:T(8,128)(2,1)S(1)}, bf16[2,8,128,512]{3,2,1,0:T(8,128)(2,1)}, u32[]{:S(2)}) copy-start(bf16[2,8,128,512]{3,2,1,0:T(8,128)(2,1)} %copy.48) | copy-start | bytes 6291460
  65.4 4.2 %collective-permute-start.2 = (bf16[1024,1024]{1,0:T(8,128)(2,1)S(1)}, bf16[1024,1024]{1,0:T(8,128)(2,1)S(1)}, u32[]{:S(2)}, u32[]{:S(2)}) collective-permute-start(bf16[1024,1024]{1,0:T(8,128)(2,1)S(1)} %pad_maximum_fusion.3), channel_id=1, source_target_pairs={{0,16},{16,0},{1,17},{17,1},{2,18},{18,2},{3,19},{19,3},{4,20},{20... | collective-permute-start | bytes 6291464 | tf_op jit(solution)/shard_map/ppermute | solution.py:54
  70.9 22.2 %collective-permute-start.8 = (bf16[1024,128]{1,0:T(8,128)(2,1)S(1)}, bf16[1024,128]{1,0:T(8,128)(2,1)S(1)}, u32[]{:S(2)}, u32[]{:S(2)}) collective-permute-start(bf16[1024,128]{1,0:T(8,128)(2,1)S(1)} %get-tuple-element.5), channel_id=1, source_target_pairs={{0,224},{32,0},{64,32},{96,64},{128,96},{160,128},{192,160},{224,1... | collective-permute-start | bytes 786440 | tf_op jit(solution)/shard_map/ppermute | solution.py:70
  76.8 16.3 %collective-permute-start.5 = (bf16[1024,128]{1,0:T(8,128)(2,1)S(1)}, bf16[1024,128]{1,0:T(8,128)(2,1)S(1)}, u32[]{:S(2)}, u32[]{:S(2)}) collective-permute-start(bf16[1024,128]{1,0:T(8,128)(2,1)S(1)} %get-tuple-element.6), channel_id=1, source_target_pairs={{0,32},{32,64},{64,96},{96,128},{128,160},{160,192},{192,224},{224... | collective-permute-start | bytes 786440 | tf_op jit(solution)/shard_map/ppermute | solution.py:70
  76.9 14.8 %collective-permute-start.6 = (bf16[512,128]{1,0:T(8,128)(2,1)S(1)}, bf16[512,128]{1,0:T(8,128)(2,1)S(1)}, u32[]{:S(2)}, u32[]{:S(2)}) collective-permute-start(bf16[512,128]{1,0:T(8,128)(2,1)S(1)} %get-tuple-element.10), channel_id=1, source_target_pairs={{0,64},{32,96},{64,128},{96,160},{128,192},{160,224},{192,0},{224,... | collective-permute-start | bytes 393224 | tf_op jit(solution)/shard_map/ppermute | solution.py:70
  77.0 16.1 %collective-permute-start.9 = (bf16[512,128]{1,0:T(8,128)(2,1)S(1)}, bf16[512,128]{1,0:T(8,128)(2,1)S(1)}, u32[]{:S(2)}, u32[]{:S(2)}) collective-permute-start(bf16[512,128]{1,0:T(8,128)(2,1)S(1)} %get-tuple-element.11), channel_id=1, source_target_pairs={{0,192},{32,224},{64,0},{96,32},{128,64},{160,96},{192,128},{224,1... | collective-permute-start | bytes 393224 | tf_op jit(solution)/shard_map/ppermute | solution.py:70
  81.1 19.3 %collective-permute-start.3 = (bf16[1024,128]{1,0:T(8,128)(2,1)S(1)}, bf16[1024,128]{1,0:T(8,128)(2,1)S(1)}, u32[]{:S(2)}, u32[]{:S(2)}) collective-permute-start(bf16[1024,128]{1,0:T(8,128)(2,1)S(1)} %get-tuple-element.4), channel_id=1, source_target_pairs={{0,32},{32,64},{64,96},{96,128},{128,160},{160,192},{192,224},{224... | collective-permute-start | bytes 786440 | tf_op jit(solution)/shard_map/ppermute | solution.py:70
  91.7 13.3 %collective-permute-start.4 = (bf16[1024,128]{1,0:T(8,128)(2,1)S(1)}, bf16[1024,128]{1,0:T(8,128)(2,1)S(1)}, u32[]{:S(2)}, u32[]{:S(2)}) collective-permute-start(bf16[1024,128]{1,0:T(8,128)(2,1)S(1)} %get-tuple-element.7), channel_id=1, source_target_pairs={{0,224},{32,0},{64,32},{96,64},{128,96},{160,128},{192,160},{224,1... | collective-permute-start | bytes 786440 | tf_op jit(solution)/shard_map/ppermute | solution.py:70
  93.3 11.8 %collective-permute-start.7 = (bf16[1024,128]{1,0:T(8,128)(2,1)S(1)}, bf16[1024,128]{1,0:T(8,128)(2,1)S(1)}, u32[]{:S(2)}, u32[]{:S(2)}) collective-permute-start(bf16[1024,128]{1,0:T(8,128)(2,1)S(1)} %get-tuple-element.8), channel_id=1, source_target_pairs={{0,64},{32,96},{64,128},{96,160},{128,192},{160,224},{192,0},{224,... | collective-permute-start | bytes 786440 | tf_op jit(solution)/shard_map/ppermute | solution.py:70
  96.0 14.9 %collective-permute-start.10 = (bf16[1024,128]{1,0:T(8,128)(2,1)S(1)}, bf16[1024,128]{1,0:T(8,128)(2,1)S(1)}, u32[]{:S(2)}, u32[]{:S(2)}) collective-permute-start(bf16[1024,128]{1,0:T(8,128)(2,1)S(1)} %get-tuple-element.9), channel_id=1, source_target_pairs={{0,192},{32,224},{64,0},{96,32},{128,64},{160,96},{192,128},{224,1... | collective-permute-start | bytes 786440 | tf_op jit(solution)/shard_map/ppermute | solution.py:70
  100.1 16.6 %copy-start.9 = (bf16[512,1024]{1,0:T(8,128)(2,1)S(1)}, bf16[512,1024]{1,0:T(8,128)(2,1)}, u32[]{:S(2)}) copy-start(bf16[512,1024]{1,0:T(8,128)(2,1)} %copy-done.8) | copy-start | bytes 3145732
  111.9 12.2 %all-to-all-start.1 = ((bf16[16,32,256]{2,1,0:T(8,128)(2,1)}), bf16[16,32,256]{2,1,0:T(8,128)(2,1)S(1)}, u32[]{:S(2)}, u32[]{:S(2)}) async-start(bf16[16,32,256]{2,1,0:T(8,128)(2,1)} %pad_maximum_fusion.10), calls=%async_computation.1 | async-start | bytes 524288 | tf_op jit(solution)/shard_map/all_to_all | solution.py:149

commit v7 on v5

--- a/solution.py
+++ b/solution.py
@@ -49,41 +49,38 @@
     return lax.dynamic_index_in_dim(stacked, index, axis=axis, keepdims=False)
 
 
-def reduce_over_rep(parts, n_z, n_core, cols):
+def reduce_round_a(part, n_z, n_core, cols):
     share = n_z * cols
-    got = lax.ppermute(
-        jnp.concatenate([p[:, share:] for p in parts], axis=0),
-        "core",
-        [(j, (j + 1) % n_core) for j in range(n_core)],
-    )
-    own = jnp.concatenate([p[:, :share] for p in parts], axis=0)
-    pair_sum = (own.astype(jnp.float32) + got.astype(jnp.float32)).astype(jnp.bfloat16)
+    got = lax.ppermute(part[:, share:], "core", [(j, (j + 1) % n_core) for j in range(n_core)])
+    pair_sum = (part[:, :share].astype(jnp.float32) + got.astype(jnp.float32)).astype(jnp.bfloat16)
     block = [pair_sum[:, k * cols : (k + 1) * cols] for k in range(n_z)]
     acc = block[0].astype(jnp.float32)
     if n_z != 8:
         for k in range(1, n_z):
-            moved = lax.ppermute(block[k], "z", [(j, (j + k) % n_z) for j in range(n_z)])
-            acc = acc + moved.astype(jnp.float32)
-        return acc
-
-    def shift(x, k):
-        return lax.ppermute(x, "z", [(j, (j + k) % n_z) for j in range(n_z)]).astype(jnp.float32)
-
+            acc = acc + shift_z(block[k], k, n_z)
+        return acc, None, None
     rows = pair_sum.shape[0]
     top = rows // 2
-    up_pair = shift(jnp.concatenate([block[1], block[3]], axis=0), 1)
-    down_pair = shift(jnp.concatenate([block[7], block[5]], axis=0), -1)
-    near_up, via_up = up_pair[:rows], up_pair[rows:]
-    near_down, via_down = down_pair[:rows], down_pair[rows:]
-    far_up = shift(block[4][:top], 2)
-    far_down = shift(block[4][top:], -2)
+    acc = acc + shift_z(block[1], 1, n_z) + shift_z(block[7], -1, n_z)
     zeros = jnp.zeros((rows - top, cols), jnp.float32)
-    agg_up = block[2].astype(jnp.float32) + via_up + jnp.concatenate([far_up, zeros], axis=0)
-    agg_down = block[6].astype(jnp.float32) + via_down + jnp.concatenate([zeros, far_down], axis=0)
-    acc = acc + near_up + near_down
-    acc = acc + shift(agg_up.astype(jnp.bfloat16), 2)
-    acc = acc + shift(agg_down.astype(jnp.bfloat16), -2)
-    return acc
+    far_up = jnp.concatenate([shift_z(block[4][:top], 2, n_z), zeros], axis=0)
+    far_down = jnp.concatenate([zeros, shift_z(block[4][top:], -2, n_z)], axis=0)
+    agg_up = block[2].astype(jnp.float32) + shift_z(block[3], 1, n_z) + far_up
+    agg_down = block[6].astype(jnp.float32) + shift_z(block[5], -1, n_z) + far_down
+    return acc, agg_up, agg_down
+
+
+def shift_z(x, k, n_z):
+    return lax.ppermute(x, "z", [(j, (j + k) % n_z) for j in range(n_z)]).astype(jnp.float32)
+
+
+def reduce_round_b(stages, n_z):
+    accs = jnp.concatenate([s[0] for s in stages], axis=0)
+    if stages[0][1] is None:
+        return accs
+    agg_up = jnp.concatenate([s[1] for s in stages], axis=0).astype(jnp.bfloat16)
+    agg_down = jnp.concatenate([s[2] for s in stages], axis=0).astype(jnp.bfloat16)
+    return accs + shift_z(agg_up, 2, n_z) + shift_z(agg_down, -2, n_z)
 
 
 def dispatch_rows(placements, sources, n_exp, capacity, n_core):
@@ -140,9 +137,8 @@
     out_part, dx_part, grad_up_e, grad_down_e = expert_math(
         rows_in, rows_grad, up_weight, down_weight, up_perm, down_perm
     )
-    acc = reduce_over_rep(
-        (out_part.astype(jnp.bfloat16), dx_part.astype(jnp.bfloat16)), n_z, n_core, cols
-    )
+    stages = [reduce_round_a(p.astype(jnp.bfloat16), n_z, n_core, cols) for p in (out_part, dx_part)]
+    acc = reduce_round_b(stages, n_z)
     slots = n_exp * capacity
     both = jnp.concatenate([acc[:slots], acc[slots:]], axis=1).astype(jnp.bfloat16)
     back_both = lax.all_to_all(

time: 129 us -> 130 us (level)
  starting transfers between devices: 21.2 us -> 33 us
  waiting for transfers between devices: 31.2 us -> 22.2 us
    ppermute x7 -> x16, starting transfers between devices: 16.4 us -> 28.2 us  [the longest x14 26.8 us: shift_z(): lax.ppermute(x, 'z', [(j, (j + k) % n_z) for j in range(n_z)])]
    ppermute x7 -> x16, waiting for transfers between devices: 26.4 us -> 17.4 us  [the longest x14 17.4 us: shift_z(): lax.ppermute(x, 'z', [(j, (j + k) % n_z) for j in range(n_z)])]
    unnamed x21 -> x19, local copies, waits for them, and re-layouts: 8.6 us -> 7.91 us
  transfers between devices with their start and end apart: 9 -> 18, of which waited for: 8 -> 8; matrix products, arithmetic and copies ran while one was open for 13% -> 16% of each run, Pallas kernels for 0% -> 0%
where the time goes in v7:
time: 130 us; the launch traced here: 129 us
  blocking collectives  34.3 us (26%)
  starting transfers between devices  33 us (25%)
  waiting for transfers between devices  22.2 us (17%)
  local copies, waits for them, and re-layouts  13.9 us (11%)
  other arithmetic  12.9 us (10%)
  matrix products  12.2 us (9%)
    all_to_all x1, blocking collectives, dispatch_rows(): lax.all_to_all(sent.reshape(n_exp, capacity, sent.shape[1]), 'exp', split...  34.3 us
    ppermute x14, starting transfers between devices, shift_z(): lax.ppermute(x, 'z', [(j, (j + k) % n_z) for j in range(n_z)])  26.8 us
    ppermute x14, waiting for transfers between devices, shift_z(): lax.ppermute(x, 'z', [(j, (j + k) % n_z) for j in range(n_z)])  17.4 us
    unnamed x19, local copies, waits for them, and re-layouts  7.91 us
    all_to_all x1, waiting for transfers between devices, local(): lax.all_to_all(both.reshape(n_exp, capacity, 2 * cols), 'exp', split_axis...  4.8 us
    all_to_all x1, starting transfers between devices, local(): lax.all_to_all(both.reshape(n_exp, capacity, 2 * cols), 'exp', split_axis...  4.78 us
    squeeze x1, other arithmetic, pick(): return lax.dynamic_index_in_dim(stacked, index, axis=axis, keepdims=False)  2.75 us
    dot_general x1, matrix products, expert_math(): lax.dot_general(hidden_units, rows_grad, (((0,), (0,)), ((), ())), prefer...  2.66 us
  transfers between devices with their start and end apart: 18, of which 8 were waited for; matrix products, arithmetic and copies ran while one was open for 16% of the time, Pallas kernels for 0%

profile of v7, /device:TPU:2, one launch (start us, length us, event | category | flops | bytes accessed | tf_op | source)
XLA Modules:
  0.0 129.4 jit_solution(6338354627446935769)
XLA Ops:
  0.6 0.8 copy.41
  1.5 0.1 eq.55
  1.6 0.1 reshape.78
  1.8 0.6 reduce-window.6
  2.4 0.2 slice_reduce_fusion
  2.7 0.1 reduce_sum.42
  2.9 1.0 dynamic-slice_convert_fusion
  3.9 0.4 mul.69
  4.3 0.7 mul.70
  5.1 0.1 mul.67
  5.4 0.4 convolution_convert_fusion.4
  5.9 0.5 convolution_convert_fusion.5
  6.4 0.2 pad_maximum_fusion
  6.6 34.3 %all_to_all.10 = bf16[16,32,2048]{2,1,0:T(8,128)(2,1)S(1)} all-to-all(bf16[16,32,2048]{2,1,0:T(8,128)(2,1)S(1)} %bitcast.62), channel_id=1, replica_groups=mesh['z'=8,'core'=2,'exp'=16] {'exp'}, dimensions={0} | all-to-all | bytes 4194304 | tf_op jit(solution)/shard_map/all_to_all | solution.py:96
  40.9 3.9 %copy.46 = bf16[1,512,2048]{1,2,0:T(8,128)(2,1)} copy(bf16[1,512,2048]{2,1,0:T(8,128)(2,1)} %param.11) | data formatting | bytes 4194304 | tf_op args[5]
  44.8 2.3 %fusion.7 = bf16[512,8,2,128]{0,3,2,1:T(8,128)(2,1)S(1)} fusion(s32[]{:T(128)S(6)} %select_n.50, bf16[512,8,2,128]{0,3,2,1:T(8,128)(2,1)} %bitcast.61), kind=kLoop, calls=%fused_computation.23 | loop fusion | flops 1048576 | bytes 4194308 | tf_op jit(solution)/shard_map/jit(_roll_dynamic)/concatenate | solution.py:123
  47.1 0.8 fusion.6
  47.9 1.5 %copy.47 = bf16[512,2,8,128]{0,3,2,1:T(8,128)(2,1)} copy(bf16[512,2,8,128]{0,3,1,2:T(8,128)(2,1)S(1)} %fusion.6) | data formatting | bytes 4194304 | tf_op jit(solution)/shard_map/transpose | solution.py:124
  49.4 0.8 copy-done.1
  50.3 0.8 fusion.4
  51.0 0.8 fusion.3
  51.8 1.5 %copy.48 = bf16[2,8,128,512]{3,2,1,0:T(8,128)(2,1)} copy(bf16[2,8,128,512]{3,2,0,1:T(8,128)(2,1)S(1)} %fusion.3) | data formatting | bytes 4194304 | tf_op jit(solution)/shard_map/transpose | solution.py:126
  53.3 2.8 %fusion.11 = (bf16[512,2048]{1,0:T(8,128)(2,1)S(1)}, bf16[512,2048]{1,0:T(8,128)(2,1)S(1)}) fusion(s32[]{:T(128)S(6)} %select_n.47, bf16[1,512,2048]{2,1,0:T(8,128)(2,1)S(1)} %bitcast.60, bf16[1,512,2048]{2,1,0:T(8,128)(2,1)} %bitcast.4, s32[]{:T(128)S(6)} %select_n.48), kind=kLoop, calls=%fused_computation.27 | loop fusion | flops 2097152 | bytes 8388616 | tf_op jit(solution)/shard_map/jit(dynamic_index_in_dim)/squeeze | solution.py:49
  56.1 0.6 fusion.44
  56.7 1.0 copy-done.2
  57.7 1.2 fusion.14
  58.9 0.3 copy-done.5
  59.3 1.3 %convolution_convert_fusion.3 = bf16[512,2048]{1,0:T(8,128)(2,1)S(1)} fusion(bf16[512,2048]{0,1:T(8,128)(2,1)S(1)} %bitcast.65, f32[512,512]{1,0:T(8,128)S(1)} %fusion.14), kind=kOutput, calls=%fused_computation.15 | convolution fusion | flops 1076101120 | bytes 5242880 | tf_op jit(solution)/shard_map/dot_general | solution.py:24
  60.7 0.8 collective-permute-start.1
  61.5 0.7 copy-done.3
  62.2 1.5 %fusion.19 = bf16[512,512]{1,0:T(8,128)(2,1)S(1)} fusion(bf16[1,512,2048]{2,1,0:T(8,128)(2,1)S(1)} %copy-done.3, bf16[512,1024]{1,0:T(8,128)(2,1)S(1)} %get-tuple-element.30, bf16[512,1024]{1,0:T(8,128)(2,1)S(1)} %get-tuple-element.7, f32[512,512]{1,0:T(8,128)S(1)} %fusion.14), kind=kOutput, calls=%fused_computation.40 | convolution fusion | flops 1080295424 | bytes 5767168 | tf_op jit(solution)/shard_map/dot_general | solution.py:25
  63.6 0.1 copy-done.4
  63.8 1.3 convolution_convert_fusion.2
  65.1 0.6 collective-permute-start.4
  65.7 0.4 add_convert_fusion.1
  66.2 5.9 %collective-permute-start.12 = (bf16[512,128]{1,0:T(8,128)(2,1)S(1)}, bf16[512,128]{1,0:T(8,128)(2,1)S(1)}, u32[]{:S(2)}, u32[]{:S(2)}) collective-permute-start(bf16[512,128]{1,0:T(8,128)(2,1)S(1)} %get-tuple-element.16), channel_id=1, source_target_pairs={{0,224},{32,0},{64,32},{96,64},{128,96},{160,128},{192,160},{224,1... | collective-permute-start | bytes 393224 | tf_op jit(solution)/shard_map/ppermute | solution.py:74
  72.2 3.2 %collective-permute-start.3 = (bf16[512,128]{1,0:T(8,128)(2,1)S(1)}, bf16[512,128]{1,0:T(8,128)(2,1)S(1)}, u32[]{:S(2)}, u32[]{:S(2)}) collective-permute-start(bf16[512,128]{1,0:T(8,128)(2,1)S(1)} %get-tuple-element.17), channel_id=1, source_target_pairs={{0,224},{32,0},{64,32},{96,64},{128,96},{160,128},{192,160},{224,1... | collective-permute-start | bytes 393224 | tf_op jit(solution)/shard_map/ppermute | solution.py:74
  75.4 0.3 collective-permute-start.13
  75.7 2.7 %collective-permute-start.8 = (bf16[256,128]{1,0:T(8,128)(2,1)S(1)}, bf16[256,128]{1,0:T(8,128)(2,1)S(1)}, u32[]{:S(2)}, u32[]{:S(2)}) collective-permute-start(bf16[256,128]{1,0:T(8,128)(2,1)S(1)} %get-tuple-element.13), channel_id=1, source_target_pairs={{0,64},{32,96},{64,128},{96,160},{128,192},{160,224},{192,0},{224,... | collective-permute-start | bytes 196616 | tf_op jit(solution)/shard_map/ppermute | solution.py:74
  78.5 0.4 add_convert_fusion
  78.9 1.8 %collective-permute-done.13 = bf16[256,128]{1,0:T(8,128)(2,1)S(1)} collective-permute-done((bf16[256,128]{1,0:T(8,128)(2,1)S(1)}, bf16[256,128]{1,0:T(8,128)(2,1)S(1)}, u32[]{:S(2)}, u32[]{:S(2)}) %collective-permute-start.13) | collective-permute-done | bytes 65568 | tf_op jit(solution)/shard_map/ppermute | solution.py:74
  80.7 1.5 %collective-permute-done.8 = bf16[256,128]{1,0:T(8,128)(2,1)S(1)} collective-permute-done((bf16[256,128]{1,0:T(8,128)(2,1)S(1)}, bf16[256,128]{1,0:T(8,128)(2,1)S(1)}, u32[]{:S(2)}, u32[]{:S(2)}) %collective-permute-start.8) | collective-permute-done | bytes 65568 | tf_op jit(solution)/shard_map/ppermute | solution.py:74
  82.2 2.9 %collective-permute-start.10 = (bf16[256,128]{1,0:T(8,128)(2,1)S(1)}, bf16[256,128]{1,0:T(8,128)(2,1)S(1)}, u32[]{:S(2)}, u32[]{:S(2)}) collective-permute-start(bf16[256,128]{1,0:T(8,128)(2,1)S(1)} %get-tuple-element.22), channel_id=1, source_target_pairs={{0,64},{32,96},{64,128},{96,160},{128,192},{160,224},{192,0},{224,... | collective-permute-start | bytes 196616 | tf_op jit(solution)/shard_map/ppermute | solution.py:74
  85.2 4.6 %collective-permute-done.10 = bf16[256,128]{1,0:T(8,128)(2,1)S(1)} collective-permute-done((bf16[256,128]{1,0:T(8,128)(2,1)S(1)}, bf16[256,128]{1,0:T(8,128)(2,1)S(1)}, u32[]{:S(2)}, u32[]{:S(2)}) %collective-permute-start.10) | collective-permute-done | bytes 65568 | tf_op jit(solution)/shard_map/ppermute | solution.py:74
  89.8 2.4 %collective-permute-start.14 = (bf16[512,128]{1,0:T(8,128)(2,1)S(1)}, bf16[512,128]{1,0:T(8,128)(2,1)S(1)}, u32[]{:S(2)}, u32[]{:S(2)}) collective-permute-start(bf16[512,128]{1,0:T(8,128)(2,1)S(1)} %get-tuple-element.25), channel_id=1, source_target_pairs={{0,224},{32,0},{64,32},{96,64},{128,96},{160,128},{192,160},{224,1... | collective-permute-start | bytes 393224 | tf_op jit(solution)/shard_map/ppermute | solution.py:74
  92.2 3.2 %collective-permute-start.6 = (bf16[512,128]{1,0:T(8,128)(2,1)S(1)}, bf16[512,128]{1,0:T(8,128)(2,1)S(1)}, u32[]{:S(2)}, u32[]{:S(2)}) collective-permute-start(bf16[512,128]{1,0:T(8,128)(2,1)S(1)} %get-tuple-element.26), channel_id=1, source_target_pairs={{0,224},{32,0},{64,32},{96,64},{128,96},{160,128},{192,160},{224,1... | collective-permute-start | bytes 393224 | tf_op jit(solution)/shard_map/ppermute | solution.py:74
  95.5 1.8 %collective-permute-start.15 = (bf16[256,128]{1,0:T(8,128)(2,1)S(1)}, bf16[256,128]{1,0:T(8,128)(2,1)S(1)}, u32[]{:S(2)}, u32[]{:S(2)}) collective-permute-start(bf16[256,128]{1,0:T(8,128)(2,1)S(1)} %get-tuple-element.23), channel_id=1, source_target_pairs={{0,192},{32,224},{64,0},{96,32},{128,64},{160,96},{192,128},{224,1... | collective-permute-start | bytes 196616 | tf_op jit(solution)/shard_map/ppermute | solution.py:74
  97.2 0.1 add_convert_fusion.5
  97.4 3.5 %collective-permute-done.15 = bf16[256,128]{1,0:T(8,128)(2,1)S(1)} collective-permute-done((bf16[256,128]{1,0:T(8,128)(2,1)S(1)}, bf16[256,128]{1,0:T(8,128)(2,1)S(1)}, u32[]{:S(2)}, u32[]{:S(2)}) %collective-permute-start.15) | collective-permute-done | bytes 65568 | tf_op jit(solution)/shard_map/ppermute | solution.py:74
  100.9 0.8 collective-permute-done.9
  101.6 0.1 add_convert_fusion.4
  101.8 0.4 collective-permute-start.11
  102.2 3.9 %collective-permute-start.16 = (bf16[1024,128]{1,0:T(8,128)(2,1)S(1)}, bf16[1024,128]{1,0:T(8,128)(2,1)S(1)}, u32[]{:S(2)}, u32[]{:S(2)}) collective-permute-start(bf16[1024,128]{1,0:T(8,128)(2,1)S(1)} %pad_maximum_fusion.10), channel_id=1, source_target_pairs={{0,192},{32,224},{64,0},{96,32},{128,64},{160,96},{192,128},{224,1... | collective-permute-start | bytes 786440 | tf_op jit(solution)/shard_map/ppermute | solution.py:74
  106.1 2.7 %fusion.1 = bf16[1,512,2048]{2,1,0:T(8,128)(2,1)} fusion(bf16[512,1024]{1,0:T(8,128)(2,1)S(1)} %get-tuple-element.30, bf16[512,1024]{1,0:T(8,128)(2,1)S(1)} %get-tuple-element.7, f32[512,512]{1,0:T(8,128)S(1)} %fusion.14), kind=kOutput, calls=%fused_computation.17 | convolution fusion | flops 1080295424 | bytes 5242880 | tf_op jit(solution)/shard_map/dot_general | solution.py:36
  108.8 5.0 %collective-permute-done.11 = bf16[1024,128]{1,0:T(8,128)(2,1)S(1)} collective-permute-done((bf16[1024,128]{1,0:T(8,128)(2,1)S(1)}, bf16[1024,128]{1,0:T(8,128)(2,1)S(1)}, u32[]{:S(2)}, u32[]{:S(2)}) %collective-permute-start.11) | collective-permute-done | bytes 262176 | tf_op jit(solution)/shard_map/ppermute | solution.py:74
  113.8 0.3 collective-permute-done.16
  114.2 0.7 pad_maximum_fusion.11
  114.9 4.8 %all-to-all-start.1 = ((bf16[16,32,256]{2,1,0:T(8,128)(2,1)}), bf16[16,32,256]{2,1,0:T(8,128)(2,1)S(1)}, u32[]{:S(2)}, u32[]{:S(2)}) async-start(bf16[16,32,256]{2,1,0:T(8,128)(2,1)} %pad_maximum_fusion.11), calls=%async_computation.1 | async-start | bytes 524288 | tf_op jit(solution)/shard_map/all_to_all | solution.py:144
  119.7 2.6 %fusion = bf16[1,2048,512]{2,1,0:T(8,128)(2,1)} fusion(bf16[512,512]{1,0:T(8,128)(2,1)S(1)} %fusion.19, bf16[512,1024]{1,0:T(8,128)(2,1)S(1)} %get-tuple-element.31, bf16[512,1024]{1,0:T(8,128)(2,1)S(1)} %get-tuple-element.6), kind=kOutput, calls=%fused_computation.16 | convolution fusion | flops 1078984704 | bytes 4718592 | tf_op jit(solution)/shard_map/dot_general | solution.py:39
  122.3 4.8 %all-to-all-done.1 = bf16[16,32,256]{2,1,0:T(8,128)(2,1)S(1)} async-done(((bf16[16,32,256]{2,1,0:T(8,128)(2,1)}), bf16[16,32,256]{2,1,0:T(8,128)(2,1)S(1)}, u32[]{:S(2)}, u32[]{:S(2)}) %all-to-all-start.1) | async-done | bytes 262176 | tf_op jit(solution)/shard_map/all_to_all | solution.py:144
  127.1 0.3 fusion.25
  127.4 0.3 fusion.26
  127.7 0.9 multiply_reduce_fusion
  128.6 0.8 reduce_sum.45
  (45 shorter events, 1.1 us)
Async XLA Ops:
  0.6 4.8 %copy-start = (bf16[128,2048]{1,0:T(8,128)(2,1)S(1)}, bf16[128,2048]{1,0:T(8,128)(2,1)}, u32[]{:S(2)}) copy-start(bf16[128,2048]{1,0:T(8,128)(2,1)} %param.6) | copy-start | bytes 1572868
  2.9 2.1 %copy-start.7 = (f32[128,2]{0,1:T(2,128)S(1)}, f32[128,2]{0,1:T(2,128)}, u32[]{:S(2)}) copy-start(f32[128,2]{0,1:T(2,128)} %param.8) | copy-start | bytes 3076
  3.9 1.4 %copy-start.6 = (s32[128,2]{0,1:T(2,128)S(1)}, s32[128,2]{0,1:T(2,128)}, u32[]{:S(2)}) copy-start(s32[128,2]{0,1:T(2,128)} %param.7) | copy-start | bytes 3076
  40.9 12.4 %collective-permute-start = (bf16[512,2048]{1,0:T(8,128)(2,1)S(1)}, bf16[512,2048]{1,0:T(8,128)(2,1)}, u32[]{:S(2)}, u32[]{:S(2)}) collective-permute-start(bf16[512,2048]{1,0:T(8,128)(2,1)S(1)} %bitcast.59), channel_id=1, source_target_pairs={{0,16},{16,0},{1,17},{17,1},{2,18},{18,2},{3,19},{19,3},{4,20},{20... | collective-permute-start | bytes 6291464 | tf_op jit(solution)/shard_map/ppermute | solution.py:99
  47.9 2.4 %copy-start.1 = (bf16[1,2048,512]{2,1,0:T(8,128)(2,1)S(1)}, bf16[1,2048,512]{2,1,0:T(8,128)(2,1)}, u32[]{:S(2)}) copy-start(bf16[1,2048,512]{2,1,0:T(8,128)(2,1)} %param.10) | copy-start | bytes 6291460
  56.1 1.6 %copy-start.2 = (bf16[1,2048,512]{2,1,0:T(8,128)(2,1)S(1)}, bf16[1,2048,512]{2,1,0:T(8,128)(2,1)}, u32[]{:S(2)}) copy-start(bf16[1,2048,512]{2,1,0:T(8,128)(2,1)} %param.10) | copy-start | bytes 6291460
  57.7 1.6 %copy-start.5 = (bf16[512,2,8,128]{0,3,2,1:T(8,128)(2,1)S(1)}, bf16[512,2,8,128]{0,3,2,1:T(8,128)(2,1)}, u32[]{:S(2)}) copy-start(bf16[512,2,8,128]{0,3,2,1:T(8,128)(2,1)} %copy.47) | copy-start | bytes 6291460
  60.6 1.6 %copy-start.3 = (bf16[1,512,2048]{2,1,0:T(8,128)(2,1)S(1)}, bf16[1,512,2048]{2,1,0:T(8,128)(2,1)}, u32[]{:S(2)}) copy-start(bf16[1,512,2048]{2,1,0:T(8,128)(2,1)} %param.11) | copy-start | bytes 6291460
  60.7 5.0 %collective-permute-start.1 = (bf16[512,1024]{1,0:T(8,128)(2,1)S(1)}, bf16[512,1024]{1,0:T(8,128)(2,1)S(1)}, u32[]{:S(2)}, u32[]{:S(2)}) collective-permute-start(bf16[512,1024]{1,0:T(8,128)(2,1)S(1)} %slice.140), channel_id=1, source_target_pairs={{0,16},{16,0},{1,17},{17,1},{2,18},{18,2},{3,19},{19,3},{4,20},{20... | collective-permute-start | bytes 3145736 | tf_op jit(solution)/shard_map/ppermute | solution.py:54
  62.2 1.6 %copy-start.4 = (bf16[2,8,128,512]{3,2,1,0:T(8,128)(2,1)S(1)}, bf16[2,8,128,512]{3,2,1,0:T(8,128)(2,1)}, u32[]{:S(2)}) copy-start(bf16[2,8,128,512]{3,2,1,0:T(8,128)(2,1)} %copy.48) | copy-start | bytes 6291460
  65.1 10.6 %collective-permute-start.4 = (bf16[512,1024]{1,0:T(8,128)(2,1)S(1)}, bf16[512,1024]{1,0:T(8,128)(2,1)S(1)}, u32[]{:S(2)}, u32[]{:S(2)}) collective-permute-start(bf16[512,1024]{1,0:T(8,128)(2,1)S(1)} %slice.147), channel_id=1, source_target_pairs={{0,16},{16,0},{1,17},{17,1},{2,18},{18,2},{3,19},{19,3},{4,20},{20... | collective-permute-start | bytes 3145736 | tf_op jit(solution)/shard_map/ppermute | solution.py:54
  66.2 26.0 %collective-permute-start.12 = (bf16[512,128]{1,0:T(8,128)(2,1)S(1)}, bf16[512,128]{1,0:T(8,128)(2,1)S(1)}, u32[]{:S(2)}, u32[]{:S(2)}) collective-permute-start(bf16[512,128]{1,0:T(8,128)(2,1)S(1)} %get-tuple-element.16), channel_id=1, source_target_pairs={{0,224},{32,0},{64,32},{96,64},{128,96},{160,128},{192,160},{224,1... | collective-permute-start | bytes 393224 | tf_op jit(solution)/shard_map/ppermute | solution.py:74
  72.2 20.1 %collective-permute-start.2 = (bf16[512,128]{1,0:T(8,128)(2,1)S(1)}, bf16[512,128]{1,0:T(8,128)(2,1)S(1)}, u32[]{:S(2)}, u32[]{:S(2)}) collective-permute-start(bf16[512,128]{1,0:T(8,128)(2,1)S(1)} %get-tuple-element.18), channel_id=1, source_target_pairs={{0,32},{32,64},{64,96},{96,128},{128,160},{160,192},{192,224},{224... | collective-permute-start | bytes 393224 | tf_op jit(solution)/shard_map/ppermute | solution.py:74
  72.2 23.3 %collective-permute-start.3 = (bf16[512,128]{1,0:T(8,128)(2,1)S(1)}, bf16[512,128]{1,0:T(8,128)(2,1)S(1)}, u32[]{:S(2)}, u32[]{:S(2)}) collective-permute-start(bf16[512,128]{1,0:T(8,128)(2,1)S(1)} %get-tuple-element.17), channel_id=1, source_target_pairs={{0,224},{32,0},{64,32},{96,64},{128,96},{160,128},{192,160},{224,1... | collective-permute-start | bytes 393224 | tf_op jit(solution)/shard_map/ppermute | solution.py:74
  75.4 5.3 %collective-permute-start.13 = (bf16[256,128]{1,0:T(8,128)(2,1)S(1)}, bf16[256,128]{1,0:T(8,128)(2,1)S(1)}, u32[]{:S(2)}, u32[]{:S(2)}) collective-permute-start(bf16[256,128]{1,0:T(8,128)(2,1)S(1)} %get-tuple-element.14), channel_id=1, source_target_pairs={{0,192},{32,224},{64,0},{96,32},{128,64},{160,96},{192,128},{224,1... | collective-permute-start | bytes 196616 | tf_op jit(solution)/shard_map/ppermute | solution.py:74
  75.7 6.5 %collective-permute-start.8 = (bf16[256,128]{1,0:T(8,128)(2,1)S(1)}, bf16[256,128]{1,0:T(8,128)(2,1)S(1)}, u32[]{:S(2)}, u32[]{:S(2)}) collective-permute-start(bf16[256,128]{1,0:T(8,128)(2,1)S(1)} %get-tuple-element.13), channel_id=1, source_target_pairs={{0,64},{32,96},{64,128},{96,160},{128,192},{160,224},{192,0},{224,... | collective-permute-start | bytes 196616 | tf_op jit(solution)/shard_map/ppermute | solution.py:74
  80.7 14.7 %collective-permute-start.7 = (bf16[512,128]{1,0:T(8,128)(2,1)S(1)}, bf16[512,128]{1,0:T(8,128)(2,1)S(1)}, u32[]{:S(2)}, u32[]{:S(2)}) collective-permute-start(bf16[512,128]{1,0:T(8,128)(2,1)S(1)} %get-tuple-element.15), channel_id=1, source_target_pairs={{0,32},{32,64},{64,96},{96,128},{128,160},{160,192},{192,224},{224... | collective-permute-start | bytes 393224 | tf_op jit(solution)/shard_map/ppermute | solution.py:74
  82.2 7.6 %collective-permute-start.10 = (bf16[256,128]{1,0:T(8,128)(2,1)S(1)}, bf16[256,128]{1,0:T(8,128)(2,1)S(1)}, u32[]{:S(2)}, u32[]{:S(2)}) collective-permute-start(bf16[256,128]{1,0:T(8,128)(2,1)S(1)} %get-tuple-element.22), channel_id=1, source_target_pairs={{0,64},{32,96},{64,128},{96,160},{128,192},{160,224},{192,0},{224,... | collective-permute-start | bytes 196616 | tf_op jit(solution)/shard_map/ppermute | solution.py:74
  89.8 11.1 %collective-permute-start.14 = (bf16[512,128]{1,0:T(8,128)(2,1)S(1)}, bf16[512,128]{1,0:T(8,128)(2,1)S(1)}, u32[]{:S(2)}, u32[]{:S(2)}) collective-permute-start(bf16[512,128]{1,0:T(8,128)(2,1)S(1)} %get-tuple-element.25), channel_id=1, source_target_pairs={{0,224},{32,0},{64,32},{96,64},{128,96},{160,128},{192,160},{224,1... | collective-permute-start | bytes 393224 | tf_op jit(solution)/shard_map/ppermute | solution.py:74
  92.2 8.6 %collective-permute-start.5 = (bf16[512,128]{1,0:T(8,128)(2,1)S(1)}, bf16[512,128]{1,0:T(8,128)(2,1)S(1)}, u32[]{:S(2)}, u32[]{:S(2)}) collective-permute-start(bf16[512,128]{1,0:T(8,128)(2,1)S(1)} %get-tuple-element.27), channel_id=1, source_target_pairs={{0,32},{32,64},{64,96},{96,128},{128,160},{160,192},{192,224},{224... | collective-permute-start | bytes 393224 | tf_op jit(solution)/shard_map/ppermute | solution.py:74
  92.2 8.6 %collective-permute-start.6 = (bf16[512,128]{1,0:T(8,128)(2,1)S(1)}, bf16[512,128]{1,0:T(8,128)(2,1)S(1)}, u32[]{:S(2)}, u32[]{:S(2)}) collective-permute-start(bf16[512,128]{1,0:T(8,128)(2,1)S(1)} %get-tuple-element.26), channel_id=1, source_target_pairs={{0,224},{32,0},{64,32},{96,64},{128,96},{160,128},{192,160},{224,1... | collective-permute-start | bytes 393224 | tf_op jit(solution)/shard_map/ppermute | solution.py:74
  95.5 6.2 %collective-permute-start.9 = (bf16[512,128]{1,0:T(8,128)(2,1)S(1)}, bf16[512,128]{1,0:T(8,128)(2,1)S(1)}, u32[]{:S(2)}, u32[]{:S(2)}) collective-permute-start(bf16[512,128]{1,0:T(8,128)(2,1)S(1)} %get-tuple-element.24), channel_id=1, source_target_pairs={{0,32},{32,64},{64,96},{96,128},{128,160},{160,192},{192,224},{224... | collective-permute-start | bytes 393224 | tf_op jit(solution)/shard_map/ppermute | solution.py:74
  95.5 5.4 %collective-permute-start.15 = (bf16[256,128]{1,0:T(8,128)(2,1)S(1)}, bf16[256,128]{1,0:T(8,128)(2,1)S(1)}, u32[]{:S(2)}, u32[]{:S(2)}) collective-permute-start(bf16[256,128]{1,0:T(8,128)(2,1)S(1)} %get-tuple-element.23), channel_id=1, source_target_pairs={{0,192},{32,224},{64,0},{96,32},{128,64},{160,96},{192,128},{224,1... | collective-permute-start | bytes 196616 | tf_op jit(solution)/shard_map/ppermute | solution.py:74
  101.8 12.0 %collective-permute-start.11 = (bf16[1024,128]{1,0:T(8,128)(2,1)S(1)}, bf16[1024,128]{1,0:T(8,128)(2,1)S(1)}, u32[]{:S(2)}, u32[]{:S(2)}) collective-permute-start(bf16[1024,128]{1,0:T(8,128)(2,1)S(1)} %pad_maximum_fusion.9), channel_id=1, source_target_pairs={{0,64},{32,96},{64,128},{96,160},{128,192},{160,224},{192,0},{224,... | collective-permute-start | bytes 786440 | tf_op jit(solution)/shard_map/ppermute | solution.py:74
  102.2 11.8 %collective-permute-start.16 = (bf16[1024,128]{1,0:T(8,128)(2,1)S(1)}, bf16[1024,128]{1,0:T(8,128)(2,1)S(1)}, u32[]{:S(2)}, u32[]{:S(2)}) collective-permute-start(bf16[1024,128]{1,0:T(8,128)(2,1)S(1)} %pad_maximum_fusion.10), channel_id=1, source_target_pairs={{0,192},{32,224},{64,0},{96,32},{128,64},{160,96},{192,128},{224,1... | collective-permute-start | bytes 786440 | tf_op jit(solution)/shard_map/ppermute | solution.py:74
  114.9 12.2 %all-to-all-start.1 = ((bf16[16,32,256]{2,1,0:T(8,128)(2,1)}), bf16[16,32,256]{2,1,0:T(8,128)(2,1)S(1)}, u32[]{:S(2)}, u32[]{:S(2)}) async-start(bf16[16,32,256]{2,1,0:T(8,128)(2,1)} %pad_maximum_fusion.11), calls=%async_computation.1 | async-start | bytes 524288 | tf_op jit(solution)/shard_map/all_to_all | solution.py:144

commit v8 on v4

--- a/solution.py
+++ b/solution.py
@@ -49,16 +49,30 @@
     return lax.dynamic_index_in_dim(stacked, index, axis=axis, keepdims=False)
 
 
+def block_order(n_z):
+    return (1, 7, 3, 5, 4, 2, 6, 0) if n_z == 8 else tuple(range(n_z))
+
+
 def reduce_over_rep(parts, n_z, n_core, cols):
     share = n_z * cols
-    got = lax.ppermute(
-        jnp.concatenate([p[:, share:] for p in parts], axis=0),
-        "core",
-        [(j, (j + 1) % n_core) for j in range(n_core)],
-    )
-    own = jnp.concatenate([p[:, :share] for p in parts], axis=0)
-    pair_sum = (own.astype(jnp.float32) + got.astype(jnp.float32)).astype(jnp.bfloat16)
-    block = [pair_sum[:, k * cols : (k + 1) * cols] for k in range(n_z)]
+    order = block_order(n_z)
+    lead = 5 if n_z == 8 else n_z
+    swap = [(j, (j + 1) % n_core) for j in range(n_core)]
+    sums = []
+    for lo, hi in ((0, lead), (lead, n_z)):
+        if lo == hi:
+            continue
+        got = lax.ppermute(
+            jnp.concatenate([p[:, share + lo * cols : share + hi * cols] for p in parts], axis=0),
+            "core",
+            swap,
+        )
+        own = jnp.concatenate([p[:, lo * cols : hi * cols] for p in parts], axis=0)
+        sums.append((own.astype(jnp.float32) + got.astype(jnp.float32)).astype(jnp.bfloat16))
+    block = {}
+    for i, offset in enumerate(order):
+        src_sum, at = (sums[0], i) if i < lead else (sums[1], i - lead)
+        block[offset] = src_sum[:, at * cols : (at + 1) * cols]
     acc = block[0].astype(jnp.float32)
     if n_z != 8:
         for k in range(1, n_z):
@@ -69,7 +83,7 @@
     def shift(x, k):
         return lax.ppermute(x, "z", [(j, (j + k) % n_z) for j in range(n_z)]).astype(jnp.float32)
 
-    rows = pair_sum.shape[0]
+    rows = acc.shape[0]
     top = rows // 2
     near_up = shift(block[1], 1)
     near_down = shift(block[7], -1)
@@ -123,9 +137,12 @@
     ff_local = up_weight.shape[1]
     zi = lax.axis_index("z")
     core = lax.axis_index("core")
+    order = jnp.array(block_order(n_z), jnp.int32)
     down_blocks = jnp.roll(down_weight.reshape(ff_local, n_z, n_core, cols), (-zi, -core), (1, 2))
+    down_blocks = jnp.take(down_blocks, order, axis=1)
     down_perm = down_blocks.transpose(0, 2, 1, 3).reshape(ff_local, width)
     up_blocks = jnp.roll(up_weight.reshape(n_z, n_core, cols, ff_local), (-zi, -core), (0, 1))
+    up_blocks = jnp.take(up_blocks, order, axis=0)
     up_perm = up_blocks.transpose(1, 0, 2, 3).reshape(width, ff_local)
     share = width // n_core
     tok_half = lax.dynamic_slice_in_dim(tokens, core * share, share, 1)

time: 126 us -> 142 us (1.13)
  local copies, waits for them, and re-layouts: 14.7 us -> 28.7 us
  waiting for transfers between devices: 28.2 us -> 21.7 us
  other arithmetic: 13.3 us -> 17.8 us
  starting transfers between devices: 21.5 us -> 24.1 us
    gather x0 -> x2, local copies, waits for them, and re-layouts: none -> 7.31 us  [the longest x1 3.72 us: local(): down_blocks = jnp.take(down_blocks, order, axis=1)]
    select_n x0 -> x2, local copies, waits for them, and re-layouts: none -> 7.01 us  [the longest x1 3.91 us: local(): down_blocks = jnp.take(down_blocks, order, axis=1)]
    ppermute x8, waiting for transfers between devices: 19.6 us -> 14.9 us  [shift(): lax.ppermute(x, 'z', [(j, (j + k) % n_z) for j in range(n_z)])]
    another operation x1 -> x2, local copies, waits for them, and re-layouts: 0.01 us -> 3.9 us  [the longest x1 3.9 us: local(): down_weight.reshape(ff_local, n_z, n_core, cols)]
    concatenate x1 -> x2, other arithmetic: 0.75 us -> 4.43 us  [local(): jnp.roll(up_weight.reshape(n_z, n_core, cols, ff_local), (-zi, -core), (0...]
    transpose x2 -> x0, local copies, waits for them, and re-layouts: 3.05 us -> none  [the longest x1 1.53 us: local(): up_perm = up_blocks.transpose(1, 0, 2, 3).reshape(width, ff_local)]
    ppermute x8, starting transfers between devices: 16.1 us -> 18.4 us  [shift(): lax.ppermute(x, 'z', [(j, (j + k) % n_z) for j in range(n_z)])]
    concatenate x1 -> x2, other arithmetic: 2.34 us -> 4.42 us  [local(): jnp.roll(down_weight.reshape(ff_local, n_z, n_core, cols), (-zi, -core),...]
  transfers between devices with their start and end apart: 11 -> 12, of which waited for: 6 -> 6; matrix products, arithmetic and copies ran while one was open for 14% -> 27% of each run, Pallas kernels for 0% -> 0%
where the time goes in v8:
time: 142 us; the launch traced here: 140 us
  blocking collectives  34.3 us (24%)
  local copies, waits for them, and re-layouts  28.7 us (20%)
  starting transfers between devices  24.1 us (17%)
  waiting for transfers between devices  21.7 us (15%)
  other arithmetic  17.8 us (13%)
  matrix products  12.2 us (9%)
    all_to_all x1, blocking collectives, dispatch_rows(): lax.all_to_all(sent.reshape(n_exp, capacity, sent.shape[1]), 'exp', split...  34.3 us
    ppermute x8, starting transfers between devices, shift(): lax.ppermute(x, 'z', [(j, (j + k) % n_z) for j in range(n_z)])  18.4 us
    ppermute x8, waiting for transfers between devices, shift(): lax.ppermute(x, 'z', [(j, (j + k) % n_z) for j in range(n_z)])  14.9 us
    unnamed x17, local copies, waits for them, and re-layouts  7.32 us
    all_to_all x1, waiting for transfers between devices, local(): lax.all_to_all(both.reshape(n_exp, capacity, 2 * cols), 'exp', split_axis...  4.79 us
    all_to_all x1, starting transfers between devices, local(): lax.all_to_all(both.reshape(n_exp, capacity, 2 * cols), 'exp', split_axis...  4.77 us
    concatenate x2, other arithmetic, local(): jnp.roll(up_weight.reshape(n_z, n_core, cols, ff_local), (-zi, -core), (0...  4.43 us
    concatenate x2, other arithmetic, local(): jnp.roll(down_weight.reshape(ff_local, n_z, n_core, cols), (-zi, -core),...  4.42 us
  transfers between devices with their start and end apart: 12, of which 6 were waited for; matrix products, arithmetic and copies ran while one was open for 27% of the time, Pallas kernels for 0%

profile of v8, /device:TPU:2, one launch (start us, length us, event | category | flops | bytes accessed | tf_op | source)
XLA Modules:
  0.0 139.7 jit_solution(6128207527945999152)
XLA Ops:
  0.7 0.8 copy.55
  1.5 0.1 reshape.83
  1.6 0.1 eq.55
  1.8 0.6 reduce-window.6
  2.4 0.2 slice_reduce_fusion
  2.7 0.1 reduce_sum.42
  2.9 0.8 copy.54
  3.8 0.7 multiply_add_fusion
  4.6 1.0 dynamic-slice_convert_fusion
  5.6 0.4 mul.69
  6.0 0.7 mul.70
  6.7 0.4 convolution_convert_fusion.4
  7.2 0.5 convolution_convert_fusion.5
  7.7 0.2 pad_maximum_fusion
  7.9 34.3 %all_to_all.10 = bf16[16,32,2048]{2,1,0:T(8,128)(2,1)S(1)} all-to-all(bf16[16,32,2048]{2,1,0:T(8,128)(2,1)S(1)} %bitcast.59), channel_id=1, replica_groups=mesh['z'=8,'core'=2,'exp'=16] {'exp'}, dimensions={0} | all-to-all | bytes 4194304 | tf_op jit(solution)/shard_map/all_to_all | solution.py:113
  42.2 2.4 %fusion.3 = bf16[8,2,128,512]{3,2,1,0:T(8,128)(2,1)S(1)} fusion(s32[]{:T(128)S(6)} %select_n.74, bf16[8,2,128,512]{3,2,1,0:T(8,128)(2,1)} %bitcast.63), kind=kLoop, calls=%fused_computation.22 | loop fusion | flops 1048576 | bytes 4194308 | tf_op jit(solution)/shard_map/jit(_roll_dynamic)/concatenate | solution.py:144
  44.6 2.1 %fusion.2 = bf16[8,2,128,512]{3,2,1,0:T(8,128)(2,1)} fusion(s32[]{:T(128)S(6)} %select_n.76, bf16[8,2,128,512]{3,2,1,0:T(8,128)(2,1)S(1)} %fusion.3), kind=kLoop, calls=%fused_computation.21 | loop fusion | flops 1048576 | bytes 4194308 | tf_op jit(solution)/shard_map/jit(_roll_dynamic)/concatenate | solution.py:144
  46.6 3.6 %gather_fusion.1 = bf16[8,2,128,512]{3,2,1,0:T(8,128)(2,1)} fusion(bf16[8,2,128,512]{3,2,1,0:T(8,128)(2,1)} %fusion.2, s32[1024]{0:T(1024)S(1)} %pad_clamp_fusion), kind=kCustom, calls=%fused_computation.1 | custom fusion | bytes 4194336 | tf_op jit(solution)/shard_map/jit(_take)/gather | solution.py:145
  50.2 3.1 %copy.64 = bf16[2,8,128,512]{3,2,1,0:T(8,128)(2,1)} copy(bf16[2,8,128,512]{3,2,0,1:T(8,128)(2,1)} %bitcast.61) | data formatting | bytes 4194304 | tf_op jit(solution)/shard_map/jit(_take)/select_n | solution.py:145
  53.3 3.9 %copy.60 = bf16[1,512,2048]{1,2,0:T(8,128)(2,1)} copy(bf16[1,512,2048]{2,1,0:T(8,128)(2,1)} %param.12) | data formatting | bytes 4194304 | tf_op args[5]
  57.2 3.9 %copy.61 = bf16[512,8,2,128]{3,0,2,1:T(8,128)(2,1)} copy(bf16[512,8,2,128]{0,3,2,1:T(8,128)(2,1)} %bitcast.62) | data formatting | bytes 4194304 | tf_op jit(solution)/shard_map/reshape;squeeze | solution.py:141
  61.1 2.3 %fusion.5 = bf16[512,8,2,128]{3,0,2,1:T(8,128)(2,1)S(1)} fusion(s32[]{:T(128)S(6)} %select_n.74, bf16[512,8,2,128]{3,0,2,1:T(8,128)(2,1)} %copy.61), kind=kLoop, calls=%fused_computation.24 | loop fusion | flops 1048576 | bytes 4194308 | tf_op jit(solution)/shard_map/jit(_roll_dynamic)/concatenate | solution.py:141
  63.5 2.1 %fusion.4 = bf16[512,8,2,128]{3,0,2,1:T(8,128)(2,1)} fusion(s32[]{:T(128)S(6)} %select_n.76, bf16[512,8,2,128]{3,0,2,1:T(8,128)(2,1)S(1)} %fusion.5), kind=kLoop, calls=%fused_computation.23 | loop fusion | flops 1048576 | bytes 4194308 | tf_op jit(solution)/shard_map/jit(_roll_dynamic)/concatenate | solution.py:141
  65.6 3.7 %gather_fusion = bf16[8,512,2,128]{3,1,2,0:T(8,128)(2,1)} fusion(bf16[512,8,2,128]{3,0,2,1:T(8,128)(2,1)} %fusion.4, s32[1024]{0:T(1024)S(1)} %pad_clamp_fusion), kind=kCustom, calls=%fused_computation | custom fusion | bytes 4194336 | tf_op jit(solution)/shard_map/jit(_take)/gather | solution.py:142
  69.3 3.9 %copy.63 = bf16[512,2,8,128]{0,3,2,1:T(8,128)(2,1)} copy(bf16[512,2,8,128]{3,0,1,2:T(8,128)(2,1)} %bitcast.60) | data formatting | bytes 4194304 | tf_op jit(solution)/shard_map/jit(_take)/select_n | solution.py:142
  73.2 2.8 %fusion.9 = (bf16[512,2048]{1,0:T(8,128)(2,1)S(1)}, bf16[512,2048]{1,0:T(8,128)(2,1)S(1)}) fusion(s32[]{:T(128)S(6)} %select_n.70, bf16[1,512,2048]{2,1,0:T(8,128)(2,1)S(1)} %bitcast.58, bf16[1,512,2048]{2,1,0:T(8,128)(2,1)} %bitcast.4, s32[]{:T(128)S(6)} %select_n.71), kind=kLoop, calls=%fused_computation.28 | loop fusion | flops 2097152 | bytes 8388616 | tf_op jit(solution)/shard_map/jit(dynamic_index_in_dim)/squeeze | solution.py:49
  76.0 0.6 fusion.44
  76.6 1.0 copy-done.2
  77.6 1.2 fusion.12
  78.8 0.3 copy-done.5
  79.2 1.3 convolution_convert_fusion.3
  80.5 0.3 copy-done.3
  80.7 1.5 %fusion.17 = bf16[512,512]{1,0:T(8,128)(2,1)S(1)} fusion(bf16[1,512,2048]{2,1,0:T(8,128)(2,1)S(1)} %copy-done.3, bf16[512,1024]{1,0:T(8,128)(2,1)S(1)} %get-tuple-element.28, bf16[512,1024]{1,0:T(8,128)(2,1)S(1)} %get-tuple-element.15, f32[512,512]{1,0:T(8,128)S(1)} %fusion.12), kind=kOutput, calls=%fused_computation.41 | convolution fusion | flops 1080295424 | bytes 5767168 | tf_op jit(solution)/shard_map/dot_general | solution.py:25
  82.3 1.3 convolution_convert_fusion.2
  83.7 0.1 fusion.43
  83.8 0.1 fusion.42
  84.1 0.6 collective-permute-start.2
  85.0 0.3 collective-permute-start.1
  85.3 2.0 %collective-permute-done.2 = bf16[1024,640]{1,0:T(8,128)(2,1)S(1)} collective-permute-done((bf16[1024,640]{1,0:T(8,128)(2,1)S(1)}, bf16[1024,640]{1,0:T(8,128)(2,1)S(1)}, u32[]{:S(2)}, u32[]{:S(2)}) %collective-permute-start.2) | collective-permute-done | bytes 1310752 | tf_op jit(solution)/shard_map/ppermute | solution.py:65
  87.4 0.4 add_convert_fusion
  87.7 3.2 %collective-permute-start.6 = (bf16[512,128]{1,0:T(8,128)(2,1)S(1)}, bf16[512,128]{1,0:T(8,128)(2,1)S(1)}, u32[]{:S(2)}, u32[]{:S(2)}) collective-permute-start(bf16[512,128]{1,0:T(8,128)(2,1)S(1)} %get-tuple-element.22), channel_id=1, source_target_pairs={{0,64},{32,96},{64,128},{96,160},{128,192},{160,224},{192,0},{224,... | collective-permute-start | bytes 393224 | tf_op jit(solution)/shard_map/ppermute | solution.py:84
  90.9 3.2 %collective-permute-start.9 = (bf16[512,128]{1,0:T(8,128)(2,1)S(1)}, bf16[512,128]{1,0:T(8,128)(2,1)S(1)}, u32[]{:S(2)}, u32[]{:S(2)}) collective-permute-start(bf16[512,128]{1,0:T(8,128)(2,1)S(1)} %get-tuple-element.23), channel_id=1, source_target_pairs={{0,192},{32,224},{64,0},{96,32},{128,64},{160,96},{192,128},{224,1... | collective-permute-start | bytes 393224 | tf_op jit(solution)/shard_map/ppermute | solution.py:84
  94.2 0.2 fusion.46
  94.4 2.5 %collective-permute-start.8 = (bf16[1024,128]{1,0:T(8,128)(2,1)S(1)}, bf16[1024,128]{1,0:T(8,128)(2,1)S(1)}, u32[]{:S(2)}, u32[]{:S(2)}) collective-permute-start(bf16[1024,128]{1,0:T(8,128)(2,1)S(1)} %get-tuple-element.19), channel_id=1, source_target_pairs={{0,224},{32,0},{64,32},{96,64},{128,96},{160,128},{192,160},{224,1... | collective-permute-start | bytes 786440 | tf_op jit(solution)/shard_map/ppermute | solution.py:84
  96.9 0.2 add_convert_fusion.1
  97.1 0.7 collective-permute-start.3
  97.8 0.9 collective-permute-done.6
  98.7 4.6 %collective-permute-start.4 = (bf16[1024,128]{1,0:T(8,128)(2,1)S(1)}, bf16[1024,128]{1,0:T(8,128)(2,1)S(1)}, u32[]{:S(2)}, u32[]{:S(2)}) collective-permute-start(bf16[1024,128]{1,0:T(8,128)(2,1)S(1)} %get-tuple-element.21), channel_id=1, source_target_pairs={{0,224},{32,0},{64,32},{96,64},{128,96},{160,128},{192,160},{224,1... | collective-permute-start | bytes 786440 | tf_op jit(solution)/shard_map/ppermute | solution.py:84
  103.2 4.5 %collective-permute-done.8 = bf16[1024,128]{1,0:T(8,128)(2,1)S(1)} collective-permute-done((bf16[1024,128]{1,0:T(8,128)(2,1)S(1)}, bf16[1024,128]{1,0:T(8,128)(2,1)S(1)}, u32[]{:S(2)}, u32[]{:S(2)}) %collective-permute-start.8) | collective-permute-done | bytes 262176 | tf_op jit(solution)/shard_map/ppermute | solution.py:84
  107.7 0.2 add_convert_fusion.4
  107.9 1.7 %collective-permute-start.7 = (bf16[1024,128]{1,0:T(8,128)(2,1)S(1)}, bf16[1024,128]{1,0:T(8,128)(2,1)S(1)}, u32[]{:S(2)}, u32[]{:S(2)}) collective-permute-start(bf16[1024,128]{1,0:T(8,128)(2,1)S(1)} %get-tuple-element.24), channel_id=1, source_target_pairs={{0,64},{32,96},{64,128},{96,160},{128,192},{160,224},{192,0},{224,... | collective-permute-start | bytes 786440 | tf_op jit(solution)/shard_map/ppermute | solution.py:84
  109.6 2.5 %collective-permute-start.10 = (bf16[1024,128]{1,0:T(8,128)(2,1)S(1)}, bf16[1024,128]{1,0:T(8,128)(2,1)S(1)}, u32[]{:S(2)}, u32[]{:S(2)}) collective-permute-start(bf16[1024,128]{1,0:T(8,128)(2,1)S(1)} %get-tuple-element.25), channel_id=1, source_target_pairs={{0,192},{32,224},{64,0},{96,32},{128,64},{160,96},{192,128},{224,1... | collective-permute-start | bytes 786440 | tf_op jit(solution)/shard_map/ppermute | solution.py:84
  112.1 2.7 %fusion.1 = bf16[1,512,2048]{2,1,0:T(8,128)(2,1)} fusion(bf16[512,1024]{1,0:T(8,128)(2,1)S(1)} %get-tuple-element.28, bf16[512,1024]{1,0:T(8,128)(2,1)S(1)} %get-tuple-element.15, f32[512,512]{1,0:T(8,128)S(1)} %fusion.12), kind=kOutput, calls=%fused_computation.19 | convolution fusion | flops 1080295424 | bytes 5242880 | tf_op jit(solution)/shard_map/dot_general | solution.py:36
  114.8 6.4 %collective-permute-done.7 = bf16[1024,128]{1,0:T(8,128)(2,1)S(1)} collective-permute-done((bf16[1024,128]{1,0:T(8,128)(2,1)S(1)}, bf16[1024,128]{1,0:T(8,128)(2,1)S(1)}, u32[]{:S(2)}, u32[]{:S(2)}) %collective-permute-start.7) | collective-permute-done | bytes 262176 | tf_op jit(solution)/shard_map/ppermute | solution.py:84
  121.2 3.1 %collective-permute-done.10 = bf16[1024,128]{1,0:T(8,128)(2,1)S(1)} collective-permute-done((bf16[1024,128]{1,0:T(8,128)(2,1)S(1)}, bf16[1024,128]{1,0:T(8,128)(2,1)S(1)}, u32[]{:S(2)}, u32[]{:S(2)}) %collective-permute-start.10) | collective-permute-done | bytes 262176 | tf_op jit(solution)/shard_map/ppermute | solution.py:84
  124.3 0.2 add_convert_fusion.2
  124.5 0.7 pad_maximum_fusion.11
  125.2 4.8 %all-to-all-start.1 = ((bf16[16,32,256]{2,1,0:T(8,128)(2,1)}), bf16[16,32,256]{2,1,0:T(8,128)(2,1)S(1)}, u32[]{:S(2)}, u32[]{:S(2)}) async-start(bf16[16,32,256]{2,1,0:T(8,128)(2,1)} %pad_maximum_fusion.11), calls=%async_computation.1 | async-start | bytes 524288 | tf_op jit(solution)/shard_map/all_to_all | solution.py:165
  130.0 2.6 %fusion = bf16[1,2048,512]{2,1,0:T(8,128)(2,1)} fusion(bf16[512,512]{1,0:T(8,128)(2,1)S(1)} %fusion.17, bf16[512,1024]{1,0:T(8,128)(2,1)S(1)} %get-tuple-element.29, bf16[512,1024]{1,0:T(8,128)(2,1)S(1)} %get-tuple-element.14), kind=kOutput, calls=%fused_computation.18 | convolution fusion | flops 1078984704 | bytes 4718592 | tf_op jit(solution)/shard_map/dot_general | solution.py:39
  132.6 4.8 %all-to-all-done.1 = bf16[16,32,256]{2,1,0:T(8,128)(2,1)S(1)} async-done(((bf16[16,32,256]{2,1,0:T(8,128)(2,1)}), bf16[16,32,256]{2,1,0:T(8,128)(2,1)S(1)}, u32[]{:S(2)}, u32[]{:S(2)}) %all-to-all-start.1) | async-done | bytes 262176 | tf_op jit(solution)/shard_map/all_to_all | solution.py:165
  137.4 0.3 fusion.21
  137.7 0.3 fusion.22
  138.0 0.9 multiply_reduce_fusion
  138.9 0.8 reduce_sum.45
  (34 shorter events, 1.0 us)
Async XLA Ops:
  0.6 6.1 %copy-start = (bf16[128,2048]{1,0:T(8,128)(2,1)S(1)}, bf16[128,2048]{1,0:T(8,128)(2,1)}, u32[]{:S(2)}) copy-start(bf16[128,2048]{1,0:T(8,128)(2,1)} %param.7) | copy-start | bytes 1572868
  7.9 34.3 %copy-start.6 = (s32[8]{0:T(128)S(1)}, s32[8]{0:T(128)}, u32[]{:S(2)}) copy-start(s32[8]{0:T(128)} %constant.139) | copy-start | bytes 100
  42.2 31.0 %collective-permute-start = (bf16[512,2048]{1,0:T(8,128)(2,1)S(1)}, bf16[512,2048]{1,0:T(8,128)(2,1)}, u32[]{:S(2)}, u32[]{:S(2)}) collective-permute-start(bf16[512,2048]{1,0:T(8,128)(2,1)S(1)} %bitcast.57), channel_id=1, source_target_pairs={{0,16},{16,0},{1,17},{17,1},{2,18},{18,2},{3,19},{19,3},{4,20},{20... | collective-permute-start | bytes 6291464 | tf_op jit(solution)/shard_map/ppermute | solution.py:116
  76.0 1.6 %copy-start.2 = (bf16[1,2048,512]{2,1,0:T(8,128)(2,1)S(1)}, bf16[1,2048,512]{2,1,0:T(8,128)(2,1)}, u32[]{:S(2)}) copy-start(bf16[1,2048,512]{2,1,0:T(8,128)(2,1)} %param.11) | copy-start | bytes 6291460
  77.6 1.6 %copy-start.5 = (bf16[512,2,8,128]{0,3,2,1:T(8,128)(2,1)S(1)}, bf16[512,2,8,128]{0,3,2,1:T(8,128)(2,1)}, u32[]{:S(2)}) copy-start(bf16[512,2,8,128]{0,3,2,1:T(8,128)(2,1)} %copy.63) | copy-start | bytes 6291460
  79.2 1.6 %copy-start.3 = (bf16[1,512,2048]{2,1,0:T(8,128)(2,1)S(1)}, bf16[1,512,2048]{2,1,0:T(8,128)(2,1)}, u32[]{:S(2)}) copy-start(bf16[1,512,2048]{2,1,0:T(8,128)(2,1)} %param.12) | copy-start | bytes 6291460
  80.7 1.6 %copy-start.4 = (bf16[2,8,128,512]{3,2,1,0:T(8,128)(2,1)S(1)}, bf16[2,8,128,512]{3,2,1,0:T(8,128)(2,1)}, u32[]{:S(2)}) copy-start(bf16[2,8,128,512]{3,2,1,0:T(8,128)(2,1)} %copy.64) | copy-start | bytes 6291460
  84.1 3.3 %collective-permute-start.2 = (bf16[1024,640]{1,0:T(8,128)(2,1)S(1)}, bf16[1024,640]{1,0:T(8,128)(2,1)S(1)}, u32[]{:S(2)}, u32[]{:S(2)}) collective-permute-start(bf16[1024,640]{1,0:T(8,128)(2,1)S(1)} %pad_maximum_fusion.7), channel_id=1, source_target_pairs={{0,16},{16,0},{1,17},{17,1},{2,18},{18,2},{3,19},{19,3},{4,20},{20... | collective-permute-start | bytes 3932168 | tf_op jit(solution)/shard_map/ppermute | solution.py:65
  85.0 11.9 %collective-permute-start.1 = (bf16[1024,384]{1,0:T(8,128)(2,1)S(1)}, bf16[1024,384]{1,0:T(8,128)(2,1)S(1)}, u32[]{:S(2)}, u32[]{:S(2)}) collective-permute-start(bf16[1024,384]{1,0:T(8,128)(2,1)S(1)} %pad_maximum_fusion.10), channel_id=1, source_target_pairs={{0,16},{16,0},{1,17},{17,1},{2,18},{18,2},{3,19},{19,3},{4,20},{20... | collective-permute-start | bytes 2359304 | tf_op jit(solution)/shard_map/ppermute | solution.py:65
  87.7 10.9 %collective-permute-start.6 = (bf16[512,128]{1,0:T(8,128)(2,1)S(1)}, bf16[512,128]{1,0:T(8,128)(2,1)S(1)}, u32[]{:S(2)}, u32[]{:S(2)}) collective-permute-start(bf16[512,128]{1,0:T(8,128)(2,1)S(1)} %get-tuple-element.22), channel_id=1, source_target_pairs={{0,64},{32,96},{64,128},{96,160},{128,192},{160,224},{192,0},{224,... | collective-permute-start | bytes 393224 | tf_op jit(solution)/shard_map/ppermute | solution.py:84
  90.9 12.3 %collective-permute-start.9 = (bf16[512,128]{1,0:T(8,128)(2,1)S(1)}, bf16[512,128]{1,0:T(8,128)(2,1)S(1)}, u32[]{:S(2)}, u32[]{:S(2)}) collective-permute-start(bf16[512,128]{1,0:T(8,128)(2,1)S(1)} %get-tuple-element.23), channel_id=1, source_target_pairs={{0,192},{32,224},{64,0},{96,32},{128,64},{160,96},{192,128},{224,1... | collective-permute-start | bytes 393224 | tf_op jit(solution)/shard_map/ppermute | solution.py:84
  94.4 13.4 %collective-permute-start.8 = (bf16[1024,128]{1,0:T(8,128)(2,1)S(1)}, bf16[1024,128]{1,0:T(8,128)(2,1)S(1)}, u32[]{:S(2)}, u32[]{:S(2)}) collective-permute-start(bf16[1024,128]{1,0:T(8,128)(2,1)S(1)} %get-tuple-element.19), channel_id=1, source_target_pairs={{0,224},{32,0},{64,32},{96,64},{128,96},{160,128},{192,160},{224,1... | collective-permute-start | bytes 786440 | tf_op jit(solution)/shard_map/ppermute | solution.py:84
  96.9 10.9 %collective-permute-start.5 = (bf16[1024,128]{1,0:T(8,128)(2,1)S(1)}, bf16[1024,128]{1,0:T(8,128)(2,1)S(1)}, u32[]{:S(2)}, u32[]{:S(2)}) collective-permute-start(bf16[1024,128]{1,0:T(8,128)(2,1)S(1)} %get-tuple-element.20), channel_id=1, source_target_pairs={{0,32},{32,64},{64,96},{96,128},{128,160},{160,192},{192,224},{224... | collective-permute-start | bytes 786440 | tf_op jit(solution)/shard_map/ppermute | solution.py:84
  97.1 17.7 %collective-permute-start.3 = (bf16[1024,128]{1,0:T(8,128)(2,1)S(1)}, bf16[1024,128]{1,0:T(8,128)(2,1)S(1)}, u32[]{:S(2)}, u32[]{:S(2)}) collective-permute-start(bf16[1024,128]{1,0:T(8,128)(2,1)S(1)} %get-tuple-element.18), channel_id=1, source_target_pairs={{0,32},{32,64},{64,96},{96,128},{128,160},{160,192},{192,224},{224... | collective-permute-start | bytes 786440 | tf_op jit(solution)/shard_map/ppermute | solution.py:84
  98.7 16.1 %collective-permute-start.4 = (bf16[1024,128]{1,0:T(8,128)(2,1)S(1)}, bf16[1024,128]{1,0:T(8,128)(2,1)S(1)}, u32[]{:S(2)}, u32[]{:S(2)}) collective-permute-start(bf16[1024,128]{1,0:T(8,128)(2,1)S(1)} %get-tuple-element.21), channel_id=1, source_target_pairs={{0,224},{32,0},{64,32},{96,64},{128,96},{160,128},{192,160},{224,1... | collective-permute-start | bytes 786440 | tf_op jit(solution)/shard_map/ppermute | solution.py:84
  107.9 13.2 %collective-permute-start.7 = (bf16[1024,128]{1,0:T(8,128)(2,1)S(1)}, bf16[1024,128]{1,0:T(8,128)(2,1)S(1)}, u32[]{:S(2)}, u32[]{:S(2)}) collective-permute-start(bf16[1024,128]{1,0:T(8,128)(2,1)S(1)} %get-tuple-element.24), channel_id=1, source_target_pairs={{0,64},{32,96},{64,128},{96,160},{128,192},{160,224},{192,0},{224,... | collective-permute-start | bytes 786440 | tf_op jit(solution)/shard_map/ppermute | solution.py:84
  109.6 14.7 %collective-permute-start.10 = (bf16[1024,128]{1,0:T(8,128)(2,1)S(1)}, bf16[1024,128]{1,0:T(8,128)(2,1)S(1)}, u32[]{:S(2)}, u32[]{:S(2)}) collective-permute-start(bf16[1024,128]{1,0:T(8,128)(2,1)S(1)} %get-tuple-element.25), channel_id=1, source_target_pairs={{0,192},{32,224},{64,0},{96,32},{128,64},{160,96},{192,128},{224,1... | collective-permute-start | bytes 786440 | tf_op jit(solution)/shard_map/ppermute | solution.py:84
  125.2 12.2 %all-to-all-start.1 = ((bf16[16,32,256]{2,1,0:T(8,128)(2,1)}), bf16[16,32,256]{2,1,0:T(8,128)(2,1)S(1)}, u32[]{:S(2)}, u32[]{:S(2)}) async-start(bf16[16,32,256]{2,1,0:T(8,128)(2,1)} %pad_maximum_fusion.11), calls=%async_computation.1 | async-start | bytes 524288 | tf_op jit(solution)/shard_map/all_to_all | solution.py:165
  130.0 9.7 %copy-start.1 = (bf16[128,2048]{1,0:T(8,128)(2,1)S(1)}, bf16[128,2048]{1,0:T(8,128)(2,1)}, u32[]{:S(2)}) copy-start(bf16[128,2048]{1,0:T(8,128)(2,1)} %param.7) | copy-start | bytes 1572868

commit v9 on v4

--- a/solution.py
+++ b/solution.py
@@ -144,12 +144,15 @@
         (out_part.astype(jnp.bfloat16), dx_part.astype(jnp.bfloat16)), n_z, n_core, cols
     )
     slots = n_exp * capacity
-    both = jnp.concatenate([acc[:slots], acc[slots:]], axis=1).astype(jnp.bfloat16)
     back_both = lax.all_to_all(
-        both.reshape(n_exp, capacity, 2 * cols), "exp", split_axis=0, concat_axis=0, tiled=True
-    ).reshape(n_exp * capacity, 2 * cols)
-    back_out = back_both[:, :cols]
-    back_dx = back_both[:, cols:]
+        acc.astype(jnp.bfloat16).reshape(2, n_exp, capacity, cols),
+        "exp",
+        split_axis=1,
+        concat_axis=1,
+        tiled=True,
+    )
+    back_out = back_both[0].reshape(slots, cols)
+    back_dx = back_both[1].reshape(slots, cols)
     pair_out = jnp.einsum(
         "st,sd->td",
         placed,

time: 126 us -> 125 us (level)
  other arithmetic: 13.3 us -> 10.9 us
    reduce_sum x2 -> x0, other arithmetic: 1.64 us -> none  [the longest x1 0.86 us: local(): jnp.sum(gate_values[:, :, None] * pair_out.reshape(tok_count, top_k, cols...]
where the time goes in v9:
time: 125 us
  blocking collectives  34.3 us (27%)
  waiting for transfers between devices  28.2 us (23%)
  starting transfers between devices  21.5 us (17%)
  local copies, waits for them, and re-layouts  15.5 us (12%)
  matrix products  13.3 us (11%)
  other arithmetic  10.9 us (9%)
    all_to_all x1, blocking collectives, dispatch_rows(): lax.all_to_all(sent.reshape(n_exp, capacity, sent.shape[1]), 'exp', split...  34.3 us
    ppermute x8, waiting for transfers between devices, shift(): lax.ppermute(x, 'z', [(j, (j + k) % n_z) for j in range(n_z)])  19.6 us
    ppermute x8, starting transfers between devices, shift(): lax.ppermute(x, 'z', [(j, (j + k) % n_z) for j in range(n_z)])  16.1 us
    unnamed x19, local copies, waits for them, and re-layouts  8.6 us
    all_to_all x1, waiting for transfers between devices, local(): lax.all_to_all(acc.astype(jnp.bfloat16).reshape(2, n_exp, capacity, cols)...  4.81 us
    all_to_all x1, starting transfers between devices, local(): lax.all_to_all(acc.astype(jnp.bfloat16).reshape(2, n_exp, capacity, cols)...  4.78 us
    ppermute x1, waiting for transfers between devices, reduce_over_rep(): lax.ppermute(jnp.concatenate([p[:, share:] for p in parts], axis=0), 'cor...  3.79 us
    squeeze x1, other arithmetic, pick(): return lax.dynamic_index_in_dim(stacked, index, axis=axis, keepdims=False)  2.75 us
  transfers between devices with their start and end apart: 11, of which 6 were waited for; matrix products, arithmetic and copies ran while one was open for 14% of the time, Pallas kernels for 0%

profile of v9, /device:TPU:2, one launch (start us, length us, event | category | flops | bytes accessed | tf_op | source)
XLA Modules:
  0.0 124.6 jit_solution(3617902233836038390)
XLA Ops:
  0.6 0.8 copy.51
  1.5 0.1 eq.77
  1.6 0.1 reshape.92
  1.8 0.6 reduce-window.6
  2.4 0.2 slice_reduce_fusion
  2.6 0.1 fusion.35
  2.7 0.1 reduce_sum.42
  2.9 1.0 dynamic-slice_convert_fusion
  3.9 0.4 mul.70
  4.3 0.7 mul.71
  5.0 0.1 copy.55
  5.1 0.1 mul.68
  5.2 0.1 copy.54
  5.3 0.1 fusion.28
  5.4 0.4 convolution_convert_fusion.4
  5.9 0.5 convolution_convert_fusion.5
  6.4 0.2 pad_maximum_fusion
  6.6 34.3 %all_to_all.10 = bf16[16,32,2048]{2,1,0:T(8,128)(2,1)S(1)} all-to-all(bf16[16,32,2048]{2,1,0:T(8,128)(2,1)S(1)} %bitcast.70), channel_id=1, replica_groups=mesh['z'=8,'core'=2,'exp'=16] {'exp'}, dimensions={0} | all-to-all | bytes 4194304 | tf_op jit(solution)/shard_map/all_to_all | solution.py:99
  40.9 3.9 %copy.56 = bf16[1,512,2048]{1,2,0:T(8,128)(2,1)} copy(bf16[1,512,2048]{2,1,0:T(8,128)(2,1)} %param.11) | data formatting | bytes 4194304 | tf_op args[5]
  44.8 2.3 %fusion.7 = bf16[512,8,2,128]{0,3,2,1:T(8,128)(2,1)S(1)} fusion(s32[]{:T(128)S(6)} %select_n.50, bf16[512,8,2,128]{0,3,2,1:T(8,128)(2,1)} %bitcast.69), kind=kLoop, calls=%fused_computation.24 | loop fusion | flops 1048576 | bytes 4194308 | tf_op jit(solution)/shard_map/jit(_roll_dynamic)/concatenate | solution.py:126
  47.1 0.8 fusion.6
  47.9 1.5 %copy.57 = bf16[512,2,8,128]{0,3,2,1:T(8,128)(2,1)} copy(bf16[512,2,8,128]{0,3,1,2:T(8,128)(2,1)S(1)} %fusion.6) | data formatting | bytes 4194304 | tf_op jit(solution)/shard_map/transpose | solution.py:127
  49.4 0.8 copy-done.1
  50.3 0.8 fusion.4
  51.0 0.8 fusion.3
  51.8 1.5 %copy.58 = bf16[2,8,128,512]{3,2,1,0:T(8,128)(2,1)} copy(bf16[2,8,128,512]{3,2,0,1:T(8,128)(2,1)S(1)} %fusion.3) | data formatting | bytes 4194304 | tf_op jit(solution)/shard_map/transpose | solution.py:129
  53.3 2.8 %fusion.11 = (bf16[512,2048]{1,0:T(8,128)(2,1)S(1)}, bf16[512,2048]{1,0:T(8,128)(2,1)S(1)}) fusion(s32[]{:T(128)S(6)} %select_n.47, bf16[1,512,2048]{2,1,0:T(8,128)(2,1)S(1)} %bitcast.68, bf16[1,512,2048]{2,1,0:T(8,128)(2,1)} %bitcast.5, s32[]{:T(128)S(6)} %select_n.48), kind=kLoop, calls=%fused_computation.28 | loop fusion | flops 2097152 | bytes 8388616 | tf_op jit(solution)/shard_map/jit(dynamic_index_in_dim)/squeeze | solution.py:49
  56.1 0.6 fusion.46
  56.7 1.0 copy-done.2
  57.7 1.2 fusion.14
  58.9 0.3 copy-done.5
  59.3 1.3 %convolution_convert_fusion.3 = bf16[512,2048]{1,0:T(8,128)(2,1)S(1)} fusion(bf16[512,2048]{0,1:T(8,128)(2,1)S(1)} %bitcast.73, f32[512,512]{1,0:T(8,128)S(1)} %fusion.14), kind=kOutput, calls=%fused_computation.16 | convolution fusion | flops 1076101120 | bytes 5242880 | tf_op jit(solution)/shard_map/dot_general | solution.py:24
  60.6 0.2 fusion.44
  60.8 1.4 %copy-done.3 = bf16[1,512,2048]{2,1,0:T(8,128)(2,1)S(1)} copy-done((bf16[1,512,2048]{2,1,0:T(8,128)(2,1)S(1)}, bf16[1,512,2048]{2,1,0:T(8,128)(2,1)}, u32[]{:S(2)}) %copy-start.3) | copy-done | bytes 2097176
  62.2 1.4 %fusion.19 = bf16[512,512]{1,0:T(8,128)(2,1)S(1)} fusion(bf16[1,512,2048]{2,1,0:T(8,128)(2,1)S(1)} %copy-done.3, bf16[512,1024]{1,0:T(8,128)(2,1)S(1)} %get-tuple-element.24, bf16[512,1024]{1,0:T(8,128)(2,1)S(1)} %get-tuple-element.19, f32[512,512]{1,0:T(8,128)S(1)} %fusion.14), kind=kOutput, calls=%fused_computation.40 | convolution fusion | flops 1080295424 | bytes 5767168 | tf_op jit(solution)/shard_map/dot_general | solution.py:25
  63.6 0.1 copy-done.4
  63.8 1.3 %convolution_convert_fusion.2 = bf16[512,2048]{1,0:T(8,128)(2,1)S(1)} fusion(bf16[512,512]{1,0:T(8,128)(2,1)S(1)} %fusion.19, bf16[2048,512]{1,0:T(8,128)(2,1)S(1)} %bitcast.72), kind=kOutput, calls=%fused_computation.15 | convolution fusion | flops 1074790400 | bytes 4718592 | tf_op jit(solution)/shard_map/dot_general | solution.py:30
  65.1 0.2 fusion.45
  65.3 0.2 pad_maximum_fusion.3
  65.5 0.6 collective-permute-start.1
  66.1 3.8 %collective-permute-done.1 = bf16[1024,1024]{1,0:T(8,128)(2,1)S(1)} collective-permute-done((bf16[1024,1024]{1,0:T(8,128)(2,1)S(1)}, bf16[1024,1024]{1,0:T(8,128)(2,1)S(1)}, u32[]{:S(2)}, u32[]{:S(2)}) %collective-permute-start.1) | collective-permute-done | bytes 2097184 | tf_op jit(solution)/shard_map/ppermute | solution.py:54
  69.9 1.0 add_convert_fusion
  70.9 0.2 fusion.42
  71.1 2.1 %collective-permute-start.4 = (bf16[1024,128]{1,0:T(8,128)(2,1)S(1)}, bf16[1024,128]{1,0:T(8,128)(2,1)S(1)}, u32[]{:S(2)}, u32[]{:S(2)}) collective-permute-start(bf16[1024,128]{1,0:T(8,128)(2,1)S(1)} %get-tuple-element.8), channel_id=1, source_target_pairs={{0,32},{32,64},{64,96},{96,128},{128,160},{160,192},{192,224},{224... | collective-permute-start | bytes 786440 | tf_op jit(solution)/shard_map/ppermute | solution.py:70
  73.2 4.1 %collective-permute-start.7 = (bf16[1024,128]{1,0:T(8,128)(2,1)S(1)}, bf16[1024,128]{1,0:T(8,128)(2,1)S(1)}, u32[]{:S(2)}, u32[]{:S(2)}) collective-permute-start(bf16[1024,128]{1,0:T(8,128)(2,1)S(1)} %get-tuple-element.7), channel_id=1, source_target_pairs={{0,224},{32,0},{64,32},{96,64},{128,96},{160,128},{192,160},{224,1... | collective-permute-start | bytes 786440 | tf_op jit(solution)/shard_map/ppermute | solution.py:70
  77.3 0.1 fusion.43
  77.4 0.1 collective-permute-start.5
  77.5 4.1 %collective-permute-start.8 = (bf16[512,128]{1,0:T(8,128)(2,1)S(1)}, bf16[512,128]{1,0:T(8,128)(2,1)S(1)}, u32[]{:S(2)}, u32[]{:S(2)}) collective-permute-start(bf16[512,128]{1,0:T(8,128)(2,1)S(1)} %get-tuple-element.13), channel_id=1, source_target_pairs={{0,192},{32,224},{64,0},{96,32},{128,64},{160,96},{192,128},{224,1... | collective-permute-start | bytes 393224 | tf_op jit(solution)/shard_map/ppermute | solution.py:70
  81.6 9.4 %collective-permute-done.5 = bf16[512,128]{1,0:T(8,128)(2,1)S(1)} collective-permute-done((bf16[512,128]{1,0:T(8,128)(2,1)S(1)}, bf16[512,128]{1,0:T(8,128)(2,1)S(1)}, u32[]{:S(2)}, u32[]{:S(2)}) %collective-permute-start.5) | collective-permute-done | bytes 131104 | tf_op jit(solution)/shard_map/ppermute | solution.py:70
  91.0 1.4 %collective-permute-start.3 = (bf16[1024,128]{1,0:T(8,128)(2,1)S(1)}, bf16[1024,128]{1,0:T(8,128)(2,1)S(1)}, u32[]{:S(2)}, u32[]{:S(2)}) collective-permute-start(bf16[1024,128]{1,0:T(8,128)(2,1)S(1)} %get-tuple-element.9), channel_id=1, source_target_pairs={{0,224},{32,0},{64,32},{96,64},{128,96},{160,128},{192,160},{224,1... | collective-permute-start | bytes 786440 | tf_op jit(solution)/shard_map/ppermute | solution.py:70
  92.4 0.2 add_convert_fusion.3
  92.6 2.2 %collective-permute-start.6 = (bf16[1024,128]{1,0:T(8,128)(2,1)S(1)}, bf16[1024,128]{1,0:T(8,128)(2,1)S(1)}, u32[]{:S(2)}, u32[]{:S(2)}) collective-permute-start(bf16[1024,128]{1,0:T(8,128)(2,1)S(1)} %get-tuple-element.10), channel_id=1, source_target_pairs={{0,64},{32,96},{64,128},{96,160},{128,192},{160,224},{192,0},{224,... | collective-permute-start | bytes 786440 | tf_op jit(solution)/shard_map/ppermute | solution.py:70
  94.8 2.0 %collective-permute-start.9 = (bf16[1024,128]{1,0:T(8,128)(2,1)S(1)}, bf16[1024,128]{1,0:T(8,128)(2,1)S(1)}, u32[]{:S(2)}, u32[]{:S(2)}) collective-permute-start(bf16[1024,128]{1,0:T(8,128)(2,1)S(1)} %get-tuple-element.11), channel_id=1, source_target_pairs={{0,192},{32,224},{64,0},{96,32},{128,64},{160,96},{192,128},{224,1... | collective-permute-start | bytes 786440 | tf_op jit(solution)/shard_map/ppermute | solution.py:70
  96.8 2.7 %fusion.1 = bf16[1,512,2048]{2,1,0:T(8,128)(2,1)} fusion(bf16[512,1024]{1,0:T(8,128)(2,1)S(1)} %get-tuple-element.24, bf16[512,1024]{1,0:T(8,128)(2,1)S(1)} %get-tuple-element.19, f32[512,512]{1,0:T(8,128)S(1)} %fusion.14), kind=kOutput, calls=%fused_computation.18 | convolution fusion | flops 1080295424 | bytes 5242880 | tf_op jit(solution)/shard_map/dot_general | solution.py:36
  99.5 2.6 %collective-permute-done.3 = bf16[1024,128]{1,0:T(8,128)(2,1)S(1)} collective-permute-done((bf16[1024,128]{1,0:T(8,128)(2,1)S(1)}, bf16[1024,128]{1,0:T(8,128)(2,1)S(1)}, u32[]{:S(2)}, u32[]{:S(2)}) %collective-permute-start.3) | collective-permute-done | bytes 262176 | tf_op jit(solution)/shard_map/ppermute | solution.py:70
  102.1 4.5 %collective-permute-done.6 = bf16[1024,128]{1,0:T(8,128)(2,1)S(1)} collective-permute-done((bf16[1024,128]{1,0:T(8,128)(2,1)S(1)}, bf16[1024,128]{1,0:T(8,128)(2,1)S(1)}, u32[]{:S(2)}, u32[]{:S(2)}) %collective-permute-start.6) | collective-permute-done | bytes 262176 | tf_op jit(solution)/shard_map/ppermute | solution.py:70
  106.5 3.1 %collective-permute-done.9 = bf16[1024,128]{1,0:T(8,128)(2,1)S(1)} collective-permute-done((bf16[1024,128]{1,0:T(8,128)(2,1)S(1)}, bf16[1024,128]{1,0:T(8,128)(2,1)S(1)}, u32[]{:S(2)}, u32[]{:S(2)}) %collective-permute-start.9) | collective-permute-done | bytes 262176 | tf_op jit(solution)/shard_map/ppermute | solution.py:70
  109.6 0.2 add_convert_fusion.1
  109.8 0.7 copy.59
  110.5 4.8 %all-to-all-start.1 = ((bf16[2,16,32,128]{3,2,0,1:T(8,128)(2,1)}), bf16[2,16,32,128]{3,2,0,1:T(8,128)(2,1)S(1)}, u32[]{:S(2)}, u32[]{:S(2)}) async-start(bf16[2,16,32,128]{3,2,0,1:T(8,128)(2,1)} %copy.59), calls=%async_computation.1 | async-start | bytes 524288 | tf_op jit(solution)/shard_map/all_to_all | solution.py:147
  115.3 2.6 %fusion = bf16[1,2048,512]{2,1,0:T(8,128)(2,1)} fusion(bf16[512,512]{1,0:T(8,128)(2,1)S(1)} %fusion.19, bf16[512,1024]{1,0:T(8,128)(2,1)S(1)} %get-tuple-element.25, bf16[512,1024]{1,0:T(8,128)(2,1)S(1)} %get-tuple-element.18), kind=kOutput, calls=%fused_computation.17 | convolution fusion | flops 1078984704 | bytes 4718592 | tf_op jit(solution)/shard_map/dot_general | solution.py:39
  117.9 4.8 %all-to-all-done.1 = bf16[2,16,32,128]{3,2,0,1:T(8,128)(2,1)S(1)} async-done(((bf16[2,16,32,128]{3,2,0,1:T(8,128)(2,1)}), bf16[2,16,32,128]{3,2,0,1:T(8,128)(2,1)S(1)}, u32[]{:S(2)}, u32[]{:S(2)}) %all-to-all-start.1) | async-done | bytes 262176 | tf_op jit(solution)/shard_map/all_to_all | solution.py:147
  122.8 0.9 convolution_reduce_fusion
  123.7 0.9 fusion.22
  (24 shorter events, 0.1 us)
Async XLA Ops:
  0.6 4.8 %copy-start = (bf16[128,2048]{1,0:T(8,128)(2,1)S(1)}, bf16[128,2048]{1,0:T(8,128)(2,1)}, u32[]{:S(2)}) copy-start(bf16[128,2048]{1,0:T(8,128)(2,1)} %param.6) | copy-start | bytes 1572868
  2.9 2.1 %copy-start.7 = (f32[128,2]{0,1:T(2,128)S(1)}, f32[128,2]{0,1:T(2,128)}, u32[]{:S(2)}) copy-start(f32[128,2]{0,1:T(2,128)} %param.8) | copy-start | bytes 3076
  3.9 1.4 %copy-start.6 = (s32[128,2]{0,1:T(2,128)S(1)}, s32[128,2]{0,1:T(2,128)}, u32[]{:S(2)}) copy-start(s32[128,2]{0,1:T(2,128)} %param.7) | copy-start | bytes 3076
  40.9 12.4 %collective-permute-start = (bf16[512,2048]{1,0:T(8,128)(2,1)S(1)}, bf16[512,2048]{1,0:T(8,128)(2,1)}, u32[]{:S(2)}, u32[]{:S(2)}) collective-permute-start(bf16[512,2048]{1,0:T(8,128)(2,1)S(1)} %bitcast.67), channel_id=1, source_target_pairs={{0,16},{16,0},{1,17},{17,1},{2,18},{18,2},{3,19},{19,3},{4,20},{20... | collective-permute-start | bytes 6291464 | tf_op jit(solution)/shard_map/ppermute | solution.py:102
  47.9 2.4 %copy-start.1 = (bf16[1,2048,512]{2,1,0:T(8,128)(2,1)S(1)}, bf16[1,2048,512]{2,1,0:T(8,128)(2,1)}, u32[]{:S(2)}) copy-start(bf16[1,2048,512]{2,1,0:T(8,128)(2,1)} %param.10) | copy-start | bytes 6291460
  56.1 1.6 %copy-start.2 = (bf16[1,2048,512]{2,1,0:T(8,128)(2,1)S(1)}, bf16[1,2048,512]{2,1,0:T(8,128)(2,1)}, u32[]{:S(2)}) copy-start(bf16[1,2048,512]{2,1,0:T(8,128)(2,1)} %param.10) | copy-start | bytes 6291460
  57.7 1.6 %copy-start.5 = (bf16[512,2,8,128]{0,3,2,1:T(8,128)(2,1)S(1)}, bf16[512,2,8,128]{0,3,2,1:T(8,128)(2,1)}, u32[]{:S(2)}) copy-start(bf16[512,2,8,128]{0,3,2,1:T(8,128)(2,1)} %copy.57) | copy-start | bytes 6291460
  60.6 1.6 %copy-start.3 = (bf16[1,512,2048]{2,1,0:T(8,128)(2,1)S(1)}, bf16[1,512,2048]{2,1,0:T(8,128)(2,1)}, u32[]{:S(2)}) copy-start(bf16[1,512,2048]{2,1,0:T(8,128)(2,1)} %param.11) | copy-start | bytes 6291460
  62.2 1.6 %copy-start.4 = (bf16[2,8,128,512]{3,2,1,0:T(8,128)(2,1)S(1)}, bf16[2,8,128,512]{3,2,1,0:T(8,128)(2,1)}, u32[]{:S(2)}) copy-start(bf16[2,8,128,512]{3,2,1,0:T(8,128)(2,1)} %copy.58) | copy-start | bytes 6291460
  65.5 4.4 %collective-permute-start.1 = (bf16[1024,1024]{1,0:T(8,128)(2,1)S(1)}, bf16[1024,1024]{1,0:T(8,128)(2,1)S(1)}, u32[]{:S(2)}, u32[]{:S(2)}) collective-permute-start(bf16[1024,1024]{1,0:T(8,128)(2,1)S(1)} %pad_maximum_fusion.3), channel_id=1, source_target_pairs={{0,16},{16,0},{1,17},{17,1},{2,18},{18,2},{3,19},{19,3},{4,20},{20... | collective-permute-start | bytes 6291464 | tf_op jit(solution)/shard_map/ppermute | solution.py:54
  71.1 21.4 %collective-permute-start.4 = (bf16[1024,128]{1,0:T(8,128)(2,1)S(1)}, bf16[1024,128]{1,0:T(8,128)(2,1)S(1)}, u32[]{:S(2)}, u32[]{:S(2)}) collective-permute-start(bf16[1024,128]{1,0:T(8,128)(2,1)S(1)} %get-tuple-element.8), channel_id=1, source_target_pairs={{0,32},{32,64},{64,96},{96,128},{128,160},{160,192},{192,224},{224... | collective-permute-start | bytes 786440 | tf_op jit(solution)/shard_map/ppermute | solution.py:70
  73.2 19.3 %collective-permute-start.7 = (bf16[1024,128]{1,0:T(8,128)(2,1)S(1)}, bf16[1024,128]{1,0:T(8,128)(2,1)S(1)}, u32[]{:S(2)}, u32[]{:S(2)}) collective-permute-start(bf16[1024,128]{1,0:T(8,128)(2,1)S(1)} %get-tuple-element.7), channel_id=1, source_target_pairs={{0,224},{32,0},{64,32},{96,64},{128,96},{160,128},{192,160},{224,1... | collective-permute-start | bytes 786440 | tf_op jit(solution)/shard_map/ppermute | solution.py:70
  77.4 13.6 %collective-permute-start.5 = (bf16[512,128]{1,0:T(8,128)(2,1)S(1)}, bf16[512,128]{1,0:T(8,128)(2,1)S(1)}, u32[]{:S(2)}, u32[]{:S(2)}) collective-permute-start(bf16[512,128]{1,0:T(8,128)(2,1)S(1)} %get-tuple-element.12), channel_id=1, source_target_pairs={{0,64},{32,96},{64,128},{96,160},{128,192},{160,224},{192,0},{224,... | collective-permute-start | bytes 393224 | tf_op jit(solution)/shard_map/ppermute | solution.py:70
  77.5 15.0 %collective-permute-start.8 = (bf16[512,128]{1,0:T(8,128)(2,1)S(1)}, bf16[512,128]{1,0:T(8,128)(2,1)S(1)}, u32[]{:S(2)}, u32[]{:S(2)}) collective-permute-start(bf16[512,128]{1,0:T(8,128)(2,1)S(1)} %get-tuple-element.13), channel_id=1, source_target_pairs={{0,192},{32,224},{64,0},{96,32},{128,64},{160,96},{192,128},{224,1... | collective-permute-start | bytes 393224 | tf_op jit(solution)/shard_map/ppermute | solution.py:70
  81.6 17.9 %collective-permute-start.2 = (bf16[1024,128]{1,0:T(8,128)(2,1)S(1)}, bf16[1024,128]{1,0:T(8,128)(2,1)S(1)}, u32[]{:S(2)}, u32[]{:S(2)}) collective-permute-start(bf16[1024,128]{1,0:T(8,128)(2,1)S(1)} %get-tuple-element.6), channel_id=1, source_target_pairs={{0,32},{32,64},{64,96},{96,128},{128,160},{160,192},{192,224},{224... | collective-permute-start | bytes 786440 | tf_op jit(solution)/shard_map/ppermute | solution.py:70
  91.0 11.1 %collective-permute-start.3 = (bf16[1024,128]{1,0:T(8,128)(2,1)S(1)}, bf16[1024,128]{1,0:T(8,128)(2,1)S(1)}, u32[]{:S(2)}, u32[]{:S(2)}) collective-permute-start(bf16[1024,128]{1,0:T(8,128)(2,1)S(1)} %get-tuple-element.9), channel_id=1, source_target_pairs={{0,224},{32,0},{64,32},{96,64},{128,96},{160,128},{192,160},{224,1... | collective-permute-start | bytes 786440 | tf_op jit(solution)/shard_map/ppermute | solution.py:70
  92.6 13.9 %collective-permute-start.6 = (bf16[1024,128]{1,0:T(8,128)(2,1)S(1)}, bf16[1024,128]{1,0:T(8,128)(2,1)S(1)}, u32[]{:S(2)}, u32[]{:S(2)}) collective-permute-start(bf16[1024,128]{1,0:T(8,128)(2,1)S(1)} %get-tuple-element.10), channel_id=1, source_target_pairs={{0,64},{32,96},{64,128},{96,160},{128,192},{160,224},{192,0},{224,... | collective-permute-start | bytes 786440 | tf_op jit(solution)/shard_map/ppermute | solution.py:70
  94.8 14.8 %collective-permute-start.9 = (bf16[1024,128]{1,0:T(8,128)(2,1)S(1)}, bf16[1024,128]{1,0:T(8,128)(2,1)S(1)}, u32[]{:S(2)}, u32[]{:S(2)}) collective-permute-start(bf16[1024,128]{1,0:T(8,128)(2,1)S(1)} %get-tuple-element.11), channel_id=1, source_target_pairs={{0,192},{32,224},{64,0},{96,32},{128,64},{160,96},{192,128},{224,1... | collective-permute-start | bytes 786440 | tf_op jit(solution)/shard_map/ppermute | solution.py:70
  110.5 12.2 %all-to-all-start.1 = ((bf16[2,16,32,128]{3,2,0,1:T(8,128)(2,1)}), bf16[2,16,32,128]{3,2,0,1:T(8,128)(2,1)S(1)}, u32[]{:S(2)}, u32[]{:S(2)}) async-start(bf16[2,16,32,128]{3,2,0,1:T(8,128)(2,1)} %copy.59), calls=%async_computation.1 | async-start | bytes 524288 | tf_op jit(solution)/shard_map/all_to_all | solution.py:147

commit v10 on v9

--- a/solution.py
+++ b/solution.py
@@ -51,13 +51,17 @@
 
 def reduce_over_rep(parts, n_z, n_core, cols):
     share = n_z * cols
-    got = lax.ppermute(
-        jnp.concatenate([p[:, share:] for p in parts], axis=0),
-        "core",
-        [(j, (j + 1) % n_core) for j in range(n_core)],
-    )
-    own = jnp.concatenate([p[:, :share] for p in parts], axis=0)
-    pair_sum = (own.astype(jnp.float32) + got.astype(jnp.float32)).astype(jnp.bfloat16)
+    swap = [(j, (j + 1) % n_core) for j in range(n_core)]
+    pair_sum = jnp.concatenate(
+        [
+            (
+                p[:, :share].astype(jnp.float32)
+                + lax.ppermute(p[:, share:], "core", swap).astype(jnp.float32)
+            ).astype(jnp.bfloat16)
+            for p in parts
+        ],
+        axis=0,
+    )
     block = [pair_sum[:, k * cols : (k + 1) * cols] for k in range(n_z)]
     acc = block[0].astype(jnp.float32)
     if n_z != 8:

time: 125 us -> 123 us (0.984)
    ppermute x1 -> x2, waiting for transfers between devices: 3.79 us -> 1.87 us  [reduce_over_rep(): lax.ppermute(p[:, share:], 'core', swap).astype(jnp.float32)]
    ppermute x8, starting transfers between devices: 16.1 us -> 14.7 us  [shift(): lax.ppermute(x, 'z', [(j, (j + k) % n_z) for j in range(n_z)])]
  transfers between devices with their start and end apart: 11 -> 12, of which waited for: 6 -> 5; matrix products, arithmetic and copies ran while one was open for 14% -> 17% of each run, Pallas kernels for 0% -> 0%
where the time goes in v10:
time: 123 us; the launch traced here: 122 us
  blocking collectives  34.3 us (28%)
  waiting for transfers between devices  27.4 us (22%)
  starting transfers between devices  20.9 us (17%)
  local copies, waits for them, and re-layouts  14.4 us (12%)
  matrix products  13.4 us (11%)
  other arithmetic  10.7 us (9%)
    all_to_all x1, blocking collectives, dispatch_rows(): lax.all_to_all(sent.reshape(n_exp, capacity, sent.shape[1]), 'exp', split...  34.3 us
    ppermute x8, waiting for transfers between devices, shift(): lax.ppermute(x, 'z', [(j, (j + k) % n_z) for j in range(n_z)])  20.7 us
    ppermute x8, starting transfers between devices, shift(): lax.ppermute(x, 'z', [(j, (j + k) % n_z) for j in range(n_z)])  14.7 us
    unnamed x19, local copies, waits for them, and re-layouts  7.91 us
    all_to_all x1, waiting for transfers between devices, local(): lax.all_to_all(acc.astype(jnp.bfloat16).reshape(2, n_exp, capacity, cols)...  4.8 us
    all_to_all x1, starting transfers between devices, local(): lax.all_to_all(acc.astype(jnp.bfloat16).reshape(2, n_exp, capacity, cols)...  4.78 us
    squeeze x1, other arithmetic, pick(): return lax.dynamic_index_in_dim(stacked, index, axis=axis, keepdims=False)  2.75 us
    dot_general x1, matrix products, expert_math(): lax.dot_general(hidden_units, rows_grad, (((0,), (0,)), ((), ())), prefer...  2.65 us
  transfers between devices with their start and end apart: 12, of which 5 were waited for; matrix products, arithmetic and copies ran while one was open for 17% of the time, Pallas kernels for 0%

profile of v10, /device:TPU:2, one launch (start us, length us, event | category | flops | bytes accessed | tf_op | source)
XLA Modules:
  0.0 122.0 jit_solution(10674776734179136954)
XLA Ops:
  0.6 0.0 copy-start
  0.6 0.8 copy.51
  1.5 0.1 eq.77
  1.6 0.1 reshape.92
  1.8 0.6 reduce-window.6
  2.4 0.2 slice_reduce_fusion
  2.6 0.1 fusion.35
  2.7 0.1 reduce_sum.42
  2.9 1.0 dynamic-slice_convert_fusion
  3.9 0.4 mul.70
  4.3 0.7 mul.71
  5.0 0.1 copy.55
  5.1 0.1 mul.68
  5.2 0.1 copy.54
  5.3 0.1 fusion.28
  5.4 0.4 convolution_convert_fusion.4
  5.9 0.5 convolution_convert_fusion.5
  6.4 0.2 pad_maximum_fusion
  6.6 34.3 %all_to_all.10 = bf16[16,32,2048]{2,1,0:T(8,128)(2,1)S(1)} all-to-all(bf16[16,32,2048]{2,1,0:T(8,128)(2,1)S(1)} %bitcast.70), channel_id=1, replica_groups=mesh['z'=8,'core'=2,'exp'=16] {'exp'}, dimensions={0} | all-to-all | bytes 4194304 | tf_op jit(solution)/shard_map/all_to_all | solution.py:103
  40.9 3.9 %copy.56 = bf16[1,512,2048]{1,2,0:T(8,128)(2,1)} copy(bf16[1,512,2048]{2,1,0:T(8,128)(2,1)} %param.11) | data formatting | bytes 4194304 | tf_op args[5]
  44.8 2.3 %fusion.7 = bf16[512,8,2,128]{0,3,2,1:T(8,128)(2,1)S(1)} fusion(s32[]{:T(128)S(6)} %select_n.50, bf16[512,8,2,128]{0,3,2,1:T(8,128)(2,1)} %bitcast.69), kind=kLoop, calls=%fused_computation.23 | loop fusion | flops 1048576 | bytes 4194308 | tf_op jit(solution)/shard_map/jit(_roll_dynamic)/concatenate | solution.py:130
  47.1 0.8 fusion.6
  47.9 1.5 %copy.57 = bf16[512,2,8,128]{0,3,2,1:T(8,128)(2,1)} copy(bf16[512,2,8,128]{0,3,1,2:T(8,128)(2,1)S(1)} %fusion.6) | data formatting | bytes 4194304 | tf_op jit(solution)/shard_map/transpose | solution.py:131
  49.4 0.8 copy-done.1
  50.3 0.8 fusion.4
  51.0 0.8 fusion.3
  51.8 1.5 %copy.58 = bf16[2,8,128,512]{3,2,1,0:T(8,128)(2,1)} copy(bf16[2,8,128,512]{3,2,0,1:T(8,128)(2,1)S(1)} %fusion.3) | data formatting | bytes 4194304 | tf_op jit(solution)/shard_map/transpose | solution.py:133
  53.3 2.8 %fusion.11 = (bf16[512,2048]{1,0:T(8,128)(2,1)S(1)}, bf16[512,2048]{1,0:T(8,128)(2,1)S(1)}) fusion(s32[]{:T(128)S(6)} %select_n.47, bf16[1,512,2048]{2,1,0:T(8,128)(2,1)S(1)} %bitcast.68, bf16[1,512,2048]{2,1,0:T(8,128)(2,1)} %bitcast.5, s32[]{:T(128)S(6)} %select_n.48), kind=kLoop, calls=%fused_computation.27 | loop fusion | flops 2097152 | bytes 8388616 | tf_op jit(solution)/shard_map/jit(dynamic_index_in_dim)/squeeze | solution.py:49
  56.1 0.6 fusion.42
  56.7 1.0 copy-done.2
  57.7 1.2 %fusion.14 = f32[512,512]{1,0:T(8,128)S(1)} fusion(bf16[1,2048,512]{2,1,0:T(8,128)(2,1)S(1)} %copy-done.2, bf16[512,1024]{1,0:T(8,128)(2,1)S(1)} %get-tuple-element.19, bf16[512,1024]{1,0:T(8,128)(2,1)S(1)} %get-tuple-element.12), kind=kOutput, calls=%fused_computation.33 | convolution fusion | flops 1077936128 | bytes 5242880 | tf_op jit(solution)/shard_map/dot_general | solution.py:21
  58.9 0.3 copy-done.5
  59.3 1.3 %convolution_convert_fusion.3 = bf16[512,2048]{1,0:T(8,128)(2,1)S(1)} fusion(bf16[512,2048]{0,1:T(8,128)(2,1)S(1)} %bitcast.73, f32[512,512]{1,0:T(8,128)S(1)} %fusion.14), kind=kOutput, calls=%fused_computation.15 | convolution fusion | flops 1076101120 | bytes 5242880 | tf_op jit(solution)/shard_map/dot_general | solution.py:24
  60.6 0.1 slice.93
  60.7 0.8 collective-permute-start.1
  61.5 0.7 copy-done.3
  62.2 1.5 %fusion.19 = bf16[512,512]{1,0:T(8,128)(2,1)S(1)} fusion(bf16[1,512,2048]{2,1,0:T(8,128)(2,1)S(1)} %copy-done.3, bf16[512,1024]{1,0:T(8,128)(2,1)S(1)} %get-tuple-element.18, bf16[512,1024]{1,0:T(8,128)(2,1)S(1)} %get-tuple-element.13, f32[512,512]{1,0:T(8,128)S(1)} %fusion.14), kind=kOutput, calls=%fused_computation.40 | convolution fusion | flops 1080295424 | bytes 5767168 | tf_op jit(solution)/shard_map/dot_general | solution.py:25
  63.6 0.1 copy-done.4
  63.8 1.3 %convolution_convert_fusion.2 = bf16[512,2048]{1,0:T(8,128)(2,1)S(1)} fusion(bf16[512,512]{1,0:T(8,128)(2,1)S(1)} %fusion.19, bf16[2048,512]{1,0:T(8,128)(2,1)S(1)} %bitcast.72), kind=kOutput, calls=%fused_computation.14 | convolution fusion | flops 1074790400 | bytes 4718592 | tf_op jit(solution)/shard_map/dot_general | solution.py:30
  65.1 0.1 slice.97
  65.2 0.6 collective-permute-start.2
  65.8 0.4 add_convert_fusion.1
  66.2 1.9 %collective-permute-done.2 = bf16[512,1024]{1,0:T(8,128)(2,1)S(1)} collective-permute-done((bf16[512,1024]{1,0:T(8,128)(2,1)S(1)}, bf16[512,1024]{1,0:T(8,128)(2,1)S(1)}, u32[]{:S(2)}, u32[]{:S(2)}) %collective-permute-start.2) | collective-permute-done | bytes 1048608 | tf_op jit(solution)/shard_map/ppermute | solution.py:59
  68.1 0.4 add_convert_fusion
  68.5 0.2 pad_maximum_fusion.12
  68.7 1.9 %collective-permute-start.5 = (bf16[1024,128]{1,0:T(8,128)(2,1)S(1)}, bf16[1024,128]{1,0:T(8,128)(2,1)S(1)}, u32[]{:S(2)}, u32[]{:S(2)}) collective-permute-start(bf16[1024,128]{1,0:T(8,128)(2,1)S(1)} %get-tuple-element.7), channel_id=1, source_target_pairs={{0,32},{32,64},{64,96},{96,128},{128,160},{160,192},{192,224},{224... | collective-permute-start | bytes 786440 | tf_op jit(solution)/shard_map/ppermute | solution.py:74
  70.6 4.1 %collective-permute-start.8 = (bf16[1024,128]{1,0:T(8,128)(2,1)S(1)}, bf16[1024,128]{1,0:T(8,128)(2,1)S(1)}, u32[]{:S(2)}, u32[]{:S(2)}) collective-permute-start(bf16[1024,128]{1,0:T(8,128)(2,1)S(1)} %get-tuple-element.9), channel_id=1, source_target_pairs={{0,224},{32,0},{64,32},{96,64},{128,96},{160,128},{192,160},{224,1... | collective-permute-start | bytes 786440 | tf_op jit(solution)/shard_map/ppermute | solution.py:74
  74.7 0.1 collective-permute-start.6
  74.9 4.2 %collective-permute-start.9 = (bf16[512,128]{1,0:T(8,128)(2,1)S(1)}, bf16[512,128]{1,0:T(8,128)(2,1)S(1)}, u32[]{:S(2)}, u32[]{:S(2)}) collective-permute-start(bf16[512,128]{1,0:T(8,128)(2,1)S(1)} %slice.99), channel_id=1, source_target_pairs={{0,192},{32,224},{64,0},{96,32},{128,64},{160,96},{192,128},{224,1... | collective-permute-start | bytes 393224 | tf_op jit(solution)/shard_map/ppermute | solution.py:74
  79.1 9.3 %collective-permute-done.6 = bf16[512,128]{1,0:T(8,128)(2,1)S(1)} collective-permute-done((bf16[512,128]{1,0:T(8,128)(2,1)S(1)}, bf16[512,128]{1,0:T(8,128)(2,1)S(1)}, u32[]{:S(2)}, u32[]{:S(2)}) %collective-permute-start.6) | collective-permute-done | bytes 131104 | tf_op jit(solution)/shard_map/ppermute | solution.py:74
  88.4 1.4 %collective-permute-start.4 = (bf16[1024,128]{1,0:T(8,128)(2,1)S(1)}, bf16[1024,128]{1,0:T(8,128)(2,1)S(1)}, u32[]{:S(2)}, u32[]{:S(2)}) collective-permute-start(bf16[1024,128]{1,0:T(8,128)(2,1)S(1)} %get-tuple-element.8), channel_id=1, source_target_pairs={{0,224},{32,0},{64,32},{96,64},{128,96},{160,128},{192,160},{224,1... | collective-permute-start | bytes 786440 | tf_op jit(solution)/shard_map/ppermute | solution.py:74
  89.9 0.2 add_convert_fusion.4
  90.1 2.7 %collective-permute-start.10 = (bf16[1024,128]{1,0:T(8,128)(2,1)S(1)}, bf16[1024,128]{1,0:T(8,128)(2,1)S(1)}, u32[]{:S(2)}, u32[]{:S(2)}) collective-permute-start(bf16[1024,128]{1,0:T(8,128)(2,1)S(1)} %get-tuple-element.11), channel_id=1, source_target_pairs={{0,192},{32,224},{64,0},{96,32},{128,64},{160,96},{192,128},{224,1... | collective-permute-start | bytes 786440 | tf_op jit(solution)/shard_map/ppermute | solution.py:74
  92.8 0.3 collective-permute-start.7
  93.1 2.7 %fusion.1 = bf16[1,512,2048]{2,1,0:T(8,128)(2,1)} fusion(bf16[512,1024]{1,0:T(8,128)(2,1)S(1)} %get-tuple-element.18, bf16[512,1024]{1,0:T(8,128)(2,1)S(1)} %get-tuple-element.13, f32[512,512]{1,0:T(8,128)S(1)} %fusion.14), kind=kOutput, calls=%fused_computation.17 | convolution fusion | flops 1080295424 | bytes 5242880 | tf_op jit(solution)/shard_map/dot_general | solution.py:36
  95.7 4.6 %collective-permute-done.4 = bf16[1024,128]{1,0:T(8,128)(2,1)S(1)} collective-permute-done((bf16[1024,128]{1,0:T(8,128)(2,1)S(1)}, bf16[1024,128]{1,0:T(8,128)(2,1)S(1)}, u32[]{:S(2)}, u32[]{:S(2)}) %collective-permute-start.4) | collective-permute-done | bytes 262176 | tf_op jit(solution)/shard_map/ppermute | solution.py:74
  100.3 6.7 %collective-permute-done.10 = bf16[1024,128]{1,0:T(8,128)(2,1)S(1)} collective-permute-done((bf16[1024,128]{1,0:T(8,128)(2,1)S(1)}, bf16[1024,128]{1,0:T(8,128)(2,1)S(1)}, u32[]{:S(2)}, u32[]{:S(2)}) %collective-permute-start.10) | collective-permute-done | bytes 262176 | tf_op jit(solution)/shard_map/ppermute | solution.py:74
  107.1 0.2 add_convert_fusion.2
  107.2 0.7 copy.59
  108.0 4.8 %all-to-all-start.1 = ((bf16[2,16,32,128]{3,2,0,1:T(8,128)(2,1)}), bf16[2,16,32,128]{3,2,0,1:T(8,128)(2,1)S(1)}, u32[]{:S(2)}, u32[]{:S(2)}) async-start(bf16[2,16,32,128]{3,2,0,1:T(8,128)(2,1)} %copy.59), calls=%async_computation.1 | async-start | bytes 524288 | tf_op jit(solution)/shard_map/all_to_all | solution.py:151
  112.7 2.6 %fusion = bf16[1,2048,512]{2,1,0:T(8,128)(2,1)} fusion(bf16[512,512]{1,0:T(8,128)(2,1)S(1)} %fusion.19, bf16[512,1024]{1,0:T(8,128)(2,1)S(1)} %get-tuple-element.19, bf16[512,1024]{1,0:T(8,128)(2,1)S(1)} %get-tuple-element.12), kind=kOutput, calls=%fused_computation.16 | convolution fusion | flops 1078984704 | bytes 4718592 | tf_op jit(solution)/shard_map/dot_general | solution.py:39
  115.4 4.8 %all-to-all-done.1 = bf16[2,16,32,128]{3,2,0,1:T(8,128)(2,1)S(1)} async-done(((bf16[2,16,32,128]{3,2,0,1:T(8,128)(2,1)}), bf16[2,16,32,128]{3,2,0,1:T(8,128)(2,1)S(1)}, u32[]{:S(2)}, u32[]{:S(2)}) %all-to-all-start.1) | async-done | bytes 262176 | tf_op jit(solution)/shard_map/all_to_all | solution.py:151
  120.2 0.9 convolution_reduce_fusion
  121.1 0.9 fusion.22
  (27 shorter events, 0.2 us)
Async XLA Ops:
  0.6 4.8 %copy-start = (bf16[128,2048]{1,0:T(8,128)(2,1)S(1)}, bf16[128,2048]{1,0:T(8,128)(2,1)}, u32[]{:S(2)}) copy-start(bf16[128,2048]{1,0:T(8,128)(2,1)} %param.6) | copy-start | bytes 1572868
  2.9 2.1 %copy-start.7 = (f32[128,2]{0,1:T(2,128)S(1)}, f32[128,2]{0,1:T(2,128)}, u32[]{:S(2)}) copy-start(f32[128,2]{0,1:T(2,128)} %param.8) | copy-start | bytes 3076
  3.9 1.4 %copy-start.6 = (s32[128,2]{0,1:T(2,128)S(1)}, s32[128,2]{0,1:T(2,128)}, u32[]{:S(2)}) copy-start(s32[128,2]{0,1:T(2,128)} %param.7) | copy-start | bytes 3076
  40.9 12.4 %collective-permute-start = (bf16[512,2048]{1,0:T(8,128)(2,1)S(1)}, bf16[512,2048]{1,0:T(8,128)(2,1)}, u32[]{:S(2)}, u32[]{:S(2)}) collective-permute-start(bf16[512,2048]{1,0:T(8,128)(2,1)S(1)} %bitcast.67), channel_id=1, source_target_pairs={{0,16},{16,0},{1,17},{17,1},{2,18},{18,2},{3,19},{19,3},{4,20},{20... | collective-permute-start | bytes 6291464 | tf_op jit(solution)/shard_map/ppermute | solution.py:106
  47.9 2.4 %copy-start.1 = (bf16[1,2048,512]{2,1,0:T(8,128)(2,1)S(1)}, bf16[1,2048,512]{2,1,0:T(8,128)(2,1)}, u32[]{:S(2)}) copy-start(bf16[1,2048,512]{2,1,0:T(8,128)(2,1)} %param.10) | copy-start | bytes 6291460
  56.1 1.6 %copy-start.2 = (bf16[1,2048,512]{2,1,0:T(8,128)(2,1)S(1)}, bf16[1,2048,512]{2,1,0:T(8,128)(2,1)}, u32[]{:S(2)}) copy-start(bf16[1,2048,512]{2,1,0:T(8,128)(2,1)} %param.10) | copy-start | bytes 6291460
  57.7 1.6 %copy-start.5 = (bf16[512,2,8,128]{0,3,2,1:T(8,128)(2,1)S(1)}, bf16[512,2,8,128]{0,3,2,1:T(8,128)(2,1)}, u32[]{:S(2)}) copy-start(bf16[512,2,8,128]{0,3,2,1:T(8,128)(2,1)} %copy.57) | copy-start | bytes 6291460
  60.6 1.6 %copy-start.3 = (bf16[1,512,2048]{2,1,0:T(8,128)(2,1)S(1)}, bf16[1,512,2048]{2,1,0:T(8,128)(2,1)}, u32[]{:S(2)}) copy-start(bf16[1,512,2048]{2,1,0:T(8,128)(2,1)} %param.11) | copy-start | bytes 6291460
  60.7 5.1 %collective-permute-start.1 = (bf16[512,1024]{1,0:T(8,128)(2,1)S(1)}, bf16[512,1024]{1,0:T(8,128)(2,1)S(1)}, u32[]{:S(2)}, u32[]{:S(2)}) collective-permute-start(bf16[512,1024]{1,0:T(8,128)(2,1)S(1)} %slice.93), channel_id=1, source_target_pairs={{0,16},{16,0},{1,17},{17,1},{2,18},{18,2},{3,19},{19,3},{4,20},{20... | collective-permute-start | bytes 3145736 | tf_op jit(solution)/shard_map/ppermute | solution.py:59
  62.2 1.6 %copy-start.4 = (bf16[2,8,128,512]{3,2,1,0:T(8,128)(2,1)S(1)}, bf16[2,8,128,512]{3,2,1,0:T(8,128)(2,1)}, u32[]{:S(2)}) copy-start(bf16[2,8,128,512]{3,2,1,0:T(8,128)(2,1)} %copy.58) | copy-start | bytes 6291460
  65.2 2.9 %collective-permute-start.2 = (bf16[512,1024]{1,0:T(8,128)(2,1)S(1)}, bf16[512,1024]{1,0:T(8,128)(2,1)S(1)}, u32[]{:S(2)}, u32[]{:S(2)}) collective-permute-start(bf16[512,1024]{1,0:T(8,128)(2,1)S(1)} %slice.97), channel_id=1, source_target_pairs={{0,16},{16,0},{1,17},{17,1},{2,18},{18,2},{3,19},{19,3},{4,20},{20... | collective-permute-start | bytes 3145736 | tf_op jit(solution)/shard_map/ppermute | solution.py:59
  68.7 21.2 %collective-permute-start.5 = (bf16[1024,128]{1,0:T(8,128)(2,1)S(1)}, bf16[1024,128]{1,0:T(8,128)(2,1)S(1)}, u32[]{:S(2)}, u32[]{:S(2)}) collective-permute-start(bf16[1024,128]{1,0:T(8,128)(2,1)S(1)} %get-tuple-element.7), channel_id=1, source_target_pairs={{0,32},{32,64},{64,96},{96,128},{128,160},{160,192},{192,224},{224... | collective-permute-start | bytes 786440 | tf_op jit(solution)/shard_map/ppermute | solution.py:74
  70.6 19.3 %collective-permute-start.8 = (bf16[1024,128]{1,0:T(8,128)(2,1)S(1)}, bf16[1024,128]{1,0:T(8,128)(2,1)S(1)}, u32[]{:S(2)}, u32[]{:S(2)}) collective-permute-start(bf16[1024,128]{1,0:T(8,128)(2,1)S(1)} %get-tuple-element.9), channel_id=1, source_target_pairs={{0,224},{32,0},{64,32},{96,64},{128,96},{160,128},{192,160},{224,1... | collective-permute-start | bytes 786440 | tf_op jit(solution)/shard_map/ppermute | solution.py:74
  74.7 13.7 %collective-permute-start.6 = (bf16[512,128]{1,0:T(8,128)(2,1)S(1)}, bf16[512,128]{1,0:T(8,128)(2,1)S(1)}, u32[]{:S(2)}, u32[]{:S(2)}) collective-permute-start(bf16[512,128]{1,0:T(8,128)(2,1)S(1)} %slice.98), channel_id=1, source_target_pairs={{0,64},{32,96},{64,128},{96,160},{128,192},{160,224},{192,0},{224,... | collective-permute-start | bytes 393224 | tf_op jit(solution)/shard_map/ppermute | solution.py:74
  74.9 15.0 %collective-permute-start.9 = (bf16[512,128]{1,0:T(8,128)(2,1)S(1)}, bf16[512,128]{1,0:T(8,128)(2,1)S(1)}, u32[]{:S(2)}, u32[]{:S(2)}) collective-permute-start(bf16[512,128]{1,0:T(8,128)(2,1)S(1)} %slice.99), channel_id=1, source_target_pairs={{0,192},{32,224},{64,0},{96,32},{128,64},{160,96},{192,128},{224,1... | collective-permute-start | bytes 393224 | tf_op jit(solution)/shard_map/ppermute | solution.py:74
  79.1 16.6 %collective-permute-start.3 = (bf16[1024,128]{1,0:T(8,128)(2,1)S(1)}, bf16[1024,128]{1,0:T(8,128)(2,1)S(1)}, u32[]{:S(2)}, u32[]{:S(2)}) collective-permute-start(bf16[1024,128]{1,0:T(8,128)(2,1)S(1)} %get-tuple-element.6), channel_id=1, source_target_pairs={{0,32},{32,64},{64,96},{96,128},{128,160},{160,192},{192,224},{224... | collective-permute-start | bytes 786440 | tf_op jit(solution)/shard_map/ppermute | solution.py:74
  88.4 11.9 %collective-permute-start.4 = (bf16[1024,128]{1,0:T(8,128)(2,1)S(1)}, bf16[1024,128]{1,0:T(8,128)(2,1)S(1)}, u32[]{:S(2)}, u32[]{:S(2)}) collective-permute-start(bf16[1024,128]{1,0:T(8,128)(2,1)S(1)} %get-tuple-element.8), channel_id=1, source_target_pairs={{0,224},{32,0},{64,32},{96,64},{128,96},{160,128},{192,160},{224,1... | collective-permute-start | bytes 786440 | tf_op jit(solution)/shard_map/ppermute | solution.py:74
  90.1 17.0 %collective-permute-start.10 = (bf16[1024,128]{1,0:T(8,128)(2,1)S(1)}, bf16[1024,128]{1,0:T(8,128)(2,1)S(1)}, u32[]{:S(2)}, u32[]{:S(2)}) collective-permute-start(bf16[1024,128]{1,0:T(8,128)(2,1)S(1)} %get-tuple-element.11), channel_id=1, source_target_pairs={{0,192},{32,224},{64,0},{96,32},{128,64},{160,96},{192,128},{224,1... | collective-permute-start | bytes 786440 | tf_op jit(solution)/shard_map/ppermute | solution.py:74
  92.8 14.3 %collective-permute-start.7 = (bf16[1024,128]{1,0:T(8,128)(2,1)S(1)}, bf16[1024,128]{1,0:T(8,128)(2,1)S(1)}, u32[]{:S(2)}, u32[]{:S(2)}) collective-permute-start(bf16[1024,128]{1,0:T(8,128)(2,1)S(1)} %get-tuple-element.10), channel_id=1, source_target_pairs={{0,64},{32,96},{64,128},{96,160},{128,192},{160,224},{192,0},{224,... | collective-permute-start | bytes 786440 | tf_op jit(solution)/shard_map/ppermute | solution.py:74
  108.0 12.2 %all-to-all-start.1 = ((bf16[2,16,32,128]{3,2,0,1:T(8,128)(2,1)}), bf16[2,16,32,128]{3,2,0,1:T(8,128)(2,1)S(1)}, u32[]{:S(2)}, u32[]{:S(2)}) async-start(bf16[2,16,32,128]{3,2,0,1:T(8,128)(2,1)} %copy.59), calls=%async_computation.1 | async-start | bytes 524288 | tf_op jit(solution)/shard_map/all_to_all | solution.py:151

commit v11 on v10

--- a/solution.py
+++ b/solution.py
@@ -103,13 +103,14 @@
     got = lax.all_to_all(
         sent.reshape(n_exp, capacity, sent.shape[1]), "exp", split_axis=0, concat_axis=0, tiled=True
     ).reshape(n_exp * capacity, sent.shape[1])
-    other = lax.ppermute(got, "core", [(j, (j + 1) % n_core) for j in range(n_core)])
-    pair = jnp.stack([got, other])
-    first, second = pick(pair, core, 0), pick(pair, 1 - core, 0)
-    return [
-        jnp.concatenate([first[:, i * share : (i + 1) * share], second[:, i * share : (i + 1) * share]], axis=1)
-        for i in range(len(sources))
-    ]
+    swap = [(j, (j + 1) % n_core) for j in range(n_core)]
+    rows = []
+    for i in range(len(sources)):
+        mine = got[:, i * share : (i + 1) * share]
+        other = lax.ppermute(mine, "core", swap)
+        pair = jnp.stack([mine, other])
+        rows.append(jnp.concatenate([pick(pair, core, 0), pick(pair, 1 - core, 0)], axis=1))
+    return rows
 
 
 def local(tokens, expert_ids, gate_values, grad_out, w_up, w_down):

time: 123 us -> 122 us (level)
    slice x2, local copies, waits for them, and re-layouts: 0.75 us -> 2.37 us  [the longest x1 2.19 us: dispatch_rows(): mine = got[:, i * share:(i + 1) * share]]
    unnamed x19 -> x27, local copies, waits for them, and re-layouts: 7.91 us -> 6.31 us
    concatenate x1, other arithmetic: 2.34 us -> 0.76 us  [local(): jnp.roll(down_weight.reshape(ff_local, n_z, n_core, cols), (-zi, -core),...]
    squeeze x1 -> x2, other arithmetic: 2.75 us -> 4.25 us  [pick(): return lax.dynamic_index_in_dim(stacked, index, axis=axis, keepdims=False)]
  transfers between devices with their start and end apart: 12 -> 13, of which waited for: 5 -> 5; matrix products, arithmetic and copies ran while one was open for 17% -> 20% of each run, Pallas kernels for 0% -> 0%
where the time goes in v11:
time: 122 us; the launch traced here: 121 us
  blocking collectives  34.3 us (28%)
  waiting for transfers between devices  26.8 us (22%)
  starting transfers between devices  20.5 us (17%)
  local copies, waits for them, and re-layouts  14.4 us (12%)
  matrix products  13.4 us (11%)
  other arithmetic  10.6 us (9%)
    all_to_all x1, blocking collectives, dispatch_rows(): lax.all_to_all(sent.reshape(n_exp, capacity, sent.shape[1]), 'exp', split...  34.3 us
    ppermute x8, waiting for transfers between devices, shift(): lax.ppermute(x, 'z', [(j, (j + k) % n_z) for j in range(n_z)])  19.8 us
    ppermute x8, starting transfers between devices, shift(): lax.ppermute(x, 'z', [(j, (j + k) % n_z) for j in range(n_z)])  14.8 us
    unnamed x27, local copies, waits for them, and re-layouts  6.31 us
    all_to_all x1, waiting for transfers between devices, local(): lax.all_to_all(acc.astype(jnp.bfloat16).reshape(2, n_exp, capacity, cols)...  4.8 us
    all_to_all x1, starting transfers between devices, local(): lax.all_to_all(acc.astype(jnp.bfloat16).reshape(2, n_exp, capacity, cols)...  4.78 us
    squeeze x2, other arithmetic, pick(): return lax.dynamic_index_in_dim(stacked, index, axis=axis, keepdims=False)  4.25 us
    dot_general x1, matrix products, expert_math(): lax.dot_general(hidden_units, rows_grad, (((0,), (0,)), ((), ())), prefer...  2.68 us
  transfers between devices with their start and end apart: 13, of which 5 were waited for; matrix products, arithmetic and copies ran while one was open for 20% of the time, Pallas kernels for 0%

profile of v11, /device:TPU:2, one launch (start us, length us, event | category | flops | bytes accessed | tf_op | source)
XLA Modules:
  0.0 121.1 jit_solution(15759115157657778720)
XLA Ops:
  0.6 0.8 copy.51
  1.5 0.1 eq.77
  1.6 0.1 reshape.92
  1.8 0.6 reduce-window.6
  2.4 0.2 slice_reduce_fusion
  2.6 0.1 fusion.39
  2.7 0.1 reduce_sum.42
  2.9 1.0 dynamic-slice_convert_fusion
  3.9 0.4 mul.70
  4.3 0.7 mul.71
  5.0 0.1 copy.55
  5.1 0.1 mul.68
  5.2 0.1 copy.54
  5.3 0.1 fusion.32
  5.4 0.4 convolution_convert_fusion.4
  5.9 0.5 convolution_convert_fusion.5
  6.4 0.2 pad_maximum_fusion
  6.6 34.3 %all_to_all.10 = bf16[16,32,2048]{2,1,0:T(8,128)(2,1)S(1)} all-to-all(bf16[16,32,2048]{2,1,0:T(8,128)(2,1)S(1)} %bitcast.77), channel_id=1, replica_groups=mesh['z'=8,'core'=2,'exp'=16] {'exp'}, dimensions={0} | all-to-all | bytes 4194304 | tf_op jit(solution)/shard_map/all_to_all | solution.py:103
  40.9 2.2 %fusion.46 = (bf16[512,1024]{1,0:T(8,128)(2,1)}, bf16[1,512,1024]{2,1,0:T(8,128)(2,1)}, bf16[1,512,1024]{2,1,0:T(8,128)(2,1)}, bf16[512,1024]{1,0:T(8,128)(2,1)}) fusion(bf16[512,2048]{1,0:T(8,128)(2,1)S(1)} %bitcast.75), kind=kLoop, calls=%fused_computation.92 | loop fusion | bytes 6291456 | tf_op jit(solution)/shard_map/slice | solution.py:109
  43.1 2.9 %copy.56 = bf16[1,512,2048]{1,2,0:T(8,128)(2,1)S(1)} copy(bf16[1,512,2048]{2,1,0:T(8,128)(2,1)} %param.11) | data formatting | bytes 4194304 | tf_op args[5]
  46.0 0.8 fusion.7
  46.7 0.8 fusion.6
  47.5 1.5 %copy.57 = bf16[512,2,8,128]{0,3,2,1:T(8,128)(2,1)} copy(bf16[512,2,8,128]{0,3,1,2:T(8,128)(2,1)S(1)} %fusion.6) | data formatting | bytes 4194304 | tf_op jit(solution)/shard_map/transpose | solution.py:132
  49.0 0.8 copy-done.3
  49.8 0.8 fusion.4
  50.6 0.6 collective-permute-start.2
  51.2 0.7 fusion.3
  51.9 1.5 %copy.58 = bf16[2,8,128,512]{3,2,1,0:T(8,128)(2,1)} copy(bf16[2,8,128,512]{3,2,0,1:T(8,128)(2,1)S(1)} %fusion.3) | data formatting | bytes 4194304 | tf_op jit(solution)/shard_map/transpose | solution.py:134
  53.5 2.1 %fusion.26 = (bf16[512,1024]{1,0:T(8,128)(2,1)S(1)}, bf16[512,1024]{1,0:T(8,128)(2,1)S(1)}) fusion(s32[]{:T(128)S(6)} %select_n.49, bf16[1,512,1024]{2,1,0:T(8,128)(2,1)S(1)} %copy-done.2, bf16[1,512,1024]{2,1,0:T(8,128)(2,1)} %bitcast.5, s32[]{:T(128)S(6)} %select_n.50), kind=kLoop, calls=%fused_computation.51 | loop fusion | flops 1048576 | bytes 4194312 | tf_op jit(solution)/shard_map/jit(dynamic_index_in_dim)/squeeze | solution.py:49
  55.6 1.3 %fusion.10 = f32[512,512]{1,0:T(8,128)S(1)} fusion(bf16[1,2048,512]{2,1,0:T(8,128)(2,1)S(1)} %copy-done.4, bf16[512,1024]{1,0:T(8,128)(2,1)S(1)} %get-tuple-element.11, bf16[512,1024]{1,0:T(8,128)(2,1)S(1)} %get-tuple-element.10), kind=kOutput, calls=%fused_computation.33 | convolution fusion | flops 1077936128 | bytes 5242880 | tf_op jit(solution)/shard_map/dot_general | solution.py:21
  56.9 0.7 copy-done.7
  57.6 1.3 %convolution_convert_fusion.3 = bf16[512,2048]{1,0:T(8,128)(2,1)S(1)} fusion(bf16[512,2048]{0,1:T(8,128)(2,1)S(1)} %bitcast.80, f32[512,512]{1,0:T(8,128)S(1)} %fusion.10), kind=kOutput, calls=%fused_computation.11 | convolution fusion | flops 1076101120 | bytes 5242880 | tf_op jit(solution)/shard_map/dot_general | solution.py:24
  58.9 0.1 slice.84
  59.0 0.3 collective-permute-start.1
  59.3 0.8 copy-done.1
  60.1 2.1 %fusion.22 = (bf16[512,1024]{1,0:T(8,128)(2,1)S(1)}, bf16[512,1024]{1,0:T(8,128)(2,1)S(1)}) fusion(s32[]{:T(128)S(6)} %select_n.49, bf16[1,512,1024]{2,1,0:T(8,128)(2,1)S(1)} %copy-done.1, bf16[1,512,1024]{2,1,0:T(8,128)(2,1)} %bitcast.13, s32[]{:T(128)S(6)} %select_n.50), kind=kLoop, calls=%fused_computation.47 | loop fusion | flops 1048576 | bytes 4194312 | tf_op jit(solution)/shard_map/jit(dynamic_index_in_dim)/squeeze | solution.py:49
  62.3 1.5 %fusion.15 = bf16[512,512]{1,0:T(8,128)(2,1)S(1)} fusion(bf16[1,512,2048]{2,1,0:T(8,128)(2,1)S(1)} %copy-done.5, bf16[512,1024]{1,0:T(8,128)(2,1)S(1)} %get-tuple-element.17, bf16[512,1024]{1,0:T(8,128)(2,1)S(1)} %get-tuple-element.16, f32[512,512]{1,0:T(8,128)S(1)} %fusion.10), kind=kOutput, calls=%fused_computation.40 | convolution fusion | flops 1080295424 | bytes 5767168 | tf_op jit(solution)/shard_map/dot_general | solution.py:25
  63.8 0.1 copy-done.6
  63.9 1.3 %convolution_convert_fusion.2 = bf16[512,2048]{1,0:T(8,128)(2,1)S(1)} fusion(bf16[512,512]{1,0:T(8,128)(2,1)S(1)} %fusion.15, bf16[2048,512]{1,0:T(8,128)(2,1)S(1)} %bitcast.79), kind=kOutput, calls=%fused_computation.10 | convolution fusion | flops 1074790400 | bytes 4718592 | tf_op jit(solution)/shard_map/dot_general | solution.py:30
  65.2 0.1 slice.87
  65.3 0.1 collective-permute-start.3
  65.4 0.4 add_convert_fusion.1
  65.8 2.2 %collective-permute-done.3 = bf16[512,1024]{1,0:T(8,128)(2,1)S(1)} collective-permute-done((bf16[512,1024]{1,0:T(8,128)(2,1)S(1)}, bf16[512,1024]{1,0:T(8,128)(2,1)S(1)}, u32[]{:S(2)}, u32[]{:S(2)}) %collective-permute-start.3) | collective-permute-done | bytes 1048608 | tf_op jit(solution)/shard_map/ppermute | solution.py:59
  68.1 0.4 add_convert_fusion
  68.5 0.2 pad_maximum_fusion.12
  68.7 2.0 %collective-permute-start.6 = (bf16[1024,128]{1,0:T(8,128)(2,1)S(1)}, bf16[1024,128]{1,0:T(8,128)(2,1)S(1)}, u32[]{:S(2)}, u32[]{:S(2)}) collective-permute-start(bf16[1024,128]{1,0:T(8,128)(2,1)S(1)} %get-tuple-element.5), channel_id=1, source_target_pairs={{0,32},{32,64},{64,96},{96,128},{128,160},{160,192},{192,224},{224... | collective-permute-start | bytes 786440 | tf_op jit(solution)/shard_map/ppermute | solution.py:74
  70.7 4.0 %collective-permute-start.9 = (bf16[1024,128]{1,0:T(8,128)(2,1)S(1)}, bf16[1024,128]{1,0:T(8,128)(2,1)S(1)}, u32[]{:S(2)}, u32[]{:S(2)}) collective-permute-start(bf16[1024,128]{1,0:T(8,128)(2,1)S(1)} %get-tuple-element.7), channel_id=1, source_target_pairs={{0,224},{32,0},{64,32},{96,64},{128,96},{160,128},{192,160},{224,1... | collective-permute-start | bytes 786440 | tf_op jit(solution)/shard_map/ppermute | solution.py:74
  74.7 0.1 collective-permute-start.7
  74.9 4.2 %collective-permute-start.10 = (bf16[512,128]{1,0:T(8,128)(2,1)S(1)}, bf16[512,128]{1,0:T(8,128)(2,1)S(1)}, u32[]{:S(2)}, u32[]{:S(2)}) collective-permute-start(bf16[512,128]{1,0:T(8,128)(2,1)S(1)} %slice.89), channel_id=1, source_target_pairs={{0,192},{32,224},{64,0},{96,32},{128,64},{160,96},{192,128},{224,1... | collective-permute-start | bytes 393224 | tf_op jit(solution)/shard_map/ppermute | solution.py:74
  79.1 9.3 %collective-permute-done.7 = bf16[512,128]{1,0:T(8,128)(2,1)S(1)} collective-permute-done((bf16[512,128]{1,0:T(8,128)(2,1)S(1)}, bf16[512,128]{1,0:T(8,128)(2,1)S(1)}, u32[]{:S(2)}, u32[]{:S(2)}) %collective-permute-start.7) | collective-permute-done | bytes 131104 | tf_op jit(solution)/shard_map/ppermute | solution.py:74
  88.4 1.5 %collective-permute-start.5 = (bf16[1024,128]{1,0:T(8,128)(2,1)S(1)}, bf16[1024,128]{1,0:T(8,128)(2,1)S(1)}, u32[]{:S(2)}, u32[]{:S(2)}) collective-permute-start(bf16[1024,128]{1,0:T(8,128)(2,1)S(1)} %get-tuple-element.6), channel_id=1, source_target_pairs={{0,224},{32,0},{64,32},{96,64},{128,96},{160,128},{192,160},{224,1... | collective-permute-start | bytes 786440 | tf_op jit(solution)/shard_map/ppermute | solution.py:74
  89.8 0.2 add_convert_fusion.4
  90.0 2.7 %collective-permute-start.11 = (bf16[1024,128]{1,0:T(8,128)(2,1)S(1)}, bf16[1024,128]{1,0:T(8,128)(2,1)S(1)}, u32[]{:S(2)}, u32[]{:S(2)}) collective-permute-start(bf16[1024,128]{1,0:T(8,128)(2,1)S(1)} %get-tuple-element.9), channel_id=1, source_target_pairs={{0,192},{32,224},{64,0},{96,32},{128,64},{160,96},{192,128},{224,1... | collective-permute-start | bytes 786440 | tf_op jit(solution)/shard_map/ppermute | solution.py:74
  92.8 0.3 collective-permute-start.8
  93.0 2.7 %fusion.1 = bf16[1,512,2048]{2,1,0:T(8,128)(2,1)} fusion(bf16[512,1024]{1,0:T(8,128)(2,1)S(1)} %get-tuple-element.17, bf16[512,1024]{1,0:T(8,128)(2,1)S(1)} %get-tuple-element.16, f32[512,512]{1,0:T(8,128)S(1)} %fusion.10), kind=kOutput, calls=%fused_computation.13 | convolution fusion | flops 1080295424 | bytes 5242880 | tf_op jit(solution)/shard_map/dot_general | solution.py:36
  95.7 4.3 %collective-permute-done.5 = bf16[1024,128]{1,0:T(8,128)(2,1)S(1)} collective-permute-done((bf16[1024,128]{1,0:T(8,128)(2,1)S(1)}, bf16[1024,128]{1,0:T(8,128)(2,1)S(1)}, u32[]{:S(2)}, u32[]{:S(2)}) %collective-permute-start.5) | collective-permute-done | bytes 262176 | tf_op jit(solution)/shard_map/ppermute | solution.py:74
  100.0 6.2 %collective-permute-done.11 = bf16[1024,128]{1,0:T(8,128)(2,1)S(1)} collective-permute-done((bf16[1024,128]{1,0:T(8,128)(2,1)S(1)}, bf16[1024,128]{1,0:T(8,128)(2,1)S(1)}, u32[]{:S(2)}, u32[]{:S(2)}) %collective-permute-start.11) | collective-permute-done | bytes 262176 | tf_op jit(solution)/shard_map/ppermute | solution.py:74
  106.2 0.2 add_convert_fusion.2
  106.4 0.7 copy.59
  107.1 4.8 %all-to-all-start.1 = ((bf16[2,16,32,128]{3,2,0,1:T(8,128)(2,1)}), bf16[2,16,32,128]{3,2,0,1:T(8,128)(2,1)S(1)}, u32[]{:S(2)}, u32[]{:S(2)}) async-start(bf16[2,16,32,128]{3,2,0,1:T(8,128)(2,1)} %copy.59), calls=%async_computation.1 | async-start | bytes 524288 | tf_op jit(solution)/shard_map/all_to_all | solution.py:152
  111.9 2.6 %fusion = bf16[1,2048,512]{2,1,0:T(8,128)(2,1)} fusion(bf16[512,512]{1,0:T(8,128)(2,1)S(1)} %fusion.15, bf16[512,1024]{1,0:T(8,128)(2,1)S(1)} %copy-done.9, bf16[512,1024]{1,0:T(8,128)(2,1)S(1)} %get-tuple-element.10), kind=kOutput, calls=%fused_computation.12 | convolution fusion | flops 1078984704 | bytes 4718592 | tf_op jit(solution)/shard_map/dot_general | solution.py:39
  114.5 4.8 %all-to-all-done.1 = bf16[2,16,32,128]{3,2,0,1:T(8,128)(2,1)S(1)} async-done(((bf16[2,16,32,128]{3,2,0,1:T(8,128)(2,1)}), bf16[2,16,32,128]{3,2,0,1:T(8,128)(2,1)S(1)}, u32[]{:S(2)}, u32[]{:S(2)}) %all-to-all-start.1) | async-done | bytes 262176 | tf_op jit(solution)/shard_map/all_to_all | solution.py:152
  119.3 0.9 convolution_reduce_fusion
  120.2 0.9 fusion.18
  (38 shorter events, 0.2 us)
Async XLA Ops:
  0.6 4.8 %copy-start = (bf16[128,2048]{1,0:T(8,128)(2,1)S(1)}, bf16[128,2048]{1,0:T(8,128)(2,1)}, u32[]{:S(2)}) copy-start(bf16[128,2048]{1,0:T(8,128)(2,1)} %param.6) | copy-start | bytes 1572868
  2.9 2.1 %copy-start.11 = (f32[128,2]{0,1:T(2,128)S(1)}, f32[128,2]{0,1:T(2,128)}, u32[]{:S(2)}) copy-start(f32[128,2]{0,1:T(2,128)} %param.8) | copy-start | bytes 3076
  3.9 1.4 %copy-start.10 = (s32[128,2]{0,1:T(2,128)S(1)}, s32[128,2]{0,1:T(2,128)}, u32[]{:S(2)}) copy-start(s32[128,2]{0,1:T(2,128)} %param.7) | copy-start | bytes 3076
  43.1 10.4 %collective-permute-start = (bf16[512,1024]{1,0:T(8,128)(2,1)}, bf16[512,1024]{1,0:T(8,128)(2,1)}, u32[]{:S(2)}, u32[]{:S(2)}) collective-permute-start(bf16[512,1024]{1,0:T(8,128)(2,1)} %get-tuple-element.12), channel_id=1, source_target_pairs={{0,16},{16,0},{1,17},{17,1},{2,18},{18,2},{3,19},{19,3},{4,20},{20... | collective-permute-start | bytes 3145736 | tf_op jit(solution)/shard_map/ppermute | solution.py:110
  47.5 2.4 %copy-start.3 = (bf16[1,2048,512]{2,1,0:T(8,128)(2,1)S(1)}, bf16[1,2048,512]{2,1,0:T(8,128)(2,1)}, u32[]{:S(2)}) copy-start(bf16[1,2048,512]{2,1,0:T(8,128)(2,1)} %param.10) | copy-start | bytes 6291460
  50.6 8.7 %collective-permute-start.2 = (bf16[512,1024]{1,0:T(8,128)(2,1)}, bf16[512,1024]{1,0:T(8,128)(2,1)}, u32[]{:S(2)}, u32[]{:S(2)}) collective-permute-start(bf16[512,1024]{1,0:T(8,128)(2,1)} %get-tuple-element.15), channel_id=1, source_target_pairs={{0,16},{16,0},{1,17},{17,1},{2,18},{18,2},{3,19},{19,3},{4,20},{20... | collective-permute-start | bytes 3145736 | tf_op jit(solution)/shard_map/ppermute | solution.py:110
  51.9 1.5 %copy-start.2 = (bf16[1,512,1024]{2,1,0:T(8,128)(2,1)S(1)}, bf16[1,512,1024]{2,1,0:T(8,128)(2,1)}, u32[]{:S(2)}) copy-start(bf16[1,512,1024]{2,1,0:T(8,128)(2,1)} %get-tuple-element.13) | copy-start | bytes 3145732
  53.5 2.1 %copy-start.4 = (bf16[1,2048,512]{2,1,0:T(8,128)(2,1)S(1)}, bf16[1,2048,512]{2,1,0:T(8,128)(2,1)}, u32[]{:S(2)}) copy-start(bf16[1,2048,512]{2,1,0:T(8,128)(2,1)} %param.10) | copy-start | bytes 6291460
  55.6 1.3 %copy-start.8 = (bf16[512,1024]{1,0:T(8,128)(2,1)}, bf16[512,1024]{1,0:T(8,128)(2,1)S(1)}, u32[]{:S(2)}) copy-start(bf16[512,1024]{1,0:T(8,128)(2,1)S(1)} %get-tuple-element.11) | copy-start | bytes 3145732
  55.6 2.0 %copy-start.7 = (bf16[512,2,8,128]{0,3,2,1:T(8,128)(2,1)S(1)}, bf16[512,2,8,128]{0,3,2,1:T(8,128)(2,1)}, u32[]{:S(2)}) copy-start(bf16[512,2,8,128]{0,3,2,1:T(8,128)(2,1)} %copy.57) | copy-start | bytes 6291460
  58.9 1.2 %copy-start.1 = (bf16[1,512,1024]{2,1,0:T(8,128)(2,1)S(1)}, bf16[1,512,1024]{2,1,0:T(8,128)(2,1)}, u32[]{:S(2)}) copy-start(bf16[1,512,1024]{2,1,0:T(8,128)(2,1)} %get-tuple-element.14) | copy-start | bytes 3145732
  59.0 6.4 %collective-permute-start.1 = (bf16[512,1024]{1,0:T(8,128)(2,1)S(1)}, bf16[512,1024]{1,0:T(8,128)(2,1)S(1)}, u32[]{:S(2)}, u32[]{:S(2)}) collective-permute-start(bf16[512,1024]{1,0:T(8,128)(2,1)S(1)} %slice.84), channel_id=1, source_target_pairs={{0,16},{16,0},{1,17},{17,1},{2,18},{18,2},{3,19},{19,3},{4,20},{20... | collective-permute-start | bytes 3145736 | tf_op jit(solution)/shard_map/ppermute | solution.py:59
  60.1 2.1 %copy-start.5 = (bf16[1,512,2048]{2,1,0:T(8,128)(2,1)S(1)}, bf16[1,512,2048]{2,1,0:T(8,128)(2,1)}, u32[]{:S(2)}) copy-start(bf16[1,512,2048]{2,1,0:T(8,128)(2,1)} %param.11) | copy-start | bytes 6291460
  62.3 1.6 %copy-start.6 = (bf16[2,8,128,512]{3,2,1,0:T(8,128)(2,1)S(1)}, bf16[2,8,128,512]{3,2,1,0:T(8,128)(2,1)}, u32[]{:S(2)}) copy-start(bf16[2,8,128,512]{3,2,1,0:T(8,128)(2,1)} %copy.58) | copy-start | bytes 6291460
  65.3 2.7 %collective-permute-start.3 = (bf16[512,1024]{1,0:T(8,128)(2,1)S(1)}, bf16[512,1024]{1,0:T(8,128)(2,1)S(1)}, u32[]{:S(2)}, u32[]{:S(2)}) collective-permute-start(bf16[512,1024]{1,0:T(8,128)(2,1)S(1)} %slice.87), channel_id=1, source_target_pairs={{0,16},{16,0},{1,17},{17,1},{2,18},{18,2},{3,19},{19,3},{4,20},{20... | collective-permute-start | bytes 3145736 | tf_op jit(solution)/shard_map/ppermute | solution.py:59
  68.7 21.2 %collective-permute-start.6 = (bf16[1024,128]{1,0:T(8,128)(2,1)S(1)}, bf16[1024,128]{1,0:T(8,128)(2,1)S(1)}, u32[]{:S(2)}, u32[]{:S(2)}) collective-permute-start(bf16[1024,128]{1,0:T(8,128)(2,1)S(1)} %get-tuple-element.5), channel_id=1, source_target_pairs={{0,32},{32,64},{64,96},{96,128},{128,160},{160,192},{192,224},{224... | collective-permute-start | bytes 786440 | tf_op jit(solution)/shard_map/ppermute | solution.py:74
  70.7 19.2 %collective-permute-start.9 = (bf16[1024,128]{1,0:T(8,128)(2,1)S(1)}, bf16[1024,128]{1,0:T(8,128)(2,1)S(1)}, u32[]{:S(2)}, u32[]{:S(2)}) collective-permute-start(bf16[1024,128]{1,0:T(8,128)(2,1)S(1)} %get-tuple-element.7), channel_id=1, source_target_pairs={{0,224},{32,0},{64,32},{96,64},{128,96},{160,128},{192,160},{224,1... | collective-permute-start | bytes 786440 | tf_op jit(solution)/shard_map/ppermute | solution.py:74
  74.7 13.7 %collective-permute-start.7 = (bf16[512,128]{1,0:T(8,128)(2,1)S(1)}, bf16[512,128]{1,0:T(8,128)(2,1)S(1)}, u32[]{:S(2)}, u32[]{:S(2)}) collective-permute-start(bf16[512,128]{1,0:T(8,128)(2,1)S(1)} %slice.88), channel_id=1, source_target_pairs={{0,64},{32,96},{64,128},{96,160},{128,192},{160,224},{192,0},{224,... | collective-permute-start | bytes 393224 | tf_op jit(solution)/shard_map/ppermute | solution.py:74
  74.9 15.0 %collective-permute-start.10 = (bf16[512,128]{1,0:T(8,128)(2,1)S(1)}, bf16[512,128]{1,0:T(8,128)(2,1)S(1)}, u32[]{:S(2)}, u32[]{:S(2)}) collective-permute-start(bf16[512,128]{1,0:T(8,128)(2,1)S(1)} %slice.89), channel_id=1, source_target_pairs={{0,192},{32,224},{64,0},{96,32},{128,64},{160,96},{192,128},{224,1... | collective-permute-start | bytes 393224 | tf_op jit(solution)/shard_map/ppermute | solution.py:74
  79.1 16.7 %collective-permute-start.4 = (bf16[1024,128]{1,0:T(8,128)(2,1)S(1)}, bf16[1024,128]{1,0:T(8,128)(2,1)S(1)}, u32[]{:S(2)}, u32[]{:S(2)}) collective-permute-start(bf16[1024,128]{1,0:T(8,128)(2,1)S(1)} %get-tuple-element.4), channel_id=1, source_target_pairs={{0,32},{32,64},{64,96},{96,128},{128,160},{160,192},{192,224},{224... | collective-permute-start | bytes 786440 | tf_op jit(solution)/shard_map/ppermute | solution.py:74
  88.4 11.6 %collective-permute-start.5 = (bf16[1024,128]{1,0:T(8,128)(2,1)S(1)}, bf16[1024,128]{1,0:T(8,128)(2,1)S(1)}, u32[]{:S(2)}, u32[]{:S(2)}) collective-permute-start(bf16[1024,128]{1,0:T(8,128)(2,1)S(1)} %get-tuple-element.6), channel_id=1, source_target_pairs={{0,224},{32,0},{64,32},{96,64},{128,96},{160,128},{192,160},{224,1... | collective-permute-start | bytes 786440 | tf_op jit(solution)/shard_map/ppermute | solution.py:74
  90.0 16.2 %collective-permute-start.11 = (bf16[1024,128]{1,0:T(8,128)(2,1)S(1)}, bf16[1024,128]{1,0:T(8,128)(2,1)S(1)}, u32[]{:S(2)}, u32[]{:S(2)}) collective-permute-start(bf16[1024,128]{1,0:T(8,128)(2,1)S(1)} %get-tuple-element.9), channel_id=1, source_target_pairs={{0,192},{32,224},{64,0},{96,32},{128,64},{160,96},{192,128},{224,1... | collective-permute-start | bytes 786440 | tf_op jit(solution)/shard_map/ppermute | solution.py:74
  92.8 13.4 %collective-permute-start.8 = (bf16[1024,128]{1,0:T(8,128)(2,1)S(1)}, bf16[1024,128]{1,0:T(8,128)(2,1)S(1)}, u32[]{:S(2)}, u32[]{:S(2)}) collective-permute-start(bf16[1024,128]{1,0:T(8,128)(2,1)S(1)} %get-tuple-element.8), channel_id=1, source_target_pairs={{0,64},{32,96},{64,128},{96,160},{128,192},{160,224},{192,0},{224,... | collective-permute-start | bytes 786440 | tf_op jit(solution)/shard_map/ppermute | solution.py:74
  95.7 16.2 %copy-start.9 = (bf16[512,1024]{1,0:T(8,128)(2,1)S(1)}, bf16[512,1024]{1,0:T(8,128)(2,1)}, u32[]{:S(2)}) copy-start(bf16[512,1024]{1,0:T(8,128)(2,1)} %copy-done.8) | copy-start | bytes 3145732
  107.1 12.2 %all-to-all-start.1 = ((bf16[2,16,32,128]{3,2,0,1:T(8,128)(2,1)}), bf16[2,16,32,128]{3,2,0,1:T(8,128)(2,1)S(1)}, u32[]{:S(2)}, u32[]{:S(2)}) async-start(bf16[2,16,32,128]{3,2,0,1:T(8,128)(2,1)} %copy.59), calls=%async_computation.1 | async-start | bytes 524288 | tf_op jit(solution)/shard_map/all_to_all | solution.py:152
